TPU v7x, 256 devices: a whole 4x4x8 slice. The times are simulated.
256 devices in a mesh: row: 16 (over y, x_lo, core), col: 16 (over x_hi, z).
Axes of the slice: x: 4 (x_hi: 2, x_lo: 2; x = x_hi * 2 + x_lo), y: 4, z: 8, core: 2. Of those that a mesh axis runs over, the one named last changes fastest.
Arguments:
- stored_blocks: float32 [512, 16, 128, 128], P('row', 'col'), may hold values from -1.8 to 1.8
- block_cols: int32 [512, 16], P('row', 'col'), may hold values from 0 to 31, as said below
- storage_map: int32 [512, 16], P('row', 'col'), may hold values from 0 to 1, as said below
Outputs:
- square_part: float32 [512, 16, 128, 128], P('row', 'col')
Inputs may be any that keep to these rules, and one draw needn't show every extreme that they name: The block pattern is symmetric: block (R, q) with column C = q * 32 + block_cols[R, q] has block_cols[C, R // 32] == R mod 32; every slab pairs its block rows with its block columns one to one; block_cols[R, R // 32] == R mod 32. Of a block and its mirror image exactly one has storage_map 1; blocks on the diagonal have 1.
All inputs are finite; a program needn't handle non-finite values.
Results may differ from a plain program's by a relative error of at most 0.0001.
Values sent between devices are 32-bit elements; how exact they have to be, the bound alone decides.
No kernel may reach another device: no remote copies, remote signals or barrier semaphores. Data moves between devices by JAX's collectives and lax.ppermute only.
A program may use at most 128 MiB of HBM per device.

v0:
```python
import jax
import jax.numpy as jnp
from jax import lax
from jax.sharding import PartitionSpec as P

STEPS = 4


def from_root(block, axis, holder):
    block = jnp.where(lax.axis_index(axis) == holder, block, jnp.zeros_like(block))
    return lax.psum(block, axis)


def shifted(block, axis, distance):
    devices = range(lax.axis_size(axis))
    route = [((i - distance) % len(devices), i) for i in devices]
    return lax.ppermute(block, axis, route)


def mirror_columns(masked):
    first = lax.all_to_all(masked, "col", split_axis=0, concat_axis=1, tiled=True)
    return lax.all_to_all(
        lax.all_to_all(first, "row", split_axis=1, concat_axis=1, tiled=True),
        "col",
        split_axis=1,
        concat_axis=0,
        tiled=True,
    )


def shards(stored_blocks, block_cols, storage_map):
    rows_total, groups = block_cols.shape
    row_count = lax.axis_size("row")
    masked = stored_blocks * storage_map.astype(jnp.float32)[:, :, None, None]
    arrived = mirror_columns(masked)
    group_ids = jnp.arange(groups, dtype=jnp.int32)[None, :]
    mirrored = arrived[block_cols, group_ids]
    density = masked + jnp.swapaxes(mirrored, 2, 3)
    col_float = block_cols.astype(jnp.float32)
    row_index = lax.axis_index("row")
    total = jnp.zeros(density.shape, jnp.float32)
    panel, panel_cols = (density, col_float)
    for step in range(STEPS):
        kappa = (row_index + step) % row_count
        holder = kappa // groups
        within = kappa % groups
        left_piece = lax.dynamic_index_in_dim(density, within, 1, keepdims=False)
        left_cols = lax.dynamic_index_in_dim(col_float, within, 1, keepdims=False)
        left_vals, left_colf = (
            from_root(left_piece, "col", holder),
            from_root(left_cols, "col", holder),
        )
        if step > 0:
            panel, panel_cols = shifted((panel, panel_cols), "row", -1)
        inner = left_colf.astype(jnp.int32)
        right = panel[inner]
        match = panel_cols[inner].astype(jnp.int32) == block_cols
        term = jnp.einsum("rik,rukj->ruij", left_vals, right, precision=lax.Precision.HIGHEST)
        total = total + jnp.where(match[:, :, None, None], term, jnp.float32(0.0))
    return total


def solution(mesh):
    return jax.shard_map(
        shards,
        mesh=mesh,
        in_specs=(P("row", "col", None, None), P("row", "col"), P("row", "col")),
        out_specs=P("row", "col", None, None),
        check_vma=False,
    )
```

profile of v0, /device:TPU:2, one launch (start us, length us, event | category | flops | bytes accessed | tf_op | source)
XLA Modules:
  0.0 476.1 jit_solution(1820990694939775161)
XLA Ops:
  6.5 0.7 convert_bitcast_fusion
  7.2 1.8 fusion.4
  9.0 60.8 %all_to_all.41 = f32[32,1,128,128]{3,2,1,0:T(8,128)S(1)} all-to-all(f32[32,1,128,128]{3,2,1,0:T(8,128)S(1)} %fusion.4), channel_id=1, replica_groups=mesh['row'=16,'col'=16] {'col'}, dimensions={0} | all-to-all | bytes 4194304 | tf_op jit(solution)/shard_map/all_to_all | solution.py:21
  69.8 32.4 %all_to_all.42 = f32[2,16,128,128]{3,2,0,1:T(8,128)} all-to-all(f32[2,16,128,128]{3,2,0,1:T(8,128)S(1)} %bitcast.110), channel_id=1, replica_groups=mesh['row'=16,'col'=16] {'row'}, dimensions={1} | all-to-all | bytes 4194304 | tf_op jit(solution)/shard_map/all_to_all | solution.py:23
  102.2 4.7 all-to-all-start.2
  106.9 0.0 all-reduce.5.cloned.1.call-start
  107.0 0.0 copy-done.8
  107.0 50.6 %all-to-all-done.2 = f32[2,16,128,128]{3,2,0,1:T(8,128)S(1)} async-done(((f32[2,16,128,128]{3,2,0,1:T(8,128)}), f32[2,16,128,128]{3,2,0,1:T(8,128)S(1)}, u32[]{:S(2)}, u32[]{:S(2)}) %all-to-all-start.2) | async-done | bytes 2097184 | tf_op jit(solution)/shard_map/all_to_all | solution.py:22
  157.6 2.0 gather_fusion.1
  159.6 2.9 copy.19
  162.5 3.9 select_bitcast_fusion
  166.4 2.7 select_bitcast_fusion.3
  169.1 0.0 all-reduce.5.cloned.1.call-update
  169.2 0.1 collective-permute-start.1
  169.2 107.8 %collective-permute-done.1 = f32[32,1,128,128]{3,2,0,1:T(8,128)S(1)} collective-permute-done((f32[32,1,128,128]{3,2,0,1:T(8,128)S(1)}, f32[32,1,128,128]{3,2,0,1:T(8,128)S(1)}, u32[]{:S(2)}, u32[]{:S(2)}) %collective-permute-start.1) | collective-permute-done | bytes 2097184 | tf_op jit(solution)/shard_map/ppermute | solution.py:17
  277.1 1.9 collective-permute-start.3
  279.0 107.8 %collective-permute-done.3 = f32[32,1,128,128]{3,2,0,1:T(8,128)} collective-permute-done((f32[32,1,128,128]{3,2,0,1:T(8,128)S(1)}, f32[32,1,128,128]{3,2,0,1:T(8,128)}, u32[]{:S(2)}, u32[]{:S(2)}) %collective-permute-start.3) | collective-permute-done | bytes 2097184 | tf_op jit(solution)/shard_map/ppermute | solution.py:17
  386.8 2.0 collective-permute-start.5
  388.8 0.0 copy-done.6
  388.8 1.8 collective-permute-start
  390.6 38.2 %all-reduce.1 = (f32[32]{0:T(128)S(1)}, f32[32]{0:T(128)S(1)}, f32[32]{0:T(128)S(1)}, f32[32]{0:T(128)S(1)}) all-reduce(f32[32]{0:T(128)S(1)} %get-tuple-element.28, f32[32]{0:T(128)S(1)} %get-tuple-element.27, f32[32]{0:T(128)S(1)} %get-tuple-element.26, f32[32]{0:T(128)S(1)} %get-tuple-element.25), channel_id=1, replica_groups=mesh['row'=16,'col'=16] {'col'}, use_global_device_ids=true, to_apply=%region_4.5 | all-reduce | flops 128 | bytes 1024 | tf_op jit(solution)/shard_map/psum | solution.py:11
  429.0 0.7 gather_fusion
  429.7 0.0 collective-permute-done
  429.7 0.1 collective-permute-start.2
  429.7 0.7 gather_fusion.3
  430.4 0.6 collective-permute-done.2
  431.0 4.3 collective-permute-start.4
  435.4 0.7 gather_fusion.5
  436.0 0.6 collective-permute-done.4
  436.6 0.7 gather_fusion.7
  437.4 2.0 gather_fusion.2
  439.4 3.6 gather_fusion.4
  443.0 3.6 gather_fusion.6
  446.6 0.0 collective-permute-done.5
  446.6 3.7 gather_fusion.8
  450.3 0.0 copy-done
  450.3 5.2 %fusion.10 = f32[32,128,128]{2,1,0:T(8,128)S(1)} fusion(f32[32,128,128]{2,1,0:T(8,128)S(1)} %copy-done, f32[32,128,128]{2,1,0:T(8,128)} %get-tuple-element.11), kind=kOutput, calls=%fused_computation.50 | convolution fusion | flops 805306368 | bytes 6291456 | tf_op jit(solution)/shard_map/rik,rukj->ruij/dot_general | solution.py:58
  455.6 0.0 copy-done.1
  455.6 0.0 copy-done.5
  455.6 0.0 copy-start.2
  455.6 0.0 copy-start.4
  455.6 3.7 fusion.11
  459.3 0.0 copy-done.2
  459.3 0.0 copy-done.4
  459.3 0.0 copy-start.3
  459.3 3.6 fusion.12
  462.9 4.5 fusion.1
  467.4 1.8 copy.24
  (22 shorter events, 0.1 us)
Async XLA Ops:
  102.2 4.8 %copy-start.8 = (s32[32,1]{0,1:T(1,128)S(1)}, s32[32,1]{0,1:T(1,128)}, u32[]{:S(2)}) copy-start(s32[32,1]{0,1:T(1,128)} %param.4) | copy-start | bytes 388
  102.2 55.4 %all-to-all-start.2 = ((f32[2,16,128,128]{3,2,0,1:T(8,128)}), f32[2,16,128,128]{3,2,0,1:T(8,128)S(1)}, u32[]{:S(2)}, u32[]{:S(2)}) async-start(f32[2,16,128,128]{3,2,0,1:T(8,128)} %all_to_all.42), calls=%async_computation.2 | async-start | bytes 4194304 | tf_op jit(solution)/shard_map/all_to_all | solution.py:22
  106.9 343.4 %all-reduce.5.cloned.1.call-start = ((), (), s32[]{:S(2)}) async-start(), calls=%async_computation.3 | async-start | bytes 16777216 | tf_op jit(solution)/shard_map/psum | solution.py:11
  169.2 107.9 %collective-permute-start.1 = (f32[32,1,128,128]{3,2,0,1:T(8,128)S(1)}, f32[32,1,128,128]{3,2,0,1:T(8,128)S(1)}, u32[]{:S(2)}, u32[]{:S(2)}) collective-permute-start(f32[32,1,128,128]{3,2,0,1:T(8,128)S(1)} %get-tuple-element.14), channel_id=1, source_target_pairs={{16,0},{32,16},{48,32},{64,48},{80,64},{96,80},{112,96},{128,112},... | collective-permute-start | bytes 6291464 | tf_op jit(solution)/shard_map/ppermute | solution.py:17
  277.1 111.7 %copy-start.6 = (f32[32,1,128,128]{3,2,0,1:T(8,128)}, f32[32,1,128,128]{3,2,0,1:T(8,128)S(1)}, u32[]{:S(2)}) copy-start(f32[32,1,128,128]{3,2,0,1:T(8,128)S(1)} %collective-permute-done.1) | copy-start | bytes 6291460
  277.1 109.7 %collective-permute-start.3 = (f32[32,1,128,128]{3,2,0,1:T(8,128)S(1)}, f32[32,1,128,128]{3,2,0,1:T(8,128)}, u32[]{:S(2)}, u32[]{:S(2)}) collective-permute-start(f32[32,1,128,128]{3,2,0,1:T(8,128)S(1)} %collective-permute-done.1), channel_id=1, source_target_pairs={{16,0},{32,16},{48,32},{64,48},{80,64},{96,80},{112,96},{128,112},... | collective-permute-start | bytes 6291464 | tf_op jit(solution)/shard_map/ppermute | solution.py:17
  386.8 59.8 %collective-permute-start.5 = (f32[32,1,128,128]{3,2,0,1:T(8,128)}, f32[32,1,128,128]{3,2,0,1:T(8,128)}, u32[]{:S(2)}, u32[]{:S(2)}) collective-permute-start(f32[32,1,128,128]{3,2,0,1:T(8,128)} %collective-permute-done.3), channel_id=1, source_target_pairs={{16,0},{32,16},{48,32},{64,48},{80,64},{96,80},{112,96},{128,112},... | collective-permute-start | bytes 6291464 | tf_op jit(solution)/shard_map/ppermute | solution.py:17
  388.8 40.9 %collective-permute-start = (f32[32,1]{0,1:T(1,128)S(1)}, f32[32,1]{0,1:T(1,128)S(1)}, u32[]{:S(2)}, u32[]{:S(2)}) collective-permute-start(f32[32,1]{0,1:T(1,128)S(1)} %get-tuple-element.24), channel_id=1, source_target_pairs={{16,0},{32,16},{48,32},{64,48},{80,64},{96,80},{112,96},{128,112},... | collective-permute-start | bytes 392 | tf_op jit(solution)/shard_map/ppermute | solution.py:17
  429.7 1.4 collective-permute-start.2
  431.0 5.6 %collective-permute-start.4 = (f32[32,1]{0,1:T(1,128)S(1)}, f32[32,1]{0,1:T(1,128)S(1)}, u32[]{:S(2)}, u32[]{:S(2)}) collective-permute-start(f32[32,1]{0,1:T(1,128)S(1)} %collective-permute-done.2), channel_id=1, source_target_pairs={{16,0},{32,16},{48,32},{64,48},{80,64},{96,80},{112,96},{128,112},... | collective-permute-start | bytes 392 | tf_op jit(solution)/shard_map/ppermute | solution.py:17
  446.6 3.7 copy-start
  450.3 5.3 %copy-start.1 = (f32[32,128,128]{2,1,0:T(8,128)S(1)}, f32[32,128,128]{2,1,0:T(8,128)}, u32[]{:S(2)}) copy-start(f32[32,128,128]{2,1,0:T(8,128)} %gather_fusion.4) | copy-start | bytes 6291460
  450.3 5.3 %copy-start.5 = (f32[32,128,128]{2,1,0:T(8,128)S(1)}, f32[32,128,128]{2,1,0:T(8,128)}, u32[]{:S(2)}) copy-start(f32[32,128,128]{2,1,0:T(8,128)} %get-tuple-element.10) | copy-start | bytes 6291460
  455.6 3.7 copy-start.2
  455.6 3.7 copy-start.4
  459.3 3.6 copy-start.3
  459.3 3.6 copy-start.7
Sparse Core Ops, SparseCore 0:
  169.3 202.5 all-reduce.4
where the time goes:
time: 480 us; the launch traced here: 476 us
  waiting for transfers between devices  267 us (56%)
  blocking collectives  131 us (27%)
  local copies, waits for them, and re-layouts  22.5 us (5%)
  matrix products  17 us (4%)
  starting transfers between devices  15 us (3%)
  between operations  13.7 us (3%)
  other arithmetic  9.16 us (2%)
    ppermute x6, waiting for transfers between devices, shifted(): return lax.ppermute(block, axis, route)  217 us
    all_to_all x1, blocking collectives, mirror_columns(): lax.all_to_all(masked, 'col', split_axis=0, concat_axis=1, tiled=True)  60.8 us
    all_to_all x1, waiting for transfers between devices, mirror_columns(): lax.all_to_all(lax.all_to_all(first, 'row', split_axis=1, concat_axis=1,...  50.6 us
    psum x1, blocking collectives, from_root(): return lax.psum(block, axis)  38.2 us
    all_to_all x1, blocking collectives, mirror_columns(): lax.all_to_all(first, 'row', split_axis=1, concat_axis=1, tiled=True)  32.4 us
    dot_general x4, matrix products, shards(): jnp.einsum('rik,rukj->ruij', left_vals, right, precision=lax.Precision.HI...  17 us
    gather x4, local copies, waits for them, and re-layouts, shards(): right = panel[inner]  12.9 us
    ppermute x6, starting transfers between devices, shifted(): return lax.ppermute(block, axis, route)  10.2 us
  transfers between devices with their start and end apart: 8, of which 5 were waited for; matrix products, arithmetic and copies ran while one was open for 3% of the time, Pallas kernels for 0%

commit v1 on v0

v1 whole, which is shorter than its diff:
```python
import jax
import jax.numpy as jnp
from jax import lax
from jax.sharding import PartitionSpec as P

STEPS = 4


def shifted(block, axis, distance):
    size = lax.axis_size(axis)
    route = [((i + distance) % size, i) for i in range(size)]
    return lax.ppermute(block, axis, route)


def transposed(block, rows, cols):
    route = [(b * cols + a, a * cols + b) for a in range(rows) for b in range(cols)]
    return lax.ppermute(block, ("row", "col"), route)


def gathered_cols(block_cols, rows, cols):
    local_rows = block_cols.shape[0]
    flat = lax.all_gather(block_cols[:, 0], ("row", "col"), axis=0, tiled=True)
    grid = flat.reshape(rows, cols, local_rows)
    return jnp.transpose(grid, (0, 2, 1)).reshape(rows * local_rows, cols)


def shards(stored_blocks, block_cols, storage_map):
    rows = lax.axis_size("row")
    cols = lax.axis_size("col")
    local_rows = stored_blocks.shape[0]
    bs = stored_blocks.shape[-1]
    row_index = lax.axis_index("row")
    col_index = lax.axis_index("col")

    all_cols = gathered_cols(block_cols, rows, cols)

    held = stored_blocks[:, 0] * storage_map.astype(jnp.float32)[:, :, None]
    arrived = transposed(held, rows, cols)
    mirrored = arrived[block_cols[:, 0]]
    density = held + jnp.swapaxes(mirrored, 1, 2)

    chunk = local_rows // cols
    pieces = density.reshape(cols, chunk, bs, bs)
    spread = lax.all_to_all(pieces, "col", 0, 0, tiled=True)
    window = (row_index + jnp.arange(STEPS, dtype=jnp.int32)) % cols
    mine = spread[window]
    left_all = lax.all_gather(mine, "col", axis=0, tiled=False)
    left_all = jnp.transpose(left_all, (1, 0, 2, 3, 4)).reshape(STEPS, local_rows, bs, bs)

    rights = [density] + [shifted(density, "row", step) for step in range(1, STEPS)]

    own_cols = block_cols[:, 0]
    total = jnp.zeros(density.shape, jnp.float32)
    for step in range(STEPS):
        kappa = (row_index + step) % cols
        inner = lax.dynamic_index_in_dim(all_cols, kappa, 1, keepdims=False)
        inner = lax.dynamic_slice_in_dim(inner, row_index * local_rows, local_rows)
        right = rights[step][inner]
        panel_cols = lax.dynamic_index_in_dim(all_cols, col_index, 1, keepdims=False)
        panel_cols = lax.dynamic_slice_in_dim(panel_cols, kappa * local_rows, local_rows)
        match = panel_cols[inner] == own_cols
        term = jnp.einsum("rik,rkj->rij", left_all[step], right, precision=lax.Precision.HIGHEST)
        total = total + jnp.where(match[:, None, None], term, jnp.float32(0.0))
    return total[:, None]


def solution(mesh):
    return jax.shard_map(
        shards,
        mesh=mesh,
        in_specs=(P("row", "col", None, None), P("row", "col"), P("row", "col")),
        out_specs=P("row", "col", None, None),
        check_vma=False,
    )
```

time: 480 us -> 479 us (level)
  waiting for transfers between devices: 267 us -> 185 us
  blocking collectives: 131 us -> 201 us
  local copies, waits for them, and re-layouts: 22.5 us -> 32.1 us
  starting transfers between devices: 15 us -> 23.2 us
  other arithmetic: 9.16 us -> 2.87 us
    ppermute x6 -> x3, waiting for transfers between devices: 217 us -> 0.01 us  [shifted(): return lax.ppermute(block, axis, route)]
    unnamed x0 -> x1, blocking collectives: none -> 201 us
    ppermute x0 -> x1, waiting for transfers between devices: none -> 137 us  [transposed(): return lax.ppermute(block, ('row', 'col'), route)]
    all_to_all x2 -> x0, blocking collectives: 93.2 us -> none  [the longest x1 60.8 us: mirror_columns(): lax.all_to_all(masked, 'col', split_axis=0, concat_axis=1, tiled=True)]
    psum x1 -> x0, blocking collectives: 38.2 us -> none  [from_root(): return lax.psum(block, axis)]
    select_n x7 -> x2, other arithmetic: 6.66 us -> 0.02 us  [the longest x1 0.01 us: shards(): mine = spread[window]]
    ppermute x0 -> x1, starting transfers between devices: none -> 5.14 us  [transposed(): return lax.ppermute(block, ('row', 'col'), route)]
    ppermute x6 -> x3, starting transfers between devices: 10.2 us -> 10.3 us  [shifted(): return lax.ppermute(block, axis, route)]
  transfers between devices with their start and end apart: 8 -> 6, of which waited for: 5 -> 2; matrix products, arithmetic and copies ran while one was open for 3% -> 3% of each run, Pallas kernels for 0% -> 0%
where the time goes in v1:
time: 479 us; the launch traced here: 477 us
  blocking collectives  201 us (42%)
  waiting for transfers between devices  185 us (39%)
  local copies, waits for them, and re-layouts  32.1 us (7%)
  starting transfers between devices  23.2 us (5%)
  matrix products  19.6 us (4%)
  between operations  13.7 us (3%)
    unnamed x1, blocking collectives  201 us
    ppermute x1, waiting for transfers between devices, transposed(): return lax.ppermute(block, ('row', 'col'), route)  137 us
    all_to_all x1, waiting for transfers between devices, shards(): spread = lax.all_to_all(pieces, 'col', 0, 0, tiled=True)  47.6 us
    dot_general x4, matrix products, shards(): jnp.einsum('rik,rkj->rij', left_all[step], right, precision=lax.Precision...  19.6 us
    gather x4, local copies, waits for them, and re-layouts, shards(): right = rights[step][inner]  12.8 us
    ppermute x3, starting transfers between devices, shifted(): return lax.ppermute(block, axis, route)  10.3 us
  transfers between devices with their start and end apart: 6, of which 2 were waited for; matrix products, arithmetic and copies ran while one was open for 3% of the time, Pallas kernels for 0%

profile of v1, /device:TPU:2, one launch (start us, length us, event | category | flops | bytes accessed | tf_op | source)
XLA Modules:
  0.0 476.6 jit_solution(3232132335825944552)
XLA Ops:
  6.5 1.9 copy.22
  8.5 0.0 copy-done.6
  8.5 0.0 copy-start
  8.5 0.0 copy-start.5
  8.5 0.2 bitcast_multiply_fusion
  8.7 1.1 copy-done
  9.8 5.1 %collective-permute-start = (f32[32,128,128]{1,2,0:T(8,128)S(1)}, f32[32,128,128]{1,2,0:T(8,128)}, u32[]{:S(2)}, u32[]{:S(2)}) collective-permute-start(f32[32,128,128]{1,2,0:T(8,128)S(1)} %bitcast_multiply_fusion), channel_id=1, source_target_pairs={{0,0},{16,1},{32,2},{48,3},{64,4},{80,5},{96,6},{112,7},{128,8},{1... | collective-permute-start | bytes 6291464 | tf_op jit(solution)/shard_map/ppermute | solution.py:17
  15.0 0.0 copy-done.5
  15.0 136.9 %collective-permute-done = f32[32,128,128]{1,2,0:T(8,128)} collective-permute-done((f32[32,128,128]{1,2,0:T(8,128)S(1)}, f32[32,128,128]{1,2,0:T(8,128)}, u32[]{:S(2)}, u32[]{:S(2)}) %collective-permute-start) | collective-permute-done | bytes 2097184 | tf_op jit(solution)/shard_map/ppermute | solution.py:17
  151.9 1.9 copy.23
  153.9 2.0 gather_fusion.1
  155.9 2.5 bitcast_add_fusion
  158.4 1.8 copy.24
  160.2 7.7 %all-to-all-start = ((f32[16,2,128,128]{3,2,1,0:T(8,128)}), f32[16,2,128,128]{3,2,1,0:T(8,128)}, u32[]{:S(2)}, u32[]{:S(2)}) async-start(f32[16,2,128,128]{3,2,1,0:T(8,128)} %copy.24), calls=%async_computation | async-start | bytes 4194304 | tf_op jit(solution)/shard_map/all_to_all | solution.py:44
  167.9 0.0 all-gather.4.cloned.1.call-start
  168.0 47.6 %all-to-all-done = f32[16,2,128,128]{3,2,1,0:T(8,128)} async-done(((f32[16,2,128,128]{3,2,1,0:T(8,128)}), f32[16,2,128,128]{3,2,1,0:T(8,128)}, u32[]{:S(2)}, u32[]{:S(2)}) %all-to-all-start) | async-done | bytes 2097184 | tf_op jit(solution)/shard_map/all_to_all | solution.py:44
  215.6 3.0 gather_fusion.2
  218.6 0.0 all-gather.4.cloned.1.call-update
  218.6 6.1 %collective-permute-start.2 = (f32[32,128,128]{1,2,0:T(8,128)S(1)}, f32[32,128,128]{1,2,0:T(8,128)}, u32[]{:S(2)}, u32[]{:S(2)}) collective-permute-start(f32[32,128,128]{1,2,0:T(8,128)S(1)} %bitcast_add_fusion), channel_id=1, source_target_pairs={{32,0},{48,16},{64,32},{80,48},{96,64},{112,80},{128,96},{144,112}... | collective-permute-start | bytes 6291464 | tf_op jit(solution)/shard_map/ppermute | solution.py:12
  224.7 0.0 collective-permute-start.1
  224.7 4.2 collective-permute-start.3
  228.8 0.1 bitcast_dynamic-update-slice_fusion
  228.9 200.6 %all-reduce = s32[8192]{0:T(1024)S(1)} all-reduce(s32[8192]{0:T(1024)S(1)} %bitcast_dynamic-update-slice_fusion), channel_id=2, replica_groups=mesh['row'=16,'col'=16] {'row','col'}, use_global_device_ids=true, to_apply=%add | all-reduce | flops 8192 | bytes 65536
  429.6 0.1 reshape.104
  429.7 0.1 reshape.105
  429.9 0.1 dynamic-slice_bitcast_fusion.3
  430.0 0.7 gather_fusion
  430.7 0.7 gather_fusion.8
  431.4 0.7 gather_fusion.4
  432.1 0.7 gather_fusion.6
  432.9 2.1 gather_fusion.3
  434.9 0.0 collective-permute-done.2
  434.9 3.6 gather_fusion.7
  438.5 0.0 collective-permute-done.1
  438.5 3.6 gather_fusion.5
  442.1 0.0 collective-permute-done.3
  442.1 3.6 gather_fusion.9
  445.7 4.4 fusion.7
  450.1 0.0 copy-done.2
  450.1 0.0 copy-start.3
  450.1 4.5 fusion.10
  454.7 0.0 copy-done.3
  454.7 0.0 copy-start.1
  454.7 4.5 fusion.9
  459.2 0.0 copy-done.1
  459.2 0.0 copy-start.4
  459.2 4.5 fusion.8
  463.7 6.0 %add_bitcast_fusion = f32[32,1,128,128]{3,2,1,0:T(8,128)} fusion(f32[32,128,128]{2,1,0:T(8,128)S(1)} %fusion.10, f32[32,128,128]{2,1,0:T(8,128)S(1)} %fusion.9, f32[32,128,128]{2,1,0:T(8,128)S(1)} %fusion.8, f32[32,128,128]{2,1,0:T(8,128)S(1)} %bitcast.62, f32[32,128,128]{1,2,0:T(8,128)S(1)} %copy-done.4, pred[32]{0:T(512)(128)(4,1)S(1)} %get-tuple-element.18, ...), kind=kOutput, calls=%fused_computation.12 | convolution fusion | flops 808976384 | bytes 12583040 | tf_op jit(solution)/shard_map/rik,rkj->rij/dot_general | solution.py:62
  (16 shorter events, 0.1 us)
Async XLA Ops:
  6.5 1.9 copy-start.6
  8.5 1.3 copy-start
  8.5 6.5 %copy-start.5 = (s32[32,1]{0,1:T(1,128)S(1)}, s32[32,1]{0,1:T(1,128)}, u32[]{:S(2)}) copy-start(s32[32,1]{0,1:T(1,128)} %param.4) | copy-start | bytes 388
  9.8 142.1 %collective-permute-start = (f32[32,128,128]{1,2,0:T(8,128)S(1)}, f32[32,128,128]{1,2,0:T(8,128)}, u32[]{:S(2)}, u32[]{:S(2)}) collective-permute-start(f32[32,128,128]{1,2,0:T(8,128)S(1)} %bitcast_multiply_fusion), channel_id=1, source_target_pairs={{0,0},{16,1},{32,2},{48,3},{64,4},{80,5},{96,6},{112,7},{128,8},{1... | collective-permute-start | bytes 6291464 | tf_op jit(solution)/shard_map/ppermute | solution.py:17
  160.2 55.4 %all-to-all-start = ((f32[16,2,128,128]{3,2,1,0:T(8,128)}), f32[16,2,128,128]{3,2,1,0:T(8,128)}, u32[]{:S(2)}, u32[]{:S(2)}) async-start(f32[16,2,128,128]{3,2,1,0:T(8,128)} %copy.24), calls=%async_computation | async-start | bytes 4194304 | tf_op jit(solution)/shard_map/all_to_all | solution.py:44
  167.9 277.8 %all-gather.4.cloned.1.call-start = ((), (), s32[]{:S(2)}) async-start(), calls=%async_computation.1 | async-start | bytes 8912896 | tf_op jit(solution)/shard_map/all_gather | solution.py:47
  218.6 216.3 %collective-permute-start.2 = (f32[32,128,128]{1,2,0:T(8,128)S(1)}, f32[32,128,128]{1,2,0:T(8,128)}, u32[]{:S(2)}, u32[]{:S(2)}) collective-permute-start(f32[32,128,128]{1,2,0:T(8,128)S(1)} %bitcast_add_fusion), channel_id=1, source_target_pairs={{32,0},{48,16},{64,32},{80,48},{96,64},{112,80},{128,96},{144,112}... | collective-permute-start | bytes 6291464 | tf_op jit(solution)/shard_map/ppermute | solution.py:12
  224.7 213.8 %collective-permute-start.1 = (f32[32,128,128]{1,2,0:T(8,128)S(1)}, f32[32,128,128]{1,2,0:T(8,128)}, u32[]{:S(2)}, u32[]{:S(2)}) collective-permute-start(f32[32,128,128]{1,2,0:T(8,128)S(1)} %bitcast_add_fusion), channel_id=1, source_target_pairs={{16,0},{32,16},{48,32},{64,48},{80,64},{96,80},{112,96},{128,112},... | collective-permute-start | bytes 6291464 | tf_op jit(solution)/shard_map/ppermute | solution.py:12
  224.7 217.4 %collective-permute-start.3 = (f32[32,128,128]{1,2,0:T(8,128)S(1)}, f32[32,128,128]{1,2,0:T(8,128)}, u32[]{:S(2)}, u32[]{:S(2)}) collective-permute-start(f32[32,128,128]{1,2,0:T(8,128)S(1)} %bitcast_add_fusion), channel_id=1, source_target_pairs={{48,0},{64,16},{80,32},{96,48},{112,64},{128,80},{144,96},{160,112... | collective-permute-start | bytes 6291464 | tf_op jit(solution)/shard_map/ppermute | solution.py:12
  445.7 4.4 copy-start.2
  450.1 4.5 copy-start.3
  454.7 4.5 copy-start.1
  459.2 4.5 copy-start.4
Sparse Core Ops, SparseCore 0:
  218.7 180.1 all-gather.3

commit v2 on v1

--- a/solution.py
+++ b/solution.py
@@ -17,22 +17,15 @@
     return lax.ppermute(block, ("row", "col"), route)
 
 
-def gathered_cols(block_cols, rows, cols):
-    local_rows = block_cols.shape[0]
-    flat = lax.all_gather(block_cols[:, 0], ("row", "col"), axis=0, tiled=True)
-    grid = flat.reshape(rows, cols, local_rows)
-    return jnp.transpose(grid, (0, 2, 1)).reshape(rows * local_rows, cols)
-
-
 def shards(stored_blocks, block_cols, storage_map):
     rows = lax.axis_size("row")
     cols = lax.axis_size("col")
     local_rows = stored_blocks.shape[0]
     bs = stored_blocks.shape[-1]
     row_index = lax.axis_index("row")
-    col_index = lax.axis_index("col")
 
-    all_cols = gathered_cols(block_cols, rows, cols)
+    row_cols = lax.all_gather(block_cols, "col", axis=1, tiled=True)
+    col_cols = lax.all_gather(block_cols, "row", axis=0, tiled=True)[:, 0]
 
     held = stored_blocks[:, 0] * storage_map.astype(jnp.float32)[:, :, None]
     arrived = transposed(held, rows, cols)
@@ -47,17 +40,18 @@
     left_all = lax.all_gather(mine, "col", axis=0, tiled=False)
     left_all = jnp.transpose(left_all, (1, 0, 2, 3, 4)).reshape(STEPS, local_rows, bs, bs)
 
-    rights = [density] + [shifted(density, "row", step) for step in range(1, STEPS)]
+    one = shifted(density, "row", 1)
+    two = shifted(density, "row", 2)
+    three = shifted(two, "row", 1)
+    rights = [density, one, two, three]
 
     own_cols = block_cols[:, 0]
     total = jnp.zeros(density.shape, jnp.float32)
     for step in range(STEPS):
         kappa = (row_index + step) % cols
-        inner = lax.dynamic_index_in_dim(all_cols, kappa, 1, keepdims=False)
-        inner = lax.dynamic_slice_in_dim(inner, row_index * local_rows, local_rows)
+        inner = lax.dynamic_index_in_dim(row_cols, kappa, 1, keepdims=False)
         right = rights[step][inner]
-        panel_cols = lax.dynamic_index_in_dim(all_cols, col_index, 1, keepdims=False)
-        panel_cols = lax.dynamic_slice_in_dim(panel_cols, kappa * local_rows, local_rows)
+        panel_cols = lax.dynamic_slice_in_dim(col_cols, kappa * local_rows, local_rows)
         match = panel_cols[inner] == own_cols
         term = jnp.einsum("rik,rkj->rij", left_all[step], right, precision=lax.Precision.HIGHEST)
         total = total + jnp.where(match[:, None, None], term, jnp.float32(0.0))

time: 479 us -> 422 us (0.88)
  blocking collectives: 201 us -> 97.1 us
  waiting for transfers between devices: 185 us -> 235 us
    unnamed x1, blocking collectives: 201 us -> 58.5 us
    ppermute x3, waiting for transfers between devices: 0.01 us -> 50.7 us  [shifted(): return lax.ppermute(block, axis, route)]
    all_gather x0 -> x1, blocking collectives: none -> 38.6 us  [shards(): row_cols = lax.all_gather(block_cols, 'col', axis=1, tiled=True)]
  transfers between devices with their start and end apart: 6 -> 6, of which waited for: 2 -> 3; matrix products, arithmetic and copies ran while one was open for 3% -> 4% of each run, Pallas kernels for 0% -> 0%
where the time goes in v2:
time: 422 us; the launch traced here: 421 us
  waiting for transfers between devices  235 us (56%)
  blocking collectives  97.1 us (23%)
  local copies, waits for them, and re-layouts  32.6 us (8%)
  matrix products  19.6 us (5%)
  starting transfers between devices  19.1 us (5%)
  between operations  14.3 us (3%)
    ppermute x1, waiting for transfers between devices, transposed(): return lax.ppermute(block, ('row', 'col'), route)  137 us
    unnamed x1, blocking collectives  58.5 us
    ppermute x3, waiting for transfers between devices, shifted(): return lax.ppermute(block, axis, route)  50.7 us
    all_to_all x1, waiting for transfers between devices, shards(): spread = lax.all_to_all(pieces, 'col', 0, 0, tiled=True)  47.6 us
    all_gather x1, blocking collectives, shards(): row_cols = lax.all_gather(block_cols, 'col', axis=1, tiled=True)  38.6 us
    dot_general x4, matrix products, shards(): jnp.einsum('rik,rkj->rij', left_all[step], right, precision=lax.Precision...  19.6 us
    gather x4, local copies, waits for them, and re-layouts, shards(): right = rights[step][inner]  12.9 us
  transfers between devices with their start and end apart: 6, of which 3 were waited for; matrix products, arithmetic and copies ran while one was open for 4% of the time, Pallas kernels for 0%

profile of v2, /device:TPU:2, one launch (start us, length us, event | category | flops | bytes accessed | tf_op | source)
XLA Modules:
  0.0 420.7 jit_solution(1843596424064097418)
XLA Ops:
  6.5 1.9 copy.20
  8.5 0.0 copy-done.6
  8.5 0.0 copy-start
  8.5 0.0 copy-start.5
  8.5 0.2 bitcast_multiply_fusion
  8.7 1.1 copy-done
  9.8 5.1 %collective-permute-start = (f32[32,128,128]{1,2,0:T(8,128)S(1)}, f32[32,128,128]{1,2,0:T(8,128)}, u32[]{:S(2)}, u32[]{:S(2)}) collective-permute-start(f32[32,128,128]{1,2,0:T(8,128)S(1)} %bitcast_multiply_fusion), channel_id=1, source_target_pairs={{0,0},{16,1},{32,2},{48,3},{64,4},{80,5},{96,6},{112,7},{128,8},{1... | collective-permute-start | bytes 6291464 | tf_op jit(solution)/shard_map/ppermute | solution.py:17
  15.0 0.0 copy-done.5
  15.0 136.9 %collective-permute-done = f32[32,128,128]{1,2,0:T(8,128)} collective-permute-done((f32[32,128,128]{1,2,0:T(8,128)S(1)}, f32[32,128,128]{1,2,0:T(8,128)}, u32[]{:S(2)}, u32[]{:S(2)}) %collective-permute-start) | collective-permute-done | bytes 2097184 | tf_op jit(solution)/shard_map/ppermute | solution.py:17
  152.0 1.9 copy.21
  153.9 2.0 gather_fusion.1
  155.9 2.5 bitcast_add_fusion
  158.4 1.8 copy.22
  160.2 7.9 %all-to-all-start = ((f32[16,2,128,128]{3,2,1,0:T(8,128)}), f32[16,2,128,128]{3,2,1,0:T(8,128)}, u32[]{:S(2)}, u32[]{:S(2)}) async-start(f32[16,2,128,128]{3,2,1,0:T(8,128)} %copy.22), calls=%async_computation | async-start | bytes 4194304 | tf_op jit(solution)/shard_map/all_to_all | solution.py:37
  168.1 0.0 all-gather.4.cloned.1.call-start
  168.2 47.6 %all-to-all-done = f32[16,2,128,128]{3,2,1,0:T(8,128)} async-done(((f32[16,2,128,128]{3,2,1,0:T(8,128)}), f32[16,2,128,128]{3,2,1,0:T(8,128)}, u32[]{:S(2)}, u32[]{:S(2)}) %all-to-all-start) | async-done | bytes 2097184 | tf_op jit(solution)/shard_map/all_to_all | solution.py:37
  215.7 3.0 gather_fusion.2
  218.7 0.0 all-gather.4.cloned.1.call-update
  218.7 6.1 %collective-permute-start.2 = (f32[32,128,128]{1,2,0:T(8,128)S(1)}, f32[32,128,128]{1,2,0:T(8,128)}, u32[]{:S(2)}, u32[]{:S(2)}) collective-permute-start(f32[32,128,128]{1,2,0:T(8,128)S(1)} %bitcast_add_fusion), channel_id=1, source_target_pairs={{32,0},{48,16},{64,32},{80,48},{96,64},{112,80},{128,96},{144,112}... | collective-permute-start | bytes 6291464 | tf_op jit(solution)/shard_map/ppermute | solution.py:12
  224.8 0.0 collective-permute-start.1
  224.8 50.7 %collective-permute-done.2 = f32[32,128,128]{1,2,0:T(8,128)} collective-permute-done((f32[32,128,128]{1,2,0:T(8,128)S(1)}, f32[32,128,128]{1,2,0:T(8,128)}, u32[]{:S(2)}, u32[]{:S(2)}) %collective-permute-start.2) | collective-permute-done | bytes 2097184 | tf_op jit(solution)/shard_map/ppermute | solution.py:12
  275.5 0.0 collective-permute-start.3
  275.5 0.0 copy-done.7
  275.5 0.6 dynamic-slice.4
  276.8 38.6 %all-gather.1 = s32[16,1,32]{2,1,0:T(1,128)S(1)} all-gather(s32[1,1,32]{2,1,0:T(1,128)S(1)} %bitcast.78), channel_id=1, replica_groups=mesh['row'=16,'col'=16] {'col'}, dimensions={0}, use_global_device_ids=true | all-gather | bytes 2176 | tf_op jit(solution)/shard_map/all_gather | solution.py:27
  315.4 0.1 bitcast_dynamic-update-slice_fusion
  315.5 58.5 %all-reduce = s32[512]{0:T(512)S(1)} all-reduce(s32[512]{0:T(512)S(1)} %bitcast_dynamic-update-slice_fusion), channel_id=1, replica_groups=mesh['row'=16,'col'=16] {'row'}, use_global_device_ids=true, to_apply=%add | all-reduce | flops 512 | bytes 4096
  374.0 0.1 fusion.12
  374.0 0.7 gather_fusion
  374.7 0.7 gather_fusion.4
  375.5 0.7 gather_fusion.6
  376.2 0.7 gather_fusion.8
  376.9 2.1 gather_fusion.3
  379.0 3.6 gather_fusion.7
  382.6 0.0 collective-permute-done.1
  382.6 3.6 gather_fusion.5
  386.2 0.0 collective-permute-done.3
  386.2 3.6 gather_fusion.9
  389.8 4.4 %fusion.11 = (f32[1,16,2,128,128]{4,3,2,0,1:T(8,128)S(1)}, f32[1,16,2,128,128]{4,3,2,0,1:T(8,128)S(1)}, f32[1,16,2,128,128]{4,3,2,0,1:T(8,128)S(1)}, f32[1,16,2,128,128]{4,3,2,0,1:T(8,128)S(1)}) fusion(f32[4,16,2,128,128]{4,3,2,0,1:T(8,128)} %bitcast.73), kind=kLoop, calls=%fused_computation.49 | loop fusion | bytes 16777216 | tf_op jit(solution)/shard_map/slice | solution.py:56
  394.2 0.0 copy-done.2
  394.2 0.0 copy-start.3
  394.2 4.5 %fusion.15 = f32[32,128,128]{2,1,0:T(8,128)S(1)} fusion(f32[32,128,128]{2,1,0:T(8,128)S(1)} %bitcast.76, f32[32,128,128]{1,2,0:T(8,128)S(1)} %copy-done.2), kind=kOutput, calls=%fused_computation.53 | convolution fusion | flops 805306368 | bytes 6291456 | tf_op jit(solution)/shard_map/rik,rkj->rij/dot_general | solution.py:56
  398.8 0.0 copy-done.3
  398.8 0.0 copy-start.1
  398.8 4.5 %fusion.14 = f32[32,128,128]{2,1,0:T(8,128)S(1)} fusion(f32[32,128,128]{2,1,0:T(8,128)S(1)} %bitcast.75, f32[32,128,128]{1,2,0:T(8,128)S(1)} %copy-done.3), kind=kOutput, calls=%fused_computation.52 | convolution fusion | flops 805306368 | bytes 6291456 | tf_op jit(solution)/shard_map/rik,rkj->rij/dot_general | solution.py:56
  403.3 0.0 copy-done.1
  403.3 4.5 %fusion.13 = f32[32,128,128]{2,1,0:T(8,128)S(1)} fusion(f32[32,128,128]{2,1,0:T(8,128)S(1)} %bitcast.74, f32[32,128,128]{1,2,0:T(8,128)S(1)} %copy-done.1), kind=kOutput, calls=%fused_computation.51 | convolution fusion | flops 805306368 | bytes 6291456 | tf_op jit(solution)/shard_map/rik,rkj->rij/dot_general | solution.py:56
  407.9 6.0 %add_bitcast_fusion = f32[32,1,128,128]{3,2,1,0:T(8,128)} fusion(f32[32,128,128]{2,1,0:T(8,128)S(1)} %fusion.15, f32[32,128,128]{2,1,0:T(8,128)S(1)} %fusion.14, f32[32,128,128]{2,1,0:T(8,128)S(1)} %fusion.13, f32[32,128,128]{2,1,0:T(8,128)S(1)} %bitcast.77, f32[32,128,128]{1,2,0:T(8,128)S(1)} %copy-done.4, pred[32]{0:T(512)(128)(4,1)S(1)} %get-tuple-element.20, ...), kind=kOutput, calls=%fused_computation.12 | convolution fusion | flops 808976384 | bytes 12583040 | tf_op jit(solution)/shard_map/rik,rkj->rij/dot_general | solution.py:56
  (18 shorter events, 0.1 us)
Async XLA Ops:
  6.5 1.9 copy-start.6
  8.5 1.3 copy-start
  8.5 6.5 %copy-start.5 = (s32[32,1]{0,1:T(1,128)S(1)}, s32[32,1]{0,1:T(1,128)}, u32[]{:S(2)}) copy-start(s32[32,1]{0,1:T(1,128)} %param.4) | copy-start | bytes 388
  9.8 142.1 %collective-permute-start = (f32[32,128,128]{1,2,0:T(8,128)S(1)}, f32[32,128,128]{1,2,0:T(8,128)}, u32[]{:S(2)}, u32[]{:S(2)}) collective-permute-start(f32[32,128,128]{1,2,0:T(8,128)S(1)} %bitcast_multiply_fusion), channel_id=1, source_target_pairs={{0,0},{16,1},{32,2},{48,3},{64,4},{80,5},{96,6},{112,7},{128,8},{1... | collective-permute-start | bytes 6291464 | tf_op jit(solution)/shard_map/ppermute | solution.py:17
  160.2 115.3 %copy-start.7 = (u32[256]{0:T(256)S(1)}, u32[256]{0:T(256)}, u32[]{:S(2)}) copy-start(u32[256]{0:T(256)} %constant.74) | copy-start | bytes 3076
  160.2 55.5 %all-to-all-start = ((f32[16,2,128,128]{3,2,1,0:T(8,128)}), f32[16,2,128,128]{3,2,1,0:T(8,128)}, u32[]{:S(2)}, u32[]{:S(2)}) async-start(f32[16,2,128,128]{3,2,1,0:T(8,128)} %copy.22), calls=%async_computation | async-start | bytes 4194304 | tf_op jit(solution)/shard_map/all_to_all | solution.py:37
  168.1 221.7 %all-gather.4.cloned.1.call-start = ((), (), s32[]{:S(2)}) async-start(), calls=%async_computation.1 | async-start | bytes 8912896 | tf_op jit(solution)/shard_map/all_gather | solution.py:40
  218.7 56.8 %collective-permute-start.2 = (f32[32,128,128]{1,2,0:T(8,128)S(1)}, f32[32,128,128]{1,2,0:T(8,128)}, u32[]{:S(2)}, u32[]{:S(2)}) collective-permute-start(f32[32,128,128]{1,2,0:T(8,128)S(1)} %bitcast_add_fusion), channel_id=1, source_target_pairs={{32,0},{48,16},{64,32},{80,48},{96,64},{112,80},{128,96},{144,112}... | collective-permute-start | bytes 6291464 | tf_op jit(solution)/shard_map/ppermute | solution.py:12
  224.8 157.8 %collective-permute-start.1 = (f32[32,128,128]{1,2,0:T(8,128)S(1)}, f32[32,128,128]{1,2,0:T(8,128)}, u32[]{:S(2)}, u32[]{:S(2)}) collective-permute-start(f32[32,128,128]{1,2,0:T(8,128)S(1)} %bitcast_add_fusion), channel_id=1, source_target_pairs={{16,0},{32,16},{48,32},{64,48},{80,64},{96,80},{112,96},{128,112},... | collective-permute-start | bytes 6291464 | tf_op jit(solution)/shard_map/ppermute | solution.py:12
  275.5 110.7 %collective-permute-start.3 = (f32[32,128,128]{1,2,0:T(8,128)}, f32[32,128,128]{1,2,0:T(8,128)}, u32[]{:S(2)}, u32[]{:S(2)}) collective-permute-start(f32[32,128,128]{1,2,0:T(8,128)} %collective-permute-done.2), channel_id=1, source_target_pairs={{16,0},{32,16},{48,32},{64,48},{80,64},{96,80},{112,96},{128,112},... | collective-permute-start | bytes 6291464 | tf_op jit(solution)/shard_map/ppermute | solution.py:12
  389.8 4.4 %copy-start.2 = (f32[32,128,128]{1,2,0:T(8,128)S(1)}, f32[32,128,128]{1,2,0:T(8,128)}, u32[]{:S(2)}) copy-start(f32[32,128,128]{1,2,0:T(8,128)} %gather_fusion.7) | copy-start | bytes 6291460
  394.2 4.5 %copy-start.3 = (f32[32,128,128]{1,2,0:T(8,128)S(1)}, f32[32,128,128]{1,2,0:T(8,128)}, u32[]{:S(2)}) copy-start(f32[32,128,128]{1,2,0:T(8,128)} %gather_fusion.5) | copy-start | bytes 6291460
  398.8 4.5 %copy-start.1 = (f32[32,128,128]{1,2,0:T(8,128)S(1)}, f32[32,128,128]{1,2,0:T(8,128)}, u32[]{:S(2)}) copy-start(f32[32,128,128]{1,2,0:T(8,128)} %gather_fusion.3) | copy-start | bytes 6291460
  403.3 4.5 %copy-start.4 = (f32[32,128,128]{1,2,0:T(8,128)S(1)}, f32[32,128,128]{1,2,0:T(8,128)}, u32[]{:S(2)}) copy-start(f32[32,128,128]{1,2,0:T(8,128)} %gather_fusion.9) | copy-start | bytes 6291460
Sparse Core Ops, SparseCore 0:
  218.9 168.5 all-gather.3

commit v3 on v2

--- a/solution.py
+++ b/solution.py
@@ -23,20 +23,30 @@
     local_rows = stored_blocks.shape[0]
     bs = stored_blocks.shape[-1]
     row_index = lax.axis_index("row")
+    col_index = lax.axis_index("col")
 
     row_cols = lax.all_gather(block_cols, "col", axis=1, tiled=True)
     col_cols = lax.all_gather(block_cols, "row", axis=0, tiled=True)[:, 0]
 
     held = stored_blocks[:, 0] * storage_map.astype(jnp.float32)[:, :, None]
     arrived = transposed(held, rows, cols)
-    mirrored = arrived[block_cols[:, 0]]
-    density = held + jnp.swapaxes(mirrored, 1, 2)
+    density = held + jnp.swapaxes(arrived[block_cols[:, 0]], 1, 2)
 
+    inverse = jnp.zeros((local_rows,), jnp.int32).at[block_cols[:, 0]].set(
+        jnp.arange(local_rows, dtype=jnp.int32)
+    )
+    mirror_out = jnp.swapaxes(held[inverse], 1, 2)
     chunk = local_rows // cols
-    pieces = density.reshape(cols, chunk, bs, bs)
-    spread = lax.all_to_all(pieces, "col", 0, 0, tiled=True)
-    window = (row_index + jnp.arange(STEPS, dtype=jnp.int32)) % cols
-    mine = spread[window]
+    pieces = jnp.stack([held, mirror_out]).reshape(2, cols, chunk, bs, bs)
+    spread = lax.all_to_all(pieces, "col", 1, 1, tiled=True)
+    mine = []
+    for step in range(STEPS):
+        own = lax.dynamic_index_in_dim(spread[0], (row_index + step) % cols, 0, keepdims=False)
+        far = lax.dynamic_index_in_dim(spread[1], (row_index - step) % cols, 0, keepdims=False)
+        if step:
+            far = shifted(far, "row", step)
+        mine.append(own + far)
+    mine = jnp.stack(mine)
     left_all = lax.all_gather(mine, "col", axis=0, tiled=False)
     left_all = jnp.transpose(left_all, (1, 0, 2, 3, 4)).reshape(STEPS, local_rows, bs, bs)
 

time: 422 us -> 503 us (1.19)
  waiting for transfers between devices: 235 us -> 322 us
  blocking collectives: 97.1 us -> 57.5 us
  starting transfers between devices: 19.1 us -> 37.3 us
  other arithmetic: 2.75 us -> 12.3 us
  local copies, waits for them, and re-layouts: 32.6 us -> 38.1 us
    all_to_all x1, waiting for transfers between devices: 47.6 us -> 96.6 us  [shards(): spread = lax.all_to_all(pieces, 'col', 1, 1, tiled=True)]
    unnamed x1, blocking collectives: 58.5 us -> 15.4 us
    ppermute x1, waiting for transfers between devices: 137 us -> 159 us  [transposed(): return lax.ppermute(block, ('row', 'col'), route)]
    ppermute x3 -> x6, starting transfers between devices: 6.08 us -> 25.1 us  [shifted(): return lax.ppermute(block, axis, route)]
    ppermute x3 -> x6, waiting for transfers between devices: 50.7 us -> 66.8 us  [shifted(): return lax.ppermute(block, axis, route)]
  transfers between devices with their start and end apart: 6 -> 9, of which waited for: 3 -> 5; matrix products, arithmetic and copies ran while one was open for 4% -> 5% of each run, Pallas kernels for 0% -> 0%
where the time goes in v3:
time: 503 us; the launch traced here: 501 us
  waiting for transfers between devices  322 us (64%)
  blocking collectives  57.5 us (11%)
  local copies, waits for them, and re-layouts  38.1 us (8%)
  starting transfers between devices  37.3 us (7%)
  matrix products  19.5 us (4%)
  between operations  14.4 us (3%)
  other arithmetic  12.3 us (2%)
    ppermute x1, waiting for transfers between devices, transposed(): return lax.ppermute(block, ('row', 'col'), route)  159 us
    all_to_all x1, waiting for transfers between devices, shards(): spread = lax.all_to_all(pieces, 'col', 1, 1, tiled=True)  96.6 us
    ppermute x6, waiting for transfers between devices, shifted(): return lax.ppermute(block, axis, route)  66.8 us
    all_gather x1, blocking collectives, shards(): row_cols = lax.all_gather(block_cols, 'col', axis=1, tiled=True)  42.1 us
    ppermute x6, starting transfers between devices, shifted(): return lax.ppermute(block, axis, route)  25.1 us
    dot_general x4, matrix products, shards(): jnp.einsum('rik,rkj->rij', left_all[step], right, precision=lax.Precision...  19.5 us
    unnamed x1, blocking collectives  15.4 us
    gather x4, local copies, waits for them, and re-layouts, shards(): right = rights[step][inner]  13.1 us
  transfers between devices with their start and end apart: 9, of which 5 were waited for; matrix products, arithmetic and copies ran while one was open for 5% of the time, Pallas kernels for 0%

profile of v3, /device:TPU:2, one launch (start us, length us, event | category | flops | bytes accessed | tf_op | source)
XLA Modules:
  0.0 501.1 jit_solution(3726696630393694125)
XLA Ops:
  6.5 0.7 convert_bitcast_fusion
  7.2 0.7 convert_reduce_fusion
  7.9 1.9 copy.13
  9.8 0.7 scatter_custom_fusion
  10.5 0.1 mul.37
  10.6 1.5 bitcast_multiply_fusion
  12.2 3.6 gather_fusion.1
  15.8 1.9 broadcast_multiply_fusion
  17.7 0.3 copy-done.3
  18.0 2.3 pad_maximum_fusion
  20.2 10.2 %all-to-all-start = ((f32[2,16,2,128,128]{4,3,2,0,1:T(8,128)}), f32[2,16,2,128,128]{4,3,2,0,1:T(8,128)}, u32[]{:S(2)}, u32[]{:S(2)}) async-start(f32[2,16,2,128,128]{4,3,2,0,1:T(8,128)} %pad_maximum_fusion), calls=%async_computation | async-start | bytes 8388608 | tf_op jit(solution)/shard_map/all_to_all | solution.py:41
  30.4 0.0 all-gather.4.cloned.1.call-start
  30.6 96.6 %all-to-all-done = f32[2,16,2,128,128]{4,3,2,0,1:T(8,128)} async-done(((f32[2,16,2,128,128]{4,3,2,0,1:T(8,128)}), f32[2,16,2,128,128]{4,3,2,0,1:T(8,128)}, u32[]{:S(2)}, u32[]{:S(2)}) %all-to-all-start) | async-done | bytes 4194336 | tf_op jit(solution)/shard_map/all_to_all | solution.py:41
  127.1 2.5 fusion.15
  129.7 1.3 copy-done.4
  131.0 0.2 collective-permute-start
  131.3 3.0 collective-permute-start.1
  134.3 1.1 collective-permute-start.2
  135.4 5.2 %collective-permute-done.1 = f32[2,128,128]{2,1,0:T(8,128)S(1)} collective-permute-done((f32[2,128,128]{2,1,0:T(8,128)S(1)}, f32[2,128,128]{2,1,0:T(8,128)S(1)}, u32[]{:S(2)}, u32[]{:S(2)}) %collective-permute-start.1) | collective-permute-done | bytes 131104 | tf_op jit(solution)/shard_map/ppermute | solution.py:12
  140.6 1.3 collective-permute-done.2
  141.8 1.1 fusion.2
  142.9 0.9 pad_maximum_fusion.1
  143.8 1.9 collective-permute-start.3
  145.7 158.7 %collective-permute-done.3 = f32[32,128,128]{1,2,0:T(8,128)} collective-permute-done((f32[32,128,128]{1,2,0:T(8,128)}, f32[32,128,128]{1,2,0:T(8,128)}, u32[]{:S(2)}, u32[]{:S(2)}) %collective-permute-start.3) | collective-permute-done | bytes 2097184 | tf_op jit(solution)/shard_map/ppermute | solution.py:17
  304.5 3.1 copy.15
  307.5 3.7 gather_fusion.2
  311.2 3.2 bitcast_add_fusion
  314.4 6.1 %collective-permute-start.4 = (f32[32,128,128]{1,2,0:T(8,128)}, f32[32,128,128]{1,2,0:T(8,128)}, u32[]{:S(2)}, u32[]{:S(2)}) collective-permute-start(f32[32,128,128]{1,2,0:T(8,128)} %bitcast_add_fusion), channel_id=1, source_target_pairs={{16,0},{32,16},{48,32},{64,48},{80,64},{96,80},{112,96},{128,112},... | collective-permute-start | bytes 6291464 | tf_op jit(solution)/shard_map/ppermute | solution.py:12
  320.5 60.3 %collective-permute-done.5 = f32[32,128,128]{1,2,0:T(8,128)} collective-permute-done((f32[32,128,128]{1,2,0:T(8,128)}, f32[32,128,128]{1,2,0:T(8,128)}, u32[]{:S(2)}, u32[]{:S(2)}) %collective-permute-start.5) | collective-permute-done | bytes 2097184 | tf_op jit(solution)/shard_map/ppermute | solution.py:12
  380.8 14.7 %collective-permute-start.6 = (f32[32,128,128]{1,2,0:T(8,128)}, f32[32,128,128]{1,2,0:T(8,128)}, u32[]{:S(2)}, u32[]{:S(2)}) collective-permute-start(f32[32,128,128]{1,2,0:T(8,128)} %collective-permute-done.5), channel_id=1, source_target_pairs={{16,0},{32,16},{48,32},{64,48},{80,64},{96,80},{112,96},{128,112},... | collective-permute-start | bytes 6291464 | tf_op jit(solution)/shard_map/ppermute | solution.py:12
  395.4 0.7 dynamic-slice.12
  396.8 42.1 %all-gather.1 = s32[16,1,32]{2,1,0:T(1,128)S(1)} all-gather(s32[1,1,32]{2,1,0:T(1,128)S(1)} %bitcast.100), channel_id=1, replica_groups=mesh['row'=16,'col'=16] {'col'}, dimensions={0}, use_global_device_ids=true | all-gather | bytes 2176 | tf_op jit(solution)/shard_map/all_gather | solution.py:28
  438.9 0.1 bitcast_dynamic-update-slice_fusion
  439.0 15.4 %all-reduce = s32[512]{0:T(512)S(1)} all-reduce(s32[512]{0:T(512)S(1)} %bitcast_dynamic-update-slice_fusion), channel_id=1, replica_groups=mesh['row'=16,'col'=16] {'row'}, use_global_device_ids=true, to_apply=%add | all-reduce | flops 512 | bytes 4096
  454.4 0.1 fusion.16
  454.5 0.7 gather_fusion
  455.2 0.7 gather_fusion.4
  455.9 0.7 gather_fusion.6
  456.6 0.7 gather_fusion.8
  457.3 3.6 gather_fusion.3
  460.9 2.3 gather_fusion.7
  463.2 3.6 gather_fusion.5
  466.8 3.7 gather_fusion.9
  470.4 4.2 fusion.14
  474.7 4.5 fusion.18
  479.2 4.5 fusion.17
  483.7 4.5 fusion.19
  488.2 6.0 %add_bitcast_fusion = f32[32,1,128,128]{3,2,1,0:T(8,128)} fusion(f32[32,128,128]{2,1,0:T(8,128)S(1)} %fusion.19, f32[32,128,128]{2,1,0:T(8,128)S(1)} %fusion.18, f32[32,128,128]{2,1,0:T(8,128)S(1)} %fusion.17, f32[32,128,128]{2,1,0:T(8,128)S(1)} %bitcast.99, f32[32,128,128]{1,2,0:T(8,128)S(1)} %copy-done.2, pred[32]{0:T(512)(128)(4,1)S(1)} %get-tuple-element.29, ...), kind=kOutput, calls=%fused_computation.14 | convolution fusion | flops 808976384 | bytes 12583040 | tf_op jit(solution)/shard_map/rik,rkj->rij/dot_general | solution.py:66
  (31 shorter events, 0.1 us)
Async XLA Ops:
  7.9 1.9 copy-start.5
  15.8 2.2 copy-start.3
  20.2 106.9 %all-to-all-start = ((f32[2,16,2,128,128]{4,3,2,0,1:T(8,128)}), f32[2,16,2,128,128]{4,3,2,0,1:T(8,128)}, u32[]{:S(2)}, u32[]{:S(2)}) async-start(f32[2,16,2,128,128]{4,3,2,0,1:T(8,128)} %pad_maximum_fusion), calls=%async_computation | async-start | bytes 8388608 | tf_op jit(solution)/shard_map/all_to_all | solution.py:41
  30.4 440.0 %all-gather.4.cloned.1.call-start = ((), (), s32[]{:S(2)}) async-start(), calls=%async_computation.1 | async-start | bytes 8912896 | tf_op jit(solution)/shard_map/all_gather | solution.py:50
  129.6 1.3 copy-start.4
  131.0 4.4 collective-permute-start
  131.3 9.3 %collective-permute-start.1 = (f32[2,128,128]{2,1,0:T(8,128)S(1)}, f32[2,128,128]{2,1,0:T(8,128)S(1)}, u32[]{:S(2)}, u32[]{:S(2)}) collective-permute-start(f32[2,128,128]{2,1,0:T(8,128)S(1)} %get-tuple-element.13), channel_id=1, source_target_pairs={{32,0},{48,16},{64,32},{80,48},{96,64},{112,80},{128,96},{144,112}... | collective-permute-start | bytes 393224 | tf_op jit(solution)/shard_map/ppermute | solution.py:12
  134.3 7.5 %collective-permute-start.2 = (f32[2,128,128]{2,1,0:T(8,128)S(1)}, f32[2,128,128]{2,1,0:T(8,128)S(1)}, u32[]{:S(2)}, u32[]{:S(2)}) collective-permute-start(f32[2,128,128]{2,1,0:T(8,128)S(1)} %get-tuple-element.12), channel_id=1, source_target_pairs={{48,0},{64,16},{80,32},{96,48},{112,64},{128,80},{144,96},{160,112... | collective-permute-start | bytes 393224 | tf_op jit(solution)/shard_map/ppermute | solution.py:12
  143.8 160.7 %collective-permute-start.3 = (f32[32,128,128]{1,2,0:T(8,128)}, f32[32,128,128]{1,2,0:T(8,128)}, u32[]{:S(2)}, u32[]{:S(2)}) collective-permute-start(f32[32,128,128]{1,2,0:T(8,128)} %bitcast_multiply_fusion), channel_id=1, source_target_pairs={{0,0},{16,1},{32,2},{48,3},{64,4},{80,5},{96,6},{112,7},{128,8},{1... | collective-permute-start | bytes 6291464 | tf_op jit(solution)/shard_map/ppermute | solution.py:17
  311.2 84.3 %copy-start.6 = (u32[256]{0:T(256)S(1)}, u32[256]{0:T(256)}, u32[]{:S(2)}) copy-start(u32[256]{0:T(256)} %constant.118) | copy-start | bytes 3076
  314.4 66.4 %collective-permute-start.5 = (f32[32,128,128]{1,2,0:T(8,128)}, f32[32,128,128]{1,2,0:T(8,128)}, u32[]{:S(2)}, u32[]{:S(2)}) collective-permute-start(f32[32,128,128]{1,2,0:T(8,128)} %bitcast_add_fusion), channel_id=1, source_target_pairs={{32,0},{48,16},{64,32},{80,48},{96,64},{112,80},{128,96},{144,112}... | collective-permute-start | bytes 6291464 | tf_op jit(solution)/shard_map/ppermute | solution.py:12
  314.4 148.8 %collective-permute-start.4 = (f32[32,128,128]{1,2,0:T(8,128)}, f32[32,128,128]{1,2,0:T(8,128)}, u32[]{:S(2)}, u32[]{:S(2)}) collective-permute-start(f32[32,128,128]{1,2,0:T(8,128)} %bitcast_add_fusion), channel_id=1, source_target_pairs={{16,0},{32,16},{48,32},{64,48},{80,64},{96,80},{112,96},{128,112},... | collective-permute-start | bytes 6291464 | tf_op jit(solution)/shard_map/ppermute | solution.py:12
  380.8 86.0 %collective-permute-start.6 = (f32[32,128,128]{1,2,0:T(8,128)}, f32[32,128,128]{1,2,0:T(8,128)}, u32[]{:S(2)}, u32[]{:S(2)}) collective-permute-start(f32[32,128,128]{1,2,0:T(8,128)} %collective-permute-done.5), channel_id=1, source_target_pairs={{16,0},{32,16},{48,32},{64,48},{80,64},{96,80},{112,96},{128,112},... | collective-permute-start | bytes 6291464 | tf_op jit(solution)/shard_map/ppermute | solution.py:12
  470.4 4.2 copy-start.1
  474.7 4.5 copy-start
  483.7 4.5 copy-start.2
Sparse Core Ops, SparseCore 0:
  143.9 279.5 all-gather.3

commit v4 on v3

--- a/solution.py
+++ b/solution.py
@@ -29,9 +29,6 @@
     col_cols = lax.all_gather(block_cols, "row", axis=0, tiled=True)[:, 0]
 
     held = stored_blocks[:, 0] * storage_map.astype(jnp.float32)[:, :, None]
-    arrived = transposed(held, rows, cols)
-    density = held + jnp.swapaxes(arrived[block_cols[:, 0]], 1, 2)
-
     inverse = jnp.zeros((local_rows,), jnp.int32).at[block_cols[:, 0]].set(
         jnp.arange(local_rows, dtype=jnp.int32)
     )
@@ -39,6 +36,10 @@
     chunk = local_rows // cols
     pieces = jnp.stack([held, mirror_out]).reshape(2, cols, chunk, bs, bs)
     spread = lax.all_to_all(pieces, "col", 1, 1, tiled=True)
+    first = jnp.swapaxes(spread[0], 0, 1)
+    second = lax.all_to_all(first, "row", 1, 1, tiled=True)
+    arrived = lax.all_to_all(second, "col", 1, 0, tiled=True).reshape(local_rows, bs, bs)
+    density = held + jnp.swapaxes(arrived[block_cols[:, 0]], 1, 2)
     mine = []
     for step in range(STEPS):
         own = lax.dynamic_index_in_dim(spread[0], (row_index + step) % cols, 0, keepdims=False)

time: 503 us -> 428 us (0.85)
  waiting for transfers between devices: 322 us -> 222 us
  blocking collectives: 57.5 us -> 93.7 us
  starting transfers between devices: 37.3 us -> 25.1 us
    ppermute x1 -> x0, waiting for transfers between devices: 159 us -> none  [transposed(): return lax.ppermute(block, ('row', 'col'), route)]
    all_to_all x0 -> x1, waiting for transfers between devices: none -> 60.4 us  [shards(): lax.all_to_all(second, 'col', 1, 0, tiled=True).reshape(local_rows, bs, bs)]
    all_to_all x0 -> x1, blocking collectives: none -> 37.8 us  [shards(): second = lax.all_to_all(first, 'row', 1, 1, tiled=True)]
    ppermute x6, starting transfers between devices: 25.1 us -> 6.89 us  [shifted(): return lax.ppermute(block, axis, route)]
    all_to_all x0 -> x1, starting transfers between devices: none -> 7.94 us  [shards(): lax.all_to_all(second, 'col', 1, 0, tiled=True).reshape(local_rows, bs, bs)]
  transfers between devices with their start and end apart: 9 -> 9, of which waited for: 5 -> 5; matrix products, arithmetic and copies ran while one was open for 5% -> 6% of each run, Pallas kernels for 0% -> 0%
where the time goes in v4:
time: 428 us
  waiting for transfers between devices  222 us (52%)
  blocking collectives  93.7 us (22%)
  local copies, waits for them, and re-layouts  36.3 us (8%)
  starting transfers between devices  25.1 us (6%)
  matrix products  19.5 us (5%)
  other arithmetic  16.6 us (4%)
  between operations  14.3 us (3%)
    all_to_all x1, waiting for transfers between devices, shards(): spread = lax.all_to_all(pieces, 'col', 1, 1, tiled=True)  96.6 us
    ppermute x6, waiting for transfers between devices, shifted(): return lax.ppermute(block, axis, route)  65 us
    all_to_all x1, waiting for transfers between devices, shards(): lax.all_to_all(second, 'col', 1, 0, tiled=True).reshape(local_rows, bs, bs)  60.4 us
    all_gather x1, blocking collectives, shards(): row_cols = lax.all_gather(block_cols, 'col', axis=1, tiled=True)  43.3 us
    all_to_all x1, blocking collectives, shards(): second = lax.all_to_all(first, 'row', 1, 1, tiled=True)  37.8 us
    dot_general x4, matrix products, shards(): jnp.einsum('rik,rkj->rij', left_all[step], right, precision=lax.Precision...  19.5 us
    gather x4, local copies, waits for them, and re-layouts, shards(): right = rights[step][inner]  13.1 us
    unnamed x1, blocking collectives  12.6 us
  transfers between devices with their start and end apart: 9, of which 5 were waited for; matrix products, arithmetic and copies ran while one was open for 6% of the time, Pallas kernels for 0%

profile of v4, /device:TPU:2, one launch (start us, length us, event | category | flops | bytes accessed | tf_op | source)
XLA Modules:
  0.0 427.5 jit_solution(16615896986640400140)
XLA Ops:
  6.5 0.7 convert_bitcast_fusion
  7.2 0.7 convert_reduce_fusion
  7.9 0.7 fusion.4
  8.5 0.7 scatter_custom_fusion
  9.2 0.1 mul.37
  9.3 1.9 copy.14
  11.2 3.2 broadcast_multiply_fusion
  14.4 1.5 bitcast_multiply_fusion
  15.9 3.6 gather_fusion.1
  19.6 4.7 %pad_maximum_fusion = f32[2,16,2,128,128]{4,3,2,0,1:T(8,128)} fusion(f32[1,16,2,128,128]{4,3,2,0,1:T(8,128)} %bitcast.105, f32[1,16,2,128,128]{4,3,2,0,1:T(8,128)} %broadcast_multiply_fusion), kind=kLoop, calls=%fused_computation.11 | loop fusion | flops 1048576 | bytes 8388608 | tf_op jit(solution)/shard_map/stack | solution.py:37
  24.2 10.2 %all-to-all-start = ((f32[2,16,2,128,128]{4,3,2,0,1:T(8,128)}), f32[2,16,2,128,128]{4,3,2,0,1:T(8,128)}, u32[]{:S(2)}, u32[]{:S(2)}) async-start(f32[2,16,2,128,128]{4,3,2,0,1:T(8,128)} %pad_maximum_fusion), calls=%async_computation | async-start | bytes 8388608 | tf_op jit(solution)/shard_map/all_to_all | solution.py:38
  34.4 0.0 all-gather.4.cloned.1.call-start
  34.6 96.6 %all-to-all-done = f32[2,16,2,128,128]{4,3,2,0,1:T(8,128)} async-done(((f32[2,16,2,128,128]{4,3,2,0,1:T(8,128)}), f32[2,16,2,128,128]{4,3,2,0,1:T(8,128)}, u32[]{:S(2)}, u32[]{:S(2)}) %all-to-all-start) | async-done | bytes 4194336 | tf_op jit(solution)/shard_map/all_to_all | solution.py:38
  131.1 4.1 slice_bitcast_fusion
  135.3 1.3 copy-done.3
  136.7 1.8 collective-permute-start.2
  138.5 1.4 collective-permute-start.1
  139.9 2.2 collective-permute-start
  142.1 0.0 collective-permute-done.2
  142.1 2.8 collective-permute-done.1
  144.9 0.3 collective-permute-done
  145.2 1.1 fusion.2
  146.3 0.9 pad_maximum_fusion.1
  147.2 37.8 %all_to_all.25 = f32[2,16,128,128]{3,2,0,1:T(8,128)} all-to-all(f32[2,16,128,128]{3,2,0,1:T(8,128)} %get-tuple-element.9), channel_id=1, replica_groups=mesh['row'=16,'col'=16] {'row'}, dimensions={1} | all-to-all | bytes 4194304 | tf_op jit(solution)/shard_map/all_to_all | solution.py:40
  185.0 7.9 %all-to-all-start.2 = ((f32[2,16,128,128]{3,2,0,1:T(8,128)}), f32[2,16,128,128]{3,2,0,1:T(8,128)}, u32[]{:S(2)}, u32[]{:S(2)}) async-start(f32[2,16,128,128]{3,2,0,1:T(8,128)} %all_to_all.25), calls=%async_computation.2 | async-start | bytes 4194304 | tf_op jit(solution)/shard_map/all_to_all | solution.py:41
  192.9 60.4 %all-to-all-done.2 = f32[2,16,128,128]{3,2,0,1:T(8,128)} async-done(((f32[2,16,128,128]{3,2,0,1:T(8,128)}), f32[2,16,128,128]{3,2,0,1:T(8,128)}, u32[]{:S(2)}, u32[]{:S(2)}) %all-to-all-start.2) | async-done | bytes 2097184 | tf_op jit(solution)/shard_map/all_to_all | solution.py:41
  253.4 3.6 gather_fusion.2
  257.0 3.2 bitcast_add_fusion
  260.2 1.5 collective-permute-start.4
  261.6 61.9 %collective-permute-done.4 = f32[32,128,128]{1,2,0:T(8,128)} collective-permute-done((f32[32,128,128]{1,2,0:T(8,128)}, f32[32,128,128]{1,2,0:T(8,128)}, u32[]{:S(2)}, u32[]{:S(2)}) %collective-permute-start.4) | collective-permute-done | bytes 2097184 | tf_op jit(solution)/shard_map/ppermute | solution.py:12
  323.5 0.7 dynamic-slice.12
  324.9 43.3 %all-gather.1 = s32[16,1,32]{2,1,0:T(1,128)S(1)} all-gather(s32[1,1,32]{2,1,0:T(1,128)S(1)} %bitcast.110), channel_id=1, replica_groups=mesh['row'=16,'col'=16] {'col'}, dimensions={0}, use_global_device_ids=true | all-gather | bytes 2176 | tf_op jit(solution)/shard_map/all_gather | solution.py:28
  368.1 0.1 bitcast_dynamic-update-slice_fusion
  368.2 12.6 %all-reduce = s32[512]{0:T(512)S(1)} all-reduce(s32[512]{0:T(512)S(1)} %bitcast_dynamic-update-slice_fusion), channel_id=1, replica_groups=mesh['row'=16,'col'=16] {'row'}, use_global_device_ids=true, to_apply=%add | all-reduce | flops 512 | bytes 4096
  380.9 0.1 fusion.15
  380.9 0.7 gather_fusion.8
  381.6 0.7 gather_fusion.6
  382.4 0.7 gather_fusion.4
  383.1 0.7 gather_fusion
  383.8 3.6 gather_fusion.3
  387.4 2.3 gather_fusion.7
  389.6 3.6 gather_fusion.5
  393.2 3.7 gather_fusion.9
  396.9 4.2 fusion.14
  401.1 4.5 %fusion.16 = f32[32,128,128]{2,1,0:T(8,128)S(1)} fusion(f32[32,128,128]{2,1,0:T(8,128)S(1)} %bitcast.108, f32[32,128,128]{1,2,0:T(8,128)S(1)} %copy-done), kind=kOutput, calls=%fused_computation.64 | convolution fusion | flops 805306368 | bytes 6291456 | tf_op jit(solution)/shard_map/rik,rkj->rij/dot_general | solution.py:67
  405.7 4.5 %fusion.18 = f32[32,128,128]{2,1,0:T(8,128)S(1)} fusion(f32[32,128,128]{2,1,0:T(8,128)S(1)} %bitcast.107, f32[32,128,128]{1,2,0:T(8,128)S(1)} %gather_fusion.7), kind=kOutput, calls=%fused_computation.66 | convolution fusion | flops 805306368 | bytes 6291456 | tf_op jit(solution)/shard_map/rik,rkj->rij/dot_general | solution.py:67
  410.2 4.5 %fusion.17 = f32[32,128,128]{2,1,0:T(8,128)S(1)} fusion(f32[32,128,128]{2,1,0:T(8,128)S(1)} %bitcast.106, f32[32,128,128]{1,2,0:T(8,128)S(1)} %copy-done.1), kind=kOutput, calls=%fused_computation.65 | convolution fusion | flops 805306368 | bytes 6291456 | tf_op jit(solution)/shard_map/rik,rkj->rij/dot_general | solution.py:67
  414.7 6.0 %add_bitcast_fusion = f32[32,1,128,128]{3,2,1,0:T(8,128)} fusion(f32[32,128,128]{2,1,0:T(8,128)S(1)} %fusion.18, f32[32,128,128]{2,1,0:T(8,128)S(1)} %fusion.17, f32[32,128,128]{2,1,0:T(8,128)S(1)} %fusion.16, f32[32,128,128]{2,1,0:T(8,128)S(1)} %bitcast.109, f32[32,128,128]{1,2,0:T(8,128)S(1)} %copy-done.2, pred[32]{0:T(512)(128)(4,1)S(1)} %get-tuple-element.30, ...), kind=kOutput, calls=%fused_computation.14 | convolution fusion | flops 808976384 | bytes 12583040 | tf_op jit(solution)/shard_map/rik,rkj->rij/dot_general | solution.py:67
  (29 shorter events, 0.1 us)
Async XLA Ops:
  24.2 106.9 %all-to-all-start = ((f32[2,16,2,128,128]{4,3,2,0,1:T(8,128)}), f32[2,16,2,128,128]{4,3,2,0,1:T(8,128)}, u32[]{:S(2)}, u32[]{:S(2)}) async-start(f32[2,16,2,128,128]{4,3,2,0,1:T(8,128)} %pad_maximum_fusion), calls=%async_computation | async-start | bytes 8388608 | tf_op jit(solution)/shard_map/all_to_all | solution.py:38
  34.4 362.5 %all-gather.4.cloned.1.call-start = ((), (), s32[]{:S(2)}) async-start(), calls=%async_computation.3 | async-start | bytes 8912896 | tf_op jit(solution)/shard_map/all_gather | solution.py:51
  135.3 1.3 copy-start.3
  136.7 5.5 %collective-permute-start.2 = (f32[2,128,128]{2,1,0:T(8,128)S(1)}, f32[2,128,128]{2,1,0:T(8,128)S(1)}, u32[]{:S(2)}, u32[]{:S(2)}) collective-permute-start(f32[2,128,128]{2,1,0:T(8,128)S(1)} %get-tuple-element.13), channel_id=1, source_target_pairs={{48,0},{64,16},{80,32},{96,48},{112,64},{128,80},{144,96},{160,112... | collective-permute-start | bytes 393224 | tf_op jit(solution)/shard_map/ppermute | solution.py:12
  138.5 6.5 %collective-permute-start.1 = (f32[2,128,128]{2,1,0:T(8,128)S(1)}, f32[2,128,128]{2,1,0:T(8,128)S(1)}, u32[]{:S(2)}, u32[]{:S(2)}) collective-permute-start(f32[2,128,128]{2,1,0:T(8,128)S(1)} %get-tuple-element.14), channel_id=1, source_target_pairs={{32,0},{48,16},{64,32},{80,48},{96,64},{112,80},{128,96},{144,112}... | collective-permute-start | bytes 393224 | tf_op jit(solution)/shard_map/ppermute | solution.py:12
  139.9 5.3 %collective-permute-start = (f32[2,128,128]{2,1,0:T(8,128)S(1)}, f32[2,128,128]{2,1,0:T(8,128)S(1)}, u32[]{:S(2)}, u32[]{:S(2)}) collective-permute-start(f32[2,128,128]{2,1,0:T(8,128)S(1)} %get-tuple-element.15), channel_id=1, source_target_pairs={{16,0},{32,16},{48,32},{64,48},{80,64},{96,80},{112,96},{128,112},... | collective-permute-start | bytes 393224 | tf_op jit(solution)/shard_map/ppermute | solution.py:12
  185.0 68.4 %all-to-all-start.2 = ((f32[2,16,128,128]{3,2,0,1:T(8,128)}), f32[2,16,128,128]{3,2,0,1:T(8,128)}, u32[]{:S(2)}, u32[]{:S(2)}) async-start(f32[2,16,128,128]{3,2,0,1:T(8,128)} %all_to_all.25), calls=%async_computation.2 | async-start | bytes 4194304 | tf_op jit(solution)/shard_map/all_to_all | solution.py:41
  257.0 66.5 %copy-start.5 = (u32[256]{0:T(256)S(1)}, u32[256]{0:T(256)}, u32[]{:S(2)}) copy-start(u32[256]{0:T(256)} %constant.118) | copy-start | bytes 3076
  257.0 67.9 %copy-start.4 = (s32[32,1]{0,1:T(1,128)S(1)}, s32[32,1]{0,1:T(1,128)}, u32[]{:S(2)}) copy-start(s32[32,1]{0,1:T(1,128)} %param.4) | copy-start | bytes 388
  260.2 63.3 %collective-permute-start.4 = (f32[32,128,128]{1,2,0:T(8,128)}, f32[32,128,128]{1,2,0:T(8,128)}, u32[]{:S(2)}, u32[]{:S(2)}) collective-permute-start(f32[32,128,128]{1,2,0:T(8,128)} %bitcast_add_fusion), channel_id=1, source_target_pairs={{32,0},{48,16},{64,32},{80,48},{96,64},{112,80},{128,96},{144,112}... | collective-permute-start | bytes 6291464 | tf_op jit(solution)/shard_map/ppermute | solution.py:12
  261.6 128.0 %collective-permute-start.3 = (f32[32,128,128]{1,2,0:T(8,128)}, f32[32,128,128]{1,2,0:T(8,128)}, u32[]{:S(2)}, u32[]{:S(2)}) collective-permute-start(f32[32,128,128]{1,2,0:T(8,128)} %bitcast_add_fusion), channel_id=1, source_target_pairs={{16,0},{32,16},{48,32},{64,48},{80,64},{96,80},{112,96},{128,112},... | collective-permute-start | bytes 6291464 | tf_op jit(solution)/shard_map/ppermute | solution.py:12
  323.5 69.8 %collective-permute-start.5 = (f32[32,128,128]{1,2,0:T(8,128)}, f32[32,128,128]{1,2,0:T(8,128)}, u32[]{:S(2)}, u32[]{:S(2)}) collective-permute-start(f32[32,128,128]{1,2,0:T(8,128)} %collective-permute-done.4), channel_id=1, source_target_pairs={{16,0},{32,16},{48,32},{64,48},{80,64},{96,80},{112,96},{128,112},... | collective-permute-start | bytes 6291464 | tf_op jit(solution)/shard_map/ppermute | solution.py:12
  396.9 4.2 copy-start
  405.6 4.5 %copy-start.1 = (f32[32,128,128]{1,2,0:T(8,128)S(1)}, f32[32,128,128]{1,2,0:T(8,128)}, u32[]{:S(2)}) copy-start(f32[32,128,128]{1,2,0:T(8,128)} %gather_fusion.5) | copy-start | bytes 6291460
  410.1 4.5 %copy-start.2 = (f32[32,128,128]{1,2,0:T(8,128)S(1)}, f32[32,128,128]{1,2,0:T(8,128)}, u32[]{:S(2)}) copy-start(f32[32,128,128]{1,2,0:T(8,128)} %gather_fusion.9) | copy-start | bytes 6291460
Sparse Core Ops, SparseCore 0:
  147.3 189.6 all-gather.3

commit v5 on v4

--- a/solution.py
+++ b/solution.py
@@ -4,6 +4,7 @@
 from jax.sharding import PartitionSpec as P
 
 STEPS = 4
+EXTRA = 8
 
 
 def shifted(block, axis, distance):
@@ -23,20 +24,22 @@
     local_rows = stored_blocks.shape[0]
     bs = stored_blocks.shape[-1]
     row_index = lax.axis_index("row")
-    col_index = lax.axis_index("col")
-
-    row_cols = lax.all_gather(block_cols, "col", axis=1, tiled=True)
-    col_cols = lax.all_gather(block_cols, "row", axis=0, tiled=True)[:, 0]
 
     held = stored_blocks[:, 0] * storage_map.astype(jnp.float32)[:, :, None]
+    own_cols = block_cols[:, 0]
+    tag = jnp.zeros((local_rows, EXTRA, bs), jnp.float32).at[:, 0, 0].set(own_cols.astype(jnp.float32))
+    blank = jnp.zeros((local_rows, EXTRA, bs), jnp.float32)
     inverse = jnp.zeros((local_rows,), jnp.int32).at[block_cols[:, 0]].set(
         jnp.arange(local_rows, dtype=jnp.int32)
     )
     mirror_out = jnp.swapaxes(held[inverse], 1, 2)
     chunk = local_rows // cols
-    pieces = jnp.stack([held, mirror_out]).reshape(2, cols, chunk, bs, bs)
+    pieces = jnp.stack([
+        jnp.concatenate([held, tag], axis=1),
+        jnp.concatenate([mirror_out, blank], axis=1),
+    ]).reshape(2, cols, chunk, bs + EXTRA, bs)
     spread = lax.all_to_all(pieces, "col", 1, 1, tiled=True)
-    first = jnp.swapaxes(spread[0], 0, 1)
+    first = jnp.swapaxes(spread[0, :, :, :bs], 0, 1)
     second = lax.all_to_all(first, "row", 1, 1, tiled=True)
     arrived = lax.all_to_all(second, "col", 1, 0, tiled=True).reshape(local_rows, bs, bs)
     density = held + jnp.swapaxes(arrived[block_cols[:, 0]], 1, 2)
@@ -49,22 +52,23 @@
         mine.append(own + far)
     mine = jnp.stack(mine)
     left_all = lax.all_gather(mine, "col", axis=0, tiled=False)
-    left_all = jnp.transpose(left_all, (1, 0, 2, 3, 4)).reshape(STEPS, local_rows, bs, bs)
+    left_all = jnp.transpose(left_all, (1, 0, 2, 3, 4)).reshape(STEPS, local_rows, bs + EXTRA, bs)
+    density = jnp.concatenate([density, tag], axis=1)
 
     one = shifted(density, "row", 1)
     two = shifted(density, "row", 2)
     three = shifted(two, "row", 1)
     rights = [density, one, two, three]
 
-    own_cols = block_cols[:, 0]
-    total = jnp.zeros(density.shape, jnp.float32)
+    total = jnp.zeros((local_rows, bs, bs), jnp.float32)
     for step in range(STEPS):
-        kappa = (row_index + step) % cols
-        inner = lax.dynamic_index_in_dim(row_cols, kappa, 1, keepdims=False)
+        left = left_all[step]
+        inner = left[:, bs, 0].astype(jnp.int32)
         right = rights[step][inner]
-        panel_cols = lax.dynamic_slice_in_dim(col_cols, kappa * local_rows, local_rows)
-        match = panel_cols[inner] == own_cols
-        term = jnp.einsum("rik,rkj->rij", left_all[step], right, precision=lax.Precision.HIGHEST)
+        match = right[:, bs, 0].astype(jnp.int32) == own_cols
+        term = jnp.einsum(
+            "rik,rkj->rij", left[:, :bs], right[:, :bs], precision=lax.Precision.HIGHEST
+        )
         total = total + jnp.where(match[:, None, None], term, jnp.float32(0.0))
     return total[:, None]
 

time: 428 us -> 414 us (0.967); the launches traced: 428 us -> 408 us
  blocking collectives: 93.7 us -> 38 us
  local copies, waits for them, and re-layouts: 36.3 us -> 50.8 us
  waiting for transfers between devices: 222 us -> 234 us
  other arithmetic: 16.6 us -> 23.6 us
    all_gather x1 -> x0, blocking collectives: 43.3 us -> none  [shards(): row_cols = lax.all_gather(block_cols, 'col', axis=1, tiled=True)]
    unnamed x1 -> x0, blocking collectives: 12.6 us -> none
    concatenate x0 -> x2, local copies, waits for them, and re-layouts: none -> 6.89 us  [the longest x1 4.99 us: shards(): density = jnp.concatenate([density, tag], axis=1)]
    concatenate x0 -> x2, other arithmetic: none -> 6.5 us  [the longest x1 4.01 us: shards(): jnp.concatenate([held, tag], axis=1)]
    all_to_all x1, waiting for transfers between devices: 96.6 us -> 102 us  [shards(): spread = lax.all_to_all(pieces, 'col', 1, 1, tiled=True)]
    all_gather x1, waiting for transfers between devices: 0.01 us -> 5.18 us  [shards(): left_all = lax.all_gather(mine, 'col', axis=0, tiled=False)]
    slice x1 -> x2, local copies, waits for them, and re-layouts: 4.19 us -> 9.21 us  [the longest x1 6.62 us: shards(): left = left_all[step]]
    another operation x0 -> x1, local copies, waits for them, and re-layouts: none -> 4.99 us  [shards(): jnp.stack([jnp.concatenate([held, tag], axis=1), jnp.concatenate([mirror_...]
  transfers between devices with their start and end apart: 9 -> 9, of which waited for: 5 -> 8; matrix products, arithmetic and copies ran while one was open for 6% -> 12% of each run, Pallas kernels for 0% -> 0%
where the time goes in v5:
time: 414 us; the launch traced here: 408 us
  waiting for transfers between devices  234 us (57%)
  local copies, waits for them, and re-layouts  50.8 us (12%)
  blocking collectives  38 us (9%)
  starting transfers between devices  28.3 us (7%)
  other arithmetic  23.6 us (6%)
  matrix products  19 us (5%)
  between operations  13.7 us (3%)
    all_to_all x1, waiting for transfers between devices, shards(): spread = lax.all_to_all(pieces, 'col', 1, 1, tiled=True)  102 us
    ppermute x6, waiting for transfers between devices, shifted(): return lax.ppermute(block, axis, route)  66.6 us
    all_to_all x1, waiting for transfers between devices, shards(): lax.all_to_all(second, 'col', 1, 0, tiled=True).reshape(local_rows, bs, bs)  60.3 us
    all_to_all x1, blocking collectives, shards(): second = lax.all_to_all(first, 'row', 1, 1, tiled=True)  38 us
    dot_general x4, matrix products, shards(): jnp.einsum('rik,rkj->rij', left[:, :bs], right[:, :bs], precision=lax.Pre...  19 us
    gather x4, local copies, waits for them, and re-layouts, shards(): right = rights[step][inner]  14.8 us
    all_to_all x1, starting transfers between devices, shards(): spread = lax.all_to_all(pieces, 'col', 1, 1, tiled=True)  10.2 us
    all_to_all x1, starting transfers between devices, shards(): lax.all_to_all(second, 'col', 1, 0, tiled=True).reshape(local_rows, bs, bs)  9.26 us
  transfers between devices with their start and end apart: 9, of which 8 were waited for; matrix products, arithmetic and copies ran while one was open for 12% of the time, Pallas kernels for 0%

profile of v5, /device:TPU:2, one launch (start us, length us, event | category | flops | bytes accessed | tf_op | source)
XLA Modules:
  0.0 407.9 jit_solution(14827230112489225621)
XLA Ops:
  6.5 0.7 convert_bitcast_fusion
  7.2 0.7 fusion.25
  7.9 0.7 scatter_custom_fusion
  8.6 1.9 copy.52
  10.6 1.5 bitcast_multiply_fusion
  12.1 3.6 gather_fusion
  15.7 4.0 fusion
  19.7 5.0 %copy.54 = f32[1,16,2,136,128]{4,3,2,0,1:T(8,128)} copy(f32[1,16,2,136,128]{3,4,2,1,0:T(8,128)} %bitcast.80) | data formatting | bytes 4456448 | tf_op jit(solution)/shard_map/stack | solution.py:37
  24.7 1.9 concatenate.13
  26.6 0.3 copy-done
  27.0 2.4 pad_maximum_fusion
  29.4 10.2 %all-to-all-start = ((f32[2,16,2,136,128]{4,3,2,0,1:T(8,128)}), f32[2,16,2,136,128]{4,3,2,0,1:T(8,128)}, u32[]{:S(2)}, u32[]{:S(2)}) async-start(f32[2,16,2,136,128]{4,3,2,0,1:T(8,128)} %pad_maximum_fusion), calls=%async_computation | async-start | bytes 8912896 | tf_op jit(solution)/shard_map/all_to_all | solution.py:41
  39.7 102.2 %all-to-all-done = f32[2,16,2,136,128]{4,3,2,0,1:T(8,128)} async-done(((f32[2,16,2,136,128]{4,3,2,0,1:T(8,128)}), f32[2,16,2,136,128]{4,3,2,0,1:T(8,128)}, u32[]{:S(2)}, u32[]{:S(2)}) %all-to-all-start) | async-done | bytes 4456480 | tf_op jit(solution)/shard_map/all_to_all | solution.py:41
  141.9 2.6 fusion.33
  144.5 1.4 copy-done.7
  145.9 1.8 collective-permute-start.2
  147.7 1.4 collective-permute-start.1
  149.2 2.2 collective-permute-start
  151.5 3.0 collective-permute-done.1
  154.7 1.1 fusion.20
  155.8 0.9 pad_maximum_fusion.1
  156.7 1.7 slice_bitcast_fusion
  158.5 38.0 %all_to_all.25 = f32[2,16,128,128]{3,2,0,1:T(8,128)} all-to-all(f32[2,16,128,128]{3,2,0,1:T(8,128)S(1)} %slice_bitcast_fusion), channel_id=1, replica_groups=mesh['row'=16,'col'=16] {'row'}, dimensions={1} | all-to-all | bytes 4194304 | tf_op jit(solution)/shard_map/all_to_all | solution.py:43
  196.5 9.3 %all-to-all-start.2 = ((f32[2,16,128,128]{3,2,0,1:T(8,128)}), f32[2,16,128,128]{3,2,0,1:T(8,128)}, u32[]{:S(2)}, u32[]{:S(2)}) async-start(f32[2,16,128,128]{3,2,0,1:T(8,128)} %all_to_all.25), calls=%async_computation.2 | async-start | bytes 4194304 | tf_op jit(solution)/shard_map/all_to_all | solution.py:44
  205.8 60.3 %all-to-all-done.2 = f32[2,16,128,128]{3,2,0,1:T(8,128)} async-done(((f32[2,16,128,128]{3,2,0,1:T(8,128)}), f32[2,16,128,128]{3,2,0,1:T(8,128)}, u32[]{:S(2)}, u32[]{:S(2)}) %all-to-all-start.2) | async-done | bytes 2097184 | tf_op jit(solution)/shard_map/all_to_all | solution.py:44
  266.1 3.6 gather_fusion.1
  269.7 1.9 bitcast_add_fusion
  271.6 2.5 fusion.1
  274.1 5.0 %copy.57 = f32[32,136,128]{2,1,0:T(8,128)} copy(f32[32,136,128]{1,2,0:T(8,128)} %fusion.1) | data formatting | bytes 4456448 | tf_op jit(solution)/shard_map/concatenate | solution.py:56
  279.0 3.4 collective-permute-start.4
  282.6 58.2 %collective-permute-done.4 = f32[32,136,128]{2,1,0:T(8,128)} collective-permute-done((f32[32,136,128]{2,1,0:T(8,128)}, f32[32,136,128]{2,1,0:T(8,128)}, u32[]{:S(2)}, u32[]{:S(2)}) %collective-permute-start.4) | collective-permute-done | bytes 2228256 | tf_op jit(solution)/shard_map/ppermute | solution.py:13
  340.7 5.2 %all-gather.3.cloned.1.call-done = f32[64,2,136,128]{3,2,1,0:T(8,128)} async-done(((f32[4,2,136,128]{3,2,1,0:T(8,128)}), f32[64,2,136,128]{3,2,1,0:T(8,128)}) %all-gather.3.cloned.1.call-update) | async-done | bytes 8912912 | tf_op jit(solution)/shard_map/all_gather | solution.py:54
  345.9 6.6 %fusion.32 = (f32[1,16,2,136,128]{4,3,2,0,1:T(8,128)}, f32[1,16,2,136,128]{4,3,2,0,1:T(8,128)S(1)}, f32[1,16,2,136,128]{4,3,2,0,1:T(8,128)}, f32[1,16,2,136,128]{4,3,2,0,1:T(8,128)S(1)}) fusion(f32[4,16,2,136,128]{4,3,2,0,1:T(8,128)} %bitcast.81), kind=kLoop, calls=%fused_computation.76 | loop fusion | bytes 17825792 | tf_op jit(solution)/shard_map/slice | solution.py:65
  352.5 1.4 copy-done.2
  353.9 0.7 fusion.22
  354.6 0.7 fusion.24
  355.3 3.7 gather_fusion.2
  359.0 3.7 gather_fusion.4
  362.7 1.6 fusion.23
  364.3 3.7 gather_fusion.3
  368.0 1.6 fusion.21
  369.6 4.5 %fusion.11 = f32[32,128,128]{2,1,0:T(8,128)S(1)} fusion(f32[32,136,128]{2,1,0:T(8,128)} %gather_fusion.2, f32[32,136,128]{2,1,0:T(8,128)} %bitcast.88), kind=kOutput, calls=%fused_computation.21 | convolution fusion | flops 805306368 | bytes 6291456 | tf_op jit(solution)/shard_map/rik,rkj->rij/dot_general | solution.py:69
  374.1 3.5 fusion.5
  377.7 3.6 fusion.8
  381.3 5.1 %collective-permute-done.5 = f32[32,136,128]{2,1,0:T(8,128)} collective-permute-done((f32[32,136,128]{2,1,0:T(8,128)}, f32[32,136,128]{2,1,0:T(8,128)}, u32[]{:S(2)}, u32[]{:S(2)}) %collective-permute-start.5) | collective-permute-done | bytes 2228256 | tf_op jit(solution)/shard_map/ppermute | solution.py:13
  386.4 3.8 gather_fusion.5
  390.1 3.5 compare_reduce_fusion.3
  393.6 7.4 %add_bitcast_fusion = f32[32,1,128,128]{3,2,1,0:T(8,128)} fusion(f32[32,128,128]{2,1,0:T(8,128)} %fusion.5, f32[32,128,128]{2,1,0:T(8,128)} %fusion.8, f32[32,128,128]{2,1,0:T(8,128)S(1)} %fusion.11, f32[32,136,128]{2,1,0:T(8,128)} %gather_fusion.5, f32[32,136,128]{2,1,0:T(8,128)} %bitcast.90, pred[32]{0:T(512)(128)(4,1)S(1)} %get-tuple-element.18, ...), kind=kOutput, calls=%fused_computation.27 | convolution fusion | flops 808976384 | bytes 12583040 | tf_op jit(solution)/shard_map/rik,rkj->rij/dot_general | solution.py:69
  (37 shorter events, 0.8 us)
Async XLA Ops:
  24.7 2.3 copy-start
  29.4 112.5 %all-to-all-start = ((f32[2,16,2,136,128]{4,3,2,0,1:T(8,128)}), f32[2,16,2,136,128]{4,3,2,0,1:T(8,128)}, u32[]{:S(2)}, u32[]{:S(2)}) async-start(f32[2,16,2,136,128]{4,3,2,0,1:T(8,128)} %pad_maximum_fusion), calls=%async_computation | async-start | bytes 8912896 | tf_op jit(solution)/shard_map/all_to_all | solution.py:41
  39.6 306.3 %all-gather.3.cloned.1.call-start = ((), (), s32[]{:S(2)}) async-start(), calls=%async_computation.3 | async-start | bytes 9469952 | tf_op jit(solution)/shard_map/all_gather | solution.py:54
  144.5 1.4 copy-start.7
  145.9 5.6 %collective-permute-start.2 = (f32[2,136,128]{2,1,0:T(8,128)S(1)}, f32[2,136,128]{2,1,0:T(8,128)S(1)}, u32[]{:S(2)}, u32[]{:S(2)}) collective-permute-start(f32[2,136,128]{2,1,0:T(8,128)S(1)} %get-tuple-element.28), channel_id=1, source_target_pairs={{48,0},{64,16},{80,32},{96,48},{112,64},{128,80},{144,96},{160,112... | collective-permute-start | bytes 417800 | tf_op jit(solution)/shard_map/ppermute | solution.py:13
  147.7 6.7 %collective-permute-start.1 = (f32[2,136,128]{2,1,0:T(8,128)S(1)}, f32[2,136,128]{2,1,0:T(8,128)S(1)}, u32[]{:S(2)}, u32[]{:S(2)}) collective-permute-start(f32[2,136,128]{2,1,0:T(8,128)S(1)} %get-tuple-element.29), channel_id=1, source_target_pairs={{32,0},{48,16},{64,32},{80,48},{96,64},{112,80},{128,96},{144,112}... | collective-permute-start | bytes 417800 | tf_op jit(solution)/shard_map/ppermute | solution.py:13
  149.2 5.6 %collective-permute-start = (f32[2,136,128]{2,1,0:T(8,128)S(1)}, f32[2,136,128]{2,1,0:T(8,128)S(1)}, u32[]{:S(2)}, u32[]{:S(2)}) collective-permute-start(f32[2,136,128]{2,1,0:T(8,128)S(1)} %get-tuple-element.30), channel_id=1, source_target_pairs={{16,0},{32,16},{48,32},{64,48},{80,64},{96,80},{112,96},{128,112},... | collective-permute-start | bytes 417800 | tf_op jit(solution)/shard_map/ppermute | solution.py:13
  196.5 69.6 %all-to-all-start.2 = ((f32[2,16,128,128]{3,2,0,1:T(8,128)}), f32[2,16,128,128]{3,2,0,1:T(8,128)}, u32[]{:S(2)}, u32[]{:S(2)}) async-start(f32[2,16,128,128]{3,2,0,1:T(8,128)} %all_to_all.25), calls=%async_computation.2 | async-start | bytes 4194304 | tf_op jit(solution)/shard_map/all_to_all | solution.py:44
  274.1 8.4 %copy-start.8 = (s32[32,1]{0,1:T(1,128)S(1)}, s32[32,1]{0,1:T(1,128)}, u32[]{:S(2)}) copy-start(s32[32,1]{0,1:T(1,128)} %param.6) | copy-start | bytes 388
  279.0 61.7 %collective-permute-start.4 = (f32[32,136,128]{2,1,0:T(8,128)}, f32[32,136,128]{2,1,0:T(8,128)}, u32[]{:S(2)}, u32[]{:S(2)}) collective-permute-start(f32[32,136,128]{2,1,0:T(8,128)} %copy.57), channel_id=1, source_target_pairs={{32,0},{48,16},{64,32},{80,48},{96,64},{112,80},{128,96},{144,112}... | collective-permute-start | bytes 6684680 | tf_op jit(solution)/shard_map/ppermute | solution.py:13
  282.5 81.8 %collective-permute-start.3 = (f32[32,136,128]{2,1,0:T(8,128)}, f32[32,136,128]{2,1,0:T(8,128)}, u32[]{:S(2)}, u32[]{:S(2)}) collective-permute-start(f32[32,136,128]{2,1,0:T(8,128)} %copy.57), channel_id=1, source_target_pairs={{16,0},{32,16},{48,32},{64,48},{80,64},{96,80},{112,96},{128,112},... | collective-permute-start | bytes 6684680 | tf_op jit(solution)/shard_map/ppermute | solution.py:13
  340.7 45.6 %collective-permute-start.5 = (f32[32,136,128]{2,1,0:T(8,128)}, f32[32,136,128]{2,1,0:T(8,128)}, u32[]{:S(2)}, u32[]{:S(2)}) collective-permute-start(f32[32,136,128]{2,1,0:T(8,128)} %collective-permute-done.4), channel_id=1, source_target_pairs={{16,0},{32,16},{48,32},{64,48},{80,64},{96,80},{112,96},{128,112},... | collective-permute-start | bytes 6684680 | tf_op jit(solution)/shard_map/ppermute | solution.py:13
  352.5 1.4 copy-start.2
  352.5 2.1 copy-start.4
  369.6 4.5 %copy-start.3 = (f32[1,16,2,136,128]{4,3,2,0,1:T(8,128)S(1)}, f32[1,16,2,136,128]{4,3,2,0,1:T(8,128)}, u32[]{:S(2)}) copy-start(f32[1,16,2,136,128]{4,3,2,0,1:T(8,128)} %copy-done.2) | copy-start | bytes 6684676
  369.6 4.5 %copy-start.5 = (f32[32,136,128]{2,1,0:T(8,128)S(1)}, f32[32,136,128]{2,1,0:T(8,128)}, u32[]{:S(2)}) copy-start(f32[32,136,128]{2,1,0:T(8,128)} %gather_fusion.4) | copy-start | bytes 6684676
  374.1 3.6 copy-start.1
  374.1 3.5 copy-start.6
Sparse Core Ops, SparseCore 0:
  156.8 189.0 all-gather.2

commit v6 on v5

--- a/solution.py
+++ b/solution.py
@@ -55,9 +55,13 @@
     left_all = jnp.transpose(left_all, (1, 0, 2, 3, 4)).reshape(STEPS, local_rows, bs + EXTRA, bs)
     density = jnp.concatenate([density, tag], axis=1)
 
-    one = shifted(density, "row", 1)
     two = shifted(density, "row", 2)
-    three = shifted(two, "row", 1)
+    odd_three = lax.ppermute(density, "row", [((i + 3) % rows, i) for i in range(1, rows, 2)])
+    to_even = lax.ppermute(jnp.stack([density, two]), "row", [(i + 1, i) for i in range(0, rows, 2)])
+    to_odd = lax.ppermute(two, "row", [(i, i + 1) for i in range(0, rows, 2)])
+    even = row_index % 2 == 0
+    one = jnp.where(even, to_even[0], to_odd)
+    three = jnp.where(even, to_even[1], odd_three)
     rights = [density, one, two, three]
 
     total = jnp.zeros((local_rows, bs, bs), jnp.float32)

time: 414 us -> 466 us (1.13)
  other arithmetic: 23.6 us -> 37.4 us
  waiting for transfers between devices: 234 us -> 247 us
  local copies, waits for them, and re-layouts: 50.8 us -> 62.7 us
  starting transfers between devices: 28.3 us -> 39.9 us
    ppermute x0 -> x3, waiting for transfers between devices: none -> 21.1 us  [the longest x1 21.1 us: shards(): lax.ppermute(density, 'row', [((i + 3) % rows, i) for i in range(1, rows,...]
    ppermute x0 -> x3, starting transfers between devices: none -> 12.5 us  [the longest x1 8.57 us: shards(): lax.ppermute(density, 'row', [((i + 3) % rows, i) for i in range(1, rows,...]
    another operation x0 -> x2, other arithmetic: none -> 12.1 us  [shards(): jnp.stack([density, two])]
    another operation x0 -> x1, local copies, waits for them, and re-layouts: none -> 7.91 us  [shards(): jnp.stack([density, two])]
    all_gather x1, waiting for transfers between devices: 5.18 us -> 0.01 us  [shards(): left_all = lax.all_gather(mine, 'col', axis=0, tiled=False)]
    select_n x0 -> x1, other arithmetic: none -> 4.79 us  [shards(): one = jnp.where(even, to_even[0], to_odd)]
    ppermute x0 -> x1, local copies, waits for them, and re-layouts: none -> 4.73 us  [shifted(): return lax.ppermute(block, axis, route)]
    ppermute x6 -> x4, waiting for transfers between devices: 66.6 us -> 63.1 us  [shifted(): return lax.ppermute(block, axis, route)]
  transfers between devices with their start and end apart: 9 -> 10, of which waited for: 8 -> 5; matrix products, arithmetic and copies ran while one was open for 12% -> 9% of each run, Pallas kernels for 0% -> 0%
where the time goes in v6:
time: 466 us; the launch traced here: 460 us
  waiting for transfers between devices  247 us (53%)
  local copies, waits for them, and re-layouts  62.7 us (13%)
  starting transfers between devices  39.9 us (9%)
  other arithmetic  37.4 us (8%)
  blocking collectives  36.4 us (8%)
  matrix products  23.4 us (5%)
  between operations  13.7 us (3%)
    all_to_all x1, waiting for transfers between devices, shards(): spread = lax.all_to_all(pieces, 'col', 1, 1, tiled=True)  102 us
    ppermute x4, waiting for transfers between devices, shifted(): return lax.ppermute(block, axis, route)  63.1 us
    all_to_all x1, waiting for transfers between devices, shards(): lax.all_to_all(second, 'col', 1, 0, tiled=True).reshape(local_rows, bs, bs)  60.4 us
    all_to_all x1, blocking collectives, shards(): second = lax.all_to_all(first, 'row', 1, 1, tiled=True)  36.4 us
    dot_general x4, matrix products, shards(): jnp.einsum('rik,rkj->rij', left[:, :bs], right[:, :bs], precision=lax.Pre...  23.4 us
    ppermute x1, waiting for transfers between devices, shards(): lax.ppermute(density, 'row', [((i + 3) % rows, i) for i in range(1, rows,...  21.1 us
    gather x4, local copies, waits for them, and re-layouts, shards(): right = rights[step][inner]  14.8 us
    another operation x2, other arithmetic, shards(): jnp.stack([density, two])  12.1 us
  transfers between devices with their start and end apart: 10, of which 5 were waited for; matrix products, arithmetic and copies ran while one was open for 9% of the time, Pallas kernels for 0%

profile of v6, /device:TPU:2, one launch (start us, length us, event | category | flops | bytes accessed | tf_op | source)
XLA Modules:
  0.0 460.2 jit_solution(15039629156327415750)
XLA Ops:
  7.3 1.9 copy.54
  9.3 0.7 scatter_custom_fusion
  10.0 1.5 bitcast_multiply_fusion
  11.5 3.6 gather_fusion
  15.1 4.0 fusion
  19.1 5.0 %copy.56 = f32[1,16,2,136,128]{4,3,2,0,1:T(8,128)} copy(f32[1,16,2,136,128]{3,4,2,1,0:T(8,128)} %bitcast.90) | data formatting | bytes 4456448 | tf_op jit(solution)/shard_map/stack | solution.py:37
  24.1 1.9 concatenate.13
  26.4 2.4 pad_maximum_fusion.1
  28.8 10.2 %all-to-all-start = ((f32[2,16,2,136,128]{4,3,2,0,1:T(8,128)}), f32[2,16,2,136,128]{4,3,2,0,1:T(8,128)}, u32[]{:S(2)}, u32[]{:S(2)}) async-start(f32[2,16,2,136,128]{4,3,2,0,1:T(8,128)} %pad_maximum_fusion.1), calls=%async_computation | async-start | bytes 8912896 | tf_op jit(solution)/shard_map/all_to_all | solution.py:41
  39.1 102.2 %all-to-all-done = f32[2,16,2,136,128]{4,3,2,0,1:T(8,128)} async-done(((f32[2,16,2,136,128]{4,3,2,0,1:T(8,128)}), f32[2,16,2,136,128]{4,3,2,0,1:T(8,128)}, u32[]{:S(2)}, u32[]{:S(2)}) %all-to-all-start) | async-done | bytes 4456480 | tf_op jit(solution)/shard_map/all_to_all | solution.py:41
  141.3 2.6 fusion.36
  143.9 1.4 copy-done.3
  145.6 3.0 collective-permute-start.2
  148.5 1.4 collective-permute-start.1
  150.0 6.6 %collective-permute-done.2 = f32[2,136,128]{2,1,0:T(8,128)S(1)} collective-permute-done((f32[2,136,128]{2,1,0:T(8,128)S(1)}, f32[2,136,128]{2,1,0:T(8,128)S(1)}, u32[]{:S(2)}, u32[]{:S(2)}) %collective-permute-start.2) | collective-permute-done | bytes 139296 | tf_op jit(solution)/shard_map/ppermute | solution.py:13
  156.6 1.1 fusion.22
  157.7 0.8 pad_maximum_fusion.2
  158.5 1.7 slice_bitcast_fusion.2
  160.3 36.4 %all_to_all.25 = f32[2,16,128,128]{3,2,0,1:T(8,128)} all-to-all(f32[2,16,128,128]{3,2,0,1:T(8,128)S(1)} %slice_bitcast_fusion.2), channel_id=1, replica_groups=mesh['row'=16,'col'=16] {'row'}, dimensions={1} | all-to-all | bytes 4194304 | tf_op jit(solution)/shard_map/all_to_all | solution.py:43
  196.7 9.2 %all-to-all-start.2 = ((f32[2,16,128,128]{3,2,0,1:T(8,128)}), f32[2,16,128,128]{3,2,0,1:T(8,128)}, u32[]{:S(2)}, u32[]{:S(2)}) async-start(f32[2,16,128,128]{3,2,0,1:T(8,128)} %all_to_all.25), calls=%async_computation.2 | async-start | bytes 4194304 | tf_op jit(solution)/shard_map/all_to_all | solution.py:44
  205.9 60.4 %all-to-all-done.2 = f32[2,16,128,128]{3,2,0,1:T(8,128)} async-done(((f32[2,16,128,128]{3,2,0,1:T(8,128)}), f32[2,16,128,128]{3,2,0,1:T(8,128)}, u32[]{:S(2)}, u32[]{:S(2)}) %all-to-all-start.2) | async-done | bytes 2097184 | tf_op jit(solution)/shard_map/all_to_all | solution.py:44
  266.3 3.6 gather_fusion.1
  269.9 1.9 bitcast_add_fusion
  271.8 4.2 fusion.34
  276.0 5.0 %copy.59 = f32[32,136,128]{2,1,0:T(8,128)} copy(f32[32,136,128]{1,2,0:T(8,128)} %get-tuple-element.37) | data formatting | bytes 4456448 | tf_op jit(solution)/shard_map/concatenate | solution.py:56
  281.0 3.4 collective-permute-start.3
  284.4 56.5 %collective-permute-done.3 = f32[32,136,128]{2,1,0:T(8,128)} collective-permute-done((f32[32,136,128]{2,1,0:T(8,128)}, f32[32,136,128]{2,1,0:T(8,128)}, u32[]{:S(2)}, u32[]{:S(2)}) %collective-permute-start.3) | collective-permute-done | bytes 2228256 | tf_op jit(solution)/shard_map/ppermute | solution.py:13
  340.8 4.7 %copy.62 = f32[32,136,128]{1,2,0:T(8,128)} copy(f32[32,136,128]{2,1,0:T(8,128)} %collective-permute-done.3) | data formatting | bytes 4456448 | tf_op jit(solution)/shard_map/ppermute | solution.py:13
  345.6 7.9 %pad_maximum_fusion = f32[2,32,136,128]{2,3,1,0:T(8,128)} fusion(f32[1,32,136,128]{2,3,1,0:T(8,128)} %bitcast.91, f32[1,32,136,128]{2,3,1,0:T(8,128)} %get-tuple-element.36), kind=kLoop, calls=%fused_computation.7 | loop fusion | flops 1114112 | bytes 8912896 | tf_op jit(solution)/shard_map/stack | solution.py:60
  353.4 7.9 %copy.63 = f32[2,32,136,128]{3,2,1,0:T(8,128)} copy(f32[2,32,136,128]{2,3,1,0:T(8,128)} %pad_maximum_fusion) | data formatting | bytes 8912896 | tf_op jit(solution)/shard_map/stack | solution.py:60
  361.4 1.3 collective-permute-start.4
  362.6 8.6 %collective-permute-start.6 = (f32[32,136,128]{2,1,0:T(8,128)}, f32[32,136,128]{2,1,0:T(8,128)}, u32[]{:S(2)}, u32[]{:S(2)}) collective-permute-start(f32[32,136,128]{2,1,0:T(8,128)} %copy.59), channel_id=1, source_target_pairs={{64,16},{96,48},{128,80},{160,112},{192,144},{224,176},{0,208},{32... | collective-permute-start | bytes 6684680 | tf_op jit(solution)/shard_map/ppermute | solution.py:59
  371.2 2.7 collective-permute-start.5
  374.0 21.1 %collective-permute-done.6 = f32[32,136,128]{2,1,0:T(8,128)} collective-permute-done((f32[32,136,128]{2,1,0:T(8,128)}, f32[32,136,128]{2,1,0:T(8,128)}, u32[]{:S(2)}, u32[]{:S(2)}) %collective-permute-start.6) | collective-permute-done | bytes 2228256 | tf_op jit(solution)/shard_map/ppermute | solution.py:59
  395.0 4.8 %fusion.3 = (f32[32,136,128]{2,1,0:T(8,128)}, f32[32,136,128]{2,1,0:T(8,128)}) fusion(f32[32,136,128]{2,1,0:T(8,128)} %collective-permute-done.5, f32[2,32,136,128]{3,2,1,0:T(8,128)} %collective-permute-done.4, pred[]{:T(512)S(6)} %eq.30, f32[32,136,128]{2,1,0:T(8,128)} %collective-permute-done.6), kind=kLoop, calls=%fused_computation.16 | loop fusion | flops 1114112 | bytes 13369345 | tf_op jit(solution)/shard_map/jit(_where)/select_n | solution.py:63
  399.8 6.6 %fusion.35 = (f32[1,16,2,136,128]{4,3,2,0,1:T(8,128)S(1)}, f32[1,16,2,136,128]{4,3,2,0,1:T(8,128)S(1)}, f32[1,16,2,136,128]{4,3,2,0,1:T(8,128)}, f32[1,16,2,136,128]{4,3,2,0,1:T(8,128)}) fusion(f32[4,16,2,136,128]{4,3,2,0,1:T(8,128)} %bitcast.92), kind=kLoop, calls=%fused_computation.82 | loop fusion | bytes 17825792 | tf_op jit(solution)/shard_map/slice | solution.py:69
  407.1 0.8 copy-done.1
  408.5 3.7 gather_fusion.5
  412.2 4.4 fusion.4
  416.6 1.6 fusion.24
  418.2 3.7 gather_fusion.4
  421.9 5.7 %fusion.7 = f32[32,128,128]{2,1,0:T(8,128)} fusion(f32[32,136,128]{2,1,0:T(8,128)} %gather_fusion.4, f32[32,136,128]{2,1,0:T(8,128)} %bitcast.97), kind=kOutput, calls=%fused_computation.20 | convolution fusion | flops 805306368 | bytes 6291456 | tf_op jit(solution)/shard_map/rik,rkj->rij/dot_general | solution.py:73
  427.6 1.6 fusion.26
  429.2 3.7 gather_fusion.2
  432.9 5.7 %fusion.13 = f32[32,128,128]{2,1,0:T(8,128)} fusion(f32[32,136,128]{2,1,0:T(8,128)} %gather_fusion.2, f32[32,136,128]{2,1,0:T(8,128)} %bitcast.95), kind=kOutput, calls=%fused_computation.26 | convolution fusion | flops 805306368 | bytes 6291456 | tf_op jit(solution)/shard_map/rik,rkj->rij/dot_general | solution.py:73
  438.6 3.7 gather_fusion.3
  442.3 3.5 compare_reduce_fusion.3
  445.8 7.6 %add_bitcast_fusion = f32[32,1,128,128]{3,2,1,0:T(8,128)} fusion(f32[32,128,128]{2,1,0:T(8,128)S(1)} %fusion.4, f32[32,128,128]{2,1,0:T(8,128)} %fusion.7, f32[32,128,128]{2,1,0:T(8,128)} %fusion.13, f32[32,136,128]{2,1,0:T(8,128)} %gather_fusion.3, f32[32,136,128]{2,1,0:T(8,128)} %bitcast.101, pred[32]{0:T(512)(128)(4,1)S(1)} %get-tuple-element.18, ...), kind=kOutput, calls=%fused_computation.32 | convolution fusion | flops 808976384 | bytes 12583040 | tf_op jit(solution)/shard_map/rik,rkj->rij/dot_general | solution.py:73
  (36 shorter events, 2.9 us)
Async XLA Ops:
  6.5 2.7 copy-start.5
  24.1 2.3 copy-start
  28.8 112.5 %all-to-all-start = ((f32[2,16,2,136,128]{4,3,2,0,1:T(8,128)}), f32[2,16,2,136,128]{4,3,2,0,1:T(8,128)}, u32[]{:S(2)}, u32[]{:S(2)}) async-start(f32[2,16,2,136,128]{4,3,2,0,1:T(8,128)} %pad_maximum_fusion.1), calls=%async_computation | async-start | bytes 8912896 | tf_op jit(solution)/shard_map/all_to_all | solution.py:41
  39.0 360.8 %all-gather.3.cloned.1.call-start = ((), (), s32[]{:S(2)}) async-start(), calls=%async_computation.3 | async-start | bytes 9469952 | tf_op jit(solution)/shard_map/all_gather | solution.py:54
  143.9 1.4 copy-start.3
  145.3 4.6 %collective-permute-start = (f32[2,136,128]{2,1,0:T(8,128)S(1)}, f32[2,136,128]{2,1,0:T(8,128)S(1)}, u32[]{:S(2)}, u32[]{:S(2)}) collective-permute-start(f32[2,136,128]{2,1,0:T(8,128)S(1)} %get-tuple-element.32), channel_id=1, source_target_pairs={{16,0},{32,16},{48,32},{64,48},{80,64},{96,80},{112,96},{128,112},... | collective-permute-start | bytes 417800 | tf_op jit(solution)/shard_map/ppermute | solution.py:13
  145.6 11.0 %collective-permute-start.2 = (f32[2,136,128]{2,1,0:T(8,128)S(1)}, f32[2,136,128]{2,1,0:T(8,128)S(1)}, u32[]{:S(2)}, u32[]{:S(2)}) collective-permute-start(f32[2,136,128]{2,1,0:T(8,128)S(1)} %get-tuple-element.30), channel_id=1, source_target_pairs={{48,0},{64,16},{80,32},{96,48},{112,64},{128,80},{144,96},{160,112... | collective-permute-start | bytes 417800 | tf_op jit(solution)/shard_map/ppermute | solution.py:13
  148.5 8.0 %collective-permute-start.1 = (f32[2,136,128]{2,1,0:T(8,128)S(1)}, f32[2,136,128]{2,1,0:T(8,128)S(1)}, u32[]{:S(2)}, u32[]{:S(2)}) collective-permute-start(f32[2,136,128]{2,1,0:T(8,128)S(1)} %get-tuple-element.31), channel_id=1, source_target_pairs={{32,0},{48,16},{64,32},{80,48},{96,64},{112,80},{128,96},{144,112}... | collective-permute-start | bytes 417800 | tf_op jit(solution)/shard_map/ppermute | solution.py:13
  196.7 69.7 %all-to-all-start.2 = ((f32[2,16,128,128]{3,2,0,1:T(8,128)}), f32[2,16,128,128]{3,2,0,1:T(8,128)}, u32[]{:S(2)}, u32[]{:S(2)}) async-start(f32[2,16,128,128]{3,2,0,1:T(8,128)} %all_to_all.25), calls=%async_computation.2 | async-start | bytes 4194304 | tf_op jit(solution)/shard_map/all_to_all | solution.py:44
  281.0 59.8 %collective-permute-start.3 = (f32[32,136,128]{2,1,0:T(8,128)}, f32[32,136,128]{2,1,0:T(8,128)}, u32[]{:S(2)}, u32[]{:S(2)}) collective-permute-start(f32[32,136,128]{2,1,0:T(8,128)} %copy.59), channel_id=1, source_target_pairs={{32,0},{48,16},{64,32},{80,48},{96,64},{112,80},{128,96},{144,112}... | collective-permute-start | bytes 6684680 | tf_op jit(solution)/shard_map/ppermute | solution.py:13
  353.4 20.4 %copy-start.4 = (s32[32,1]{0,1:T(1,128)S(1)}, s32[32,1]{0,1:T(1,128)}, u32[]{:S(2)}) copy-start(s32[32,1]{0,1:T(1,128)} %param.6) | copy-start | bytes 388
  361.4 33.7 %collective-permute-start.4 = (f32[2,32,136,128]{3,2,1,0:T(8,128)}, f32[2,32,136,128]{3,2,1,0:T(8,128)}, u32[]{:S(2)}, u32[]{:S(2)}) collective-permute-start(f32[2,32,136,128]{3,2,1,0:T(8,128)} %copy.63), channel_id=1, source_target_pairs={{16,0},{48,32},{80,64},{112,96},{144,128},{176,160},{208,192},{240... | collective-permute-start | bytes 13369352 | tf_op jit(solution)/shard_map/ppermute | solution.py:60
  362.6 32.4 %collective-permute-start.6 = (f32[32,136,128]{2,1,0:T(8,128)}, f32[32,136,128]{2,1,0:T(8,128)}, u32[]{:S(2)}, u32[]{:S(2)}) collective-permute-start(f32[32,136,128]{2,1,0:T(8,128)} %copy.59), channel_id=1, source_target_pairs={{64,16},{96,48},{128,80},{160,112},{192,144},{224,176},{0,208},{32... | collective-permute-start | bytes 6684680 | tf_op jit(solution)/shard_map/ppermute | solution.py:59
  371.2 23.8 %collective-permute-start.5 = (f32[32,136,128]{2,1,0:T(8,128)}, f32[32,136,128]{2,1,0:T(8,128)}, u32[]{:S(2)}, u32[]{:S(2)}) collective-permute-start(f32[32,136,128]{2,1,0:T(8,128)} %collective-permute-done.3), channel_id=1, source_target_pairs={{0,16},{32,48},{64,80},{96,112},{128,144},{160,176},{192,208},{224... | collective-permute-start | bytes 6684680 | tf_op jit(solution)/shard_map/ppermute | solution.py:61
  406.4 1.4 copy-start.1
  406.4 2.1 copy-start.2
Sparse Core Ops, SparseCore 0:
  158.7 185.5 all-gather.2

commit v7 on v5

--- a/solution.py
+++ b/solution.py
@@ -57,7 +57,7 @@
 
     one = shifted(density, "row", 1)
     two = shifted(density, "row", 2)
-    three = shifted(two, "row", 1)
+    three = shifted(density, "row", 3)
     rights = [density, one, two, three]
 
     total = jnp.zeros((local_rows, bs, bs), jnp.float32)

time: 414 us -> 431 us (1.041)
  waiting for transfers between devices: 234 us -> 251 us
    all_gather x1, waiting for transfers between devices: 5.18 us -> 63 us  [shards(): left_all = lax.all_gather(mine, 'col', axis=0, tiled=False)]
    ppermute x6, waiting for transfers between devices: 66.6 us -> 25.3 us  [shifted(): return lax.ppermute(block, axis, route)]
  transfers between devices with their start and end apart: 9 -> 9, of which waited for: 8 -> 7; matrix products, arithmetic and copies ran while one was open for 12% -> 11% of each run, Pallas kernels for 0% -> 0%
where the time goes in v7:
time: 431 us; the launch traced here: 425 us
  waiting for transfers between devices  251 us (58%)
  local copies, waits for them, and re-layouts  50.9 us (12%)
  blocking collectives  38 us (9%)
  starting transfers between devices  28.7 us (7%)
  other arithmetic  23.6 us (5%)
  matrix products  19 us (4%)
  between operations  13.7 us (3%)
    all_to_all x1, waiting for transfers between devices, shards(): spread = lax.all_to_all(pieces, 'col', 1, 1, tiled=True)  102 us
    all_gather x1, waiting for transfers between devices, shards(): left_all = lax.all_gather(mine, 'col', axis=0, tiled=False)  63 us
    all_to_all x1, waiting for transfers between devices, shards(): lax.all_to_all(second, 'col', 1, 0, tiled=True).reshape(local_rows, bs, bs)  60.3 us
    all_to_all x1, blocking collectives, shards(): second = lax.all_to_all(first, 'row', 1, 1, tiled=True)  38 us
    ppermute x6, waiting for transfers between devices, shifted(): return lax.ppermute(block, axis, route)  25.3 us
    dot_general x4, matrix products, shards(): jnp.einsum('rik,rkj->rij', left[:, :bs], right[:, :bs], precision=lax.Pre...  19 us
    gather x4, local copies, waits for them, and re-layouts, shards(): right = rights[step][inner]  15 us
    all_to_all x1, starting transfers between devices, shards(): spread = lax.all_to_all(pieces, 'col', 1, 1, tiled=True)  10.2 us
  transfers between devices with their start and end apart: 9, of which 7 were waited for; matrix products, arithmetic and copies ran while one was open for 11% of the time, Pallas kernels for 0%

profile of v7, /device:TPU:2, one launch (start us, length us, event | category | flops | bytes accessed | tf_op | source)
XLA Modules:
  0.0 424.8 jit_solution(17260330368071650185)
XLA Ops:
  6.5 0.7 convert_bitcast_fusion
  7.2 0.7 fusion.25
  7.9 0.7 scatter_custom_fusion
  8.6 1.9 copy.53
  10.6 1.5 bitcast_multiply_fusion
  12.1 3.6 gather_fusion
  15.7 4.0 fusion
  19.8 5.0 %copy.55 = f32[1,16,2,136,128]{4,3,2,0,1:T(8,128)} copy(f32[1,16,2,136,128]{3,4,2,1,0:T(8,128)} %bitcast.80) | data formatting | bytes 4456448 | tf_op jit(solution)/shard_map/stack | solution.py:37
  24.7 1.9 concatenate.13
  26.6 0.3 copy-done
  27.0 2.4 pad_maximum_fusion
  29.4 10.2 %all-to-all-start = ((f32[2,16,2,136,128]{4,3,2,0,1:T(8,128)}), f32[2,16,2,136,128]{4,3,2,0,1:T(8,128)}, u32[]{:S(2)}, u32[]{:S(2)}) async-start(f32[2,16,2,136,128]{4,3,2,0,1:T(8,128)} %pad_maximum_fusion), calls=%async_computation | async-start | bytes 8912896 | tf_op jit(solution)/shard_map/all_to_all | solution.py:41
  39.7 102.2 %all-to-all-done = f32[2,16,2,136,128]{4,3,2,0,1:T(8,128)} async-done(((f32[2,16,2,136,128]{4,3,2,0,1:T(8,128)}), f32[2,16,2,136,128]{4,3,2,0,1:T(8,128)}, u32[]{:S(2)}, u32[]{:S(2)}) %all-to-all-start) | async-done | bytes 4456480 | tf_op jit(solution)/shard_map/all_to_all | solution.py:41
  141.9 2.6 fusion.33
  144.5 1.4 copy-done.7
  146.0 1.8 collective-permute-start.2
  147.8 1.4 collective-permute-start.1
  149.2 2.2 collective-permute-start
  151.5 3.0 collective-permute-done.1
  154.8 1.1 fusion.20
  155.9 0.9 pad_maximum_fusion.1
  156.7 1.7 slice_bitcast_fusion
  158.5 38.0 %all_to_all.25 = f32[2,16,128,128]{3,2,0,1:T(8,128)} all-to-all(f32[2,16,128,128]{3,2,0,1:T(8,128)S(1)} %slice_bitcast_fusion), channel_id=1, replica_groups=mesh['row'=16,'col'=16] {'row'}, dimensions={1} | all-to-all | bytes 4194304 | tf_op jit(solution)/shard_map/all_to_all | solution.py:43
  196.5 9.3 %all-to-all-start.2 = ((f32[2,16,128,128]{3,2,0,1:T(8,128)}), f32[2,16,128,128]{3,2,0,1:T(8,128)}, u32[]{:S(2)}, u32[]{:S(2)}) async-start(f32[2,16,128,128]{3,2,0,1:T(8,128)} %all_to_all.25), calls=%async_computation.2 | async-start | bytes 4194304 | tf_op jit(solution)/shard_map/all_to_all | solution.py:44
  205.8 60.3 %all-to-all-done.2 = f32[2,16,128,128]{3,2,0,1:T(8,128)} async-done(((f32[2,16,128,128]{3,2,0,1:T(8,128)}), f32[2,16,128,128]{3,2,0,1:T(8,128)}, u32[]{:S(2)}, u32[]{:S(2)}) %all-to-all-start.2) | async-done | bytes 2097184 | tf_op jit(solution)/shard_map/all_to_all | solution.py:44
  266.1 3.6 gather_fusion.1
  269.7 1.9 bitcast_add_fusion
  271.6 2.5 fusion.1
  274.1 5.0 %copy.58 = f32[32,136,128]{2,1,0:T(8,128)} copy(f32[32,136,128]{1,2,0:T(8,128)} %fusion.1) | data formatting | bytes 4456448 | tf_op jit(solution)/shard_map/concatenate | solution.py:56
  279.0 3.4 collective-permute-start.4
  282.6 0.4 collective-permute-start.5
  282.9 63.0 %all-gather.3.cloned.1.call-done = f32[64,2,136,128]{3,2,1,0:T(8,128)} async-done(((f32[4,2,136,128]{3,2,1,0:T(8,128)}), f32[64,2,136,128]{3,2,1,0:T(8,128)}) %all-gather.3.cloned.1.call-update) | async-done | bytes 8912912 | tf_op jit(solution)/shard_map/all_gather | solution.py:54
  346.0 6.6 %fusion.32 = (f32[1,16,2,136,128]{4,3,2,0,1:T(8,128)}, f32[1,16,2,136,128]{4,3,2,0,1:T(8,128)S(1)}, f32[1,16,2,136,128]{4,3,2,0,1:T(8,128)}, f32[1,16,2,136,128]{4,3,2,0,1:T(8,128)S(1)}) fusion(f32[4,16,2,136,128]{4,3,2,0,1:T(8,128)} %bitcast.81), kind=kLoop, calls=%fused_computation.76 | loop fusion | bytes 17825792 | tf_op jit(solution)/shard_map/slice | solution.py:65
  352.6 1.3 copy-done.2
  353.9 0.7 fusion.22
  354.6 0.7 fusion.24
  355.3 3.7 gather_fusion.2
  359.1 3.8 gather_fusion.4
  362.8 1.6 fusion.23
  364.4 22.0 %collective-permute-done.3 = f32[32,136,128]{2,1,0:T(8,128)} collective-permute-done((f32[32,136,128]{2,1,0:T(8,128)}, f32[32,136,128]{2,1,0:T(8,128)}, u32[]{:S(2)}, u32[]{:S(2)}) %collective-permute-start.3) | collective-permute-done | bytes 2228256 | tf_op jit(solution)/shard_map/ppermute | solution.py:13
  386.4 3.8 gather_fusion.3
  390.2 1.6 fusion.21
  391.8 4.5 %fusion.11 = f32[32,128,128]{2,1,0:T(8,128)S(1)} fusion(f32[32,136,128]{2,1,0:T(8,128)} %gather_fusion.2, f32[32,136,128]{2,1,0:T(8,128)} %bitcast.88), kind=kOutput, calls=%fused_computation.21 | convolution fusion | flops 805306368 | bytes 6291456 | tf_op jit(solution)/shard_map/rik,rkj->rij/dot_general | solution.py:69
  396.3 3.5 fusion.5
  399.9 3.5 fusion.8
  403.4 3.7 gather_fusion.5
  407.1 3.5 compare_reduce_fusion.3
  410.6 7.4 %add_bitcast_fusion = f32[32,1,128,128]{3,2,1,0:T(8,128)} fusion(f32[32,128,128]{2,1,0:T(8,128)} %fusion.5, f32[32,128,128]{2,1,0:T(8,128)} %fusion.8, f32[32,128,128]{2,1,0:T(8,128)S(1)} %fusion.11, f32[32,136,128]{2,1,0:T(8,128)} %gather_fusion.5, f32[32,136,128]{2,1,0:T(8,128)} %bitcast.90, pred[32]{0:T(512)(128)(4,1)S(1)} %get-tuple-element.18, ...), kind=kOutput, calls=%fused_computation.27 | convolution fusion | flops 808976384 | bytes 12583040 | tf_op jit(solution)/shard_map/rik,rkj->rij/dot_general | solution.py:69
  (37 shorter events, 0.8 us)
Async XLA Ops:
  24.7 2.3 copy-start
  29.4 112.5 %all-to-all-start = ((f32[2,16,2,136,128]{4,3,2,0,1:T(8,128)}), f32[2,16,2,136,128]{4,3,2,0,1:T(8,128)}, u32[]{:S(2)}, u32[]{:S(2)}) async-start(f32[2,16,2,136,128]{4,3,2,0,1:T(8,128)} %pad_maximum_fusion), calls=%async_computation | async-start | bytes 8912896 | tf_op jit(solution)/shard_map/all_to_all | solution.py:41
  39.6 306.4 %all-gather.3.cloned.1.call-start = ((), (), s32[]{:S(2)}) async-start(), calls=%async_computation.3 | async-start | bytes 9469952 | tf_op jit(solution)/shard_map/all_gather | solution.py:54
  144.5 1.4 copy-start.7
  146.0 5.6 %collective-permute-start.2 = (f32[2,136,128]{2,1,0:T(8,128)S(1)}, f32[2,136,128]{2,1,0:T(8,128)S(1)}, u32[]{:S(2)}, u32[]{:S(2)}) collective-permute-start(f32[2,136,128]{2,1,0:T(8,128)S(1)} %get-tuple-element.28), channel_id=1, source_target_pairs={{48,0},{64,16},{80,32},{96,48},{112,64},{128,80},{144,96},{160,112... | collective-permute-start | bytes 417800 | tf_op jit(solution)/shard_map/ppermute | solution.py:13
  147.8 6.7 %collective-permute-start.1 = (f32[2,136,128]{2,1,0:T(8,128)S(1)}, f32[2,136,128]{2,1,0:T(8,128)S(1)}, u32[]{:S(2)}, u32[]{:S(2)}) collective-permute-start(f32[2,136,128]{2,1,0:T(8,128)S(1)} %get-tuple-element.29), channel_id=1, source_target_pairs={{32,0},{48,16},{64,32},{80,48},{96,64},{112,80},{128,96},{144,112}... | collective-permute-start | bytes 417800 | tf_op jit(solution)/shard_map/ppermute | solution.py:13
  149.2 5.6 %collective-permute-start = (f32[2,136,128]{2,1,0:T(8,128)S(1)}, f32[2,136,128]{2,1,0:T(8,128)S(1)}, u32[]{:S(2)}, u32[]{:S(2)}) collective-permute-start(f32[2,136,128]{2,1,0:T(8,128)S(1)} %get-tuple-element.30), channel_id=1, source_target_pairs={{16,0},{32,16},{48,32},{64,48},{80,64},{96,80},{112,96},{128,112},... | collective-permute-start | bytes 417800 | tf_op jit(solution)/shard_map/ppermute | solution.py:13
  196.5 69.6 %all-to-all-start.2 = ((f32[2,16,128,128]{3,2,0,1:T(8,128)}), f32[2,16,128,128]{3,2,0,1:T(8,128)}, u32[]{:S(2)}, u32[]{:S(2)}) async-start(f32[2,16,128,128]{3,2,0,1:T(8,128)} %all_to_all.25), calls=%async_computation.2 | async-start | bytes 4194304 | tf_op jit(solution)/shard_map/all_to_all | solution.py:44
  274.1 8.4 %copy-start.8 = (s32[32,1]{0,1:T(1,128)S(1)}, s32[32,1]{0,1:T(1,128)}, u32[]{:S(2)}) copy-start(s32[32,1]{0,1:T(1,128)} %param.6) | copy-start | bytes 388
  279.0 80.0 %collective-permute-start.4 = (f32[32,136,128]{2,1,0:T(8,128)}, f32[32,136,128]{2,1,0:T(8,128)}, u32[]{:S(2)}, u32[]{:S(2)}) collective-permute-start(f32[32,136,128]{2,1,0:T(8,128)} %copy.58), channel_id=1, source_target_pairs={{32,0},{48,16},{64,32},{80,48},{96,64},{112,80},{128,96},{144,112}... | collective-permute-start | bytes 6684680 | tf_op jit(solution)/shard_map/ppermute | solution.py:13
  282.5 103.9 %collective-permute-start.3 = (f32[32,136,128]{2,1,0:T(8,128)}, f32[32,136,128]{2,1,0:T(8,128)}, u32[]{:S(2)}, u32[]{:S(2)}) collective-permute-start(f32[32,136,128]{2,1,0:T(8,128)} %copy.58), channel_id=1, source_target_pairs={{16,0},{32,16},{48,32},{64,48},{80,64},{96,80},{112,96},{128,112},... | collective-permute-start | bytes 6684680 | tf_op jit(solution)/shard_map/ppermute | solution.py:13
  282.6 120.8 %collective-permute-start.5 = (f32[32,136,128]{2,1,0:T(8,128)}, f32[32,136,128]{2,1,0:T(8,128)}, u32[]{:S(2)}, u32[]{:S(2)}) collective-permute-start(f32[32,136,128]{2,1,0:T(8,128)} %copy.58), channel_id=1, source_target_pairs={{48,0},{64,16},{80,32},{96,48},{112,64},{128,80},{144,96},{160,112... | collective-permute-start | bytes 6684680 | tf_op jit(solution)/shard_map/ppermute | solution.py:13
  352.6 1.3 copy-start.2
  352.6 2.1 copy-start.4
  391.8 4.5 %copy-start.3 = (f32[1,16,2,136,128]{4,3,2,0,1:T(8,128)S(1)}, f32[1,16,2,136,128]{4,3,2,0,1:T(8,128)}, u32[]{:S(2)}) copy-start(f32[1,16,2,136,128]{4,3,2,0,1:T(8,128)} %copy-done.2) | copy-start | bytes 6684676
  391.8 4.5 %copy-start.5 = (f32[32,136,128]{2,1,0:T(8,128)S(1)}, f32[32,136,128]{2,1,0:T(8,128)}, u32[]{:S(2)}) copy-start(f32[32,136,128]{2,1,0:T(8,128)} %gather_fusion.4) | copy-start | bytes 6684676
  396.3 3.6 copy-start.1
  396.3 3.5 copy-start.6
Sparse Core Ops, SparseCore 0:
  156.9 189.0 all-gather.2

commit v8 on v5

--- a/solution.py
+++ b/solution.py
@@ -32,7 +32,7 @@
     inverse = jnp.zeros((local_rows,), jnp.int32).at[block_cols[:, 0]].set(
         jnp.arange(local_rows, dtype=jnp.int32)
     )
-    mirror_out = jnp.swapaxes(held[inverse], 1, 2)
+    mirror_out = held[inverse]
     chunk = local_rows // cols
     pieces = jnp.stack([
         jnp.concatenate([held, tag], axis=1),
@@ -47,6 +47,7 @@
     for step in range(STEPS):
         own = lax.dynamic_index_in_dim(spread[0], (row_index + step) % cols, 0, keepdims=False)
         far = lax.dynamic_index_in_dim(spread[1], (row_index - step) % cols, 0, keepdims=False)
+        far = jnp.concatenate([jnp.swapaxes(far[:, :bs], 1, 2), far[:, bs:]], axis=1)
         if step:
             far = shifted(far, "row", step)
         mine.append(own + far)

time: 414 us -> 424 us (1.024)
  local copies, waits for them, and re-layouts: 50.8 us -> 58.2 us
    another operation x1 -> x2, local copies, waits for them, and re-layouts: 4.99 us -> 10 us  [shards(): jnp.stack([jnp.concatenate([held, tag], axis=1), jnp.concatenate([mirror_...]
  transfers between devices with their start and end apart: 9 -> 9, of which waited for: 8 -> 7; matrix products, arithmetic and copies ran while one was open for 12% -> 12% of each run, Pallas kernels for 0% -> 0%
where the time goes in v8:
time: 424 us; the launch traced here: 418 us
  waiting for transfers between devices  235 us (55%)
  local copies, waits for them, and re-layouts  58.2 us (14%)
  blocking collectives  37 us (9%)
  starting transfers between devices  28.2 us (7%)
  other arithmetic  26.8 us (6%)
  matrix products  19 us (4%)
  between operations  13.8 us (3%)
    all_to_all x1, waiting for transfers between devices, shards(): spread = lax.all_to_all(pieces, 'col', 1, 1, tiled=True)  102 us
    ppermute x6, waiting for transfers between devices, shifted(): return lax.ppermute(block, axis, route)  66.7 us
    all_to_all x1, waiting for transfers between devices, shards(): lax.all_to_all(second, 'col', 1, 0, tiled=True).reshape(local_rows, bs, bs)  60.4 us
    all_to_all x1, blocking collectives, shards(): second = lax.all_to_all(first, 'row', 1, 1, tiled=True)  37 us
    dot_general x4, matrix products, shards(): jnp.einsum('rik,rkj->rij', left[:, :bs], right[:, :bs], precision=lax.Pre...  19 us
    gather x4, local copies, waits for them, and re-layouts, shards(): right = rights[step][inner]  14.8 us
    all_to_all x1, starting transfers between devices, shards(): spread = lax.all_to_all(pieces, 'col', 1, 1, tiled=True)  10.2 us
    another operation x2, local copies, waits for them, and re-layouts, shards(): jnp.stack([jnp.concatenate([held, tag], axis=1), jnp.concatenate([mirror_...  10 us
  transfers between devices with their start and end apart: 9, of which 7 were waited for; matrix products, arithmetic and copies ran while one was open for 12% of the time, Pallas kernels for 0%

profile of v8, /device:TPU:2, one launch (start us, length us, event | category | flops | bytes accessed | tf_op | source)
XLA Modules:
  0.0 417.6 jit_solution(14265594652415776466)
XLA Ops:
  7.2 0.7 fusion.25
  7.9 0.7 scatter_custom_fusion
  8.6 1.9 copy.63
  10.6 1.5 bitcast_multiply_fusion
  12.1 3.6 gather_fusion
  15.7 4.0 fusion
  19.8 5.0 %copy.65 = f32[1,16,2,136,128]{4,3,2,0,1:T(8,128)} copy(f32[1,16,2,136,128]{3,4,2,1,0:T(8,128)} %bitcast.107) | data formatting | bytes 4456448 | tf_op jit(solution)/shard_map/stack | solution.py:37
  24.8 4.0 concatenate.36
  28.8 5.0 %copy.66 = f32[1,16,2,136,128]{4,3,2,0,1:T(8,128)} copy(f32[1,16,2,136,128]{3,4,2,1,0:T(8,128)} %bitcast.106) | data formatting | bytes 4456448 | tf_op jit(solution)/shard_map/stack | solution.py:37
  33.9 4.7 %pad_maximum_fusion = f32[2,16,2,136,128]{4,3,2,0,1:T(8,128)} fusion(f32[1,16,2,136,128]{4,3,2,0,1:T(8,128)} %copy.66, f32[1,16,2,136,128]{4,3,2,0,1:T(8,128)} %copy.65), kind=kLoop, calls=%fused_computation.7 | loop fusion | flops 1114112 | bytes 8912896 | tf_op jit(solution)/shard_map/stack | solution.py:37
  38.6 10.2 %all-to-all-start = ((f32[2,16,2,136,128]{4,3,2,0,1:T(8,128)}), f32[2,16,2,136,128]{4,3,2,0,1:T(8,128)}, u32[]{:S(2)}, u32[]{:S(2)}) async-start(f32[2,16,2,136,128]{4,3,2,0,1:T(8,128)} %pad_maximum_fusion), calls=%async_computation | async-start | bytes 8912896 | tf_op jit(solution)/shard_map/all_to_all | solution.py:41
  48.9 102.2 %all-to-all-done = f32[2,16,2,136,128]{4,3,2,0,1:T(8,128)} async-done(((f32[2,16,2,136,128]{4,3,2,0,1:T(8,128)}), f32[2,16,2,136,128]{4,3,2,0,1:T(8,128)}, u32[]{:S(2)}, u32[]{:S(2)}) %all-to-all-start) | async-done | bytes 4456480 | tf_op jit(solution)/shard_map/all_to_all | solution.py:41
  151.1 4.0 fusion.33
  155.5 1.8 collective-permute-start.2
  157.3 2.5 collective-permute-start
  159.9 1.5 collective-permute-start.1
  161.5 0.9 maximum_add_fusion
  162.4 1.0 collective-permute-done
  163.5 2.4 collective-permute-done.1
  165.9 1.1 fusion.20
  167.0 0.9 pad_maximum_fusion.1
  167.9 1.7 slice_bitcast_fusion
  169.6 37.0 %all_to_all.25 = f32[2,16,128,128]{3,2,0,1:T(8,128)} all-to-all(f32[2,16,128,128]{3,2,0,1:T(8,128)S(1)} %slice_bitcast_fusion), channel_id=1, replica_groups=mesh['row'=16,'col'=16] {'row'}, dimensions={1} | all-to-all | bytes 4194304 | tf_op jit(solution)/shard_map/all_to_all | solution.py:43
  206.6 8.8 %all-to-all-start.2 = ((f32[2,16,128,128]{3,2,0,1:T(8,128)}), f32[2,16,128,128]{3,2,0,1:T(8,128)}, u32[]{:S(2)}, u32[]{:S(2)}) async-start(f32[2,16,128,128]{3,2,0,1:T(8,128)} %all_to_all.25), calls=%async_computation.2 | async-start | bytes 4194304 | tf_op jit(solution)/shard_map/all_to_all | solution.py:44
  215.5 60.4 %all-to-all-done.2 = f32[2,16,128,128]{3,2,0,1:T(8,128)} async-done(((f32[2,16,128,128]{3,2,0,1:T(8,128)}), f32[2,16,128,128]{3,2,0,1:T(8,128)}, u32[]{:S(2)}, u32[]{:S(2)}) %all-to-all-start.2) | async-done | bytes 2097184 | tf_op jit(solution)/shard_map/all_to_all | solution.py:44
  275.9 3.6 gather_fusion.1
  279.5 1.9 bitcast_add_fusion
  281.4 2.5 fusion.1
  283.9 5.0 %copy.74 = f32[32,136,128]{2,1,0:T(8,128)} copy(f32[32,136,128]{1,2,0:T(8,128)} %fusion.1) | data formatting | bytes 4456448 | tf_op jit(solution)/shard_map/concatenate | solution.py:57
  288.9 3.3 collective-permute-start.4
  292.3 58.1 %collective-permute-done.4 = f32[32,136,128]{2,1,0:T(8,128)} collective-permute-done((f32[32,136,128]{2,1,0:T(8,128)}, f32[32,136,128]{2,1,0:T(8,128)}, u32[]{:S(2)}, u32[]{:S(2)}) %collective-permute-start.4) | collective-permute-done | bytes 2228256 | tf_op jit(solution)/shard_map/ppermute | solution.py:13
  350.4 5.2 %all-gather.3.cloned.1.call-done = f32[64,2,136,128]{3,2,1,0:T(8,128)} async-done(((f32[4,2,136,128]{3,2,1,0:T(8,128)}), f32[64,2,136,128]{3,2,1,0:T(8,128)}) %all-gather.3.cloned.1.call-update) | async-done | bytes 8912912 | tf_op jit(solution)/shard_map/all_gather | solution.py:55
  355.6 6.6 %fusion.32 = (f32[1,16,2,136,128]{4,3,2,0,1:T(8,128)}, f32[1,16,2,136,128]{4,3,2,0,1:T(8,128)S(1)}, f32[1,16,2,136,128]{4,3,2,0,1:T(8,128)}, f32[1,16,2,136,128]{4,3,2,0,1:T(8,128)S(1)}) fusion(f32[4,16,2,136,128]{4,3,2,0,1:T(8,128)} %bitcast.108), kind=kLoop, calls=%fused_computation.82 | loop fusion | bytes 17825792 | tf_op jit(solution)/shard_map/slice | solution.py:66
  362.2 1.4 copy-done.1
  363.6 0.7 fusion.22
  364.3 0.7 fusion.24
  365.0 3.7 gather_fusion.2
  368.7 3.7 gather_fusion.4
  372.4 1.6 fusion.23
  374.0 3.7 gather_fusion.3
  377.7 1.6 fusion.21
  379.3 4.5 %fusion.11 = f32[32,128,128]{2,1,0:T(8,128)S(1)} fusion(f32[32,136,128]{2,1,0:T(8,128)} %gather_fusion.2, f32[32,136,128]{2,1,0:T(8,128)} %bitcast.114), kind=kOutput, calls=%fused_computation.21 | convolution fusion | flops 805306368 | bytes 6291456 | tf_op jit(solution)/shard_map/rik,rkj->rij/dot_general | solution.py:70
  383.9 3.5 fusion.5
  387.4 3.6 fusion.8
  391.0 5.2 %collective-permute-done.5 = f32[32,136,128]{2,1,0:T(8,128)} collective-permute-done((f32[32,136,128]{2,1,0:T(8,128)}, f32[32,136,128]{2,1,0:T(8,128)}, u32[]{:S(2)}, u32[]{:S(2)}) %collective-permute-start.5) | collective-permute-done | bytes 2228256 | tf_op jit(solution)/shard_map/ppermute | solution.py:13
  396.1 3.8 gather_fusion.5
  399.9 3.5 compare_reduce_fusion.3
  403.4 7.4 %add_bitcast_fusion = f32[32,1,128,128]{3,2,1,0:T(8,128)} fusion(f32[32,128,128]{2,1,0:T(8,128)} %fusion.5, f32[32,128,128]{2,1,0:T(8,128)} %fusion.8, f32[32,128,128]{2,1,0:T(8,128)S(1)} %fusion.11, f32[32,136,128]{2,1,0:T(8,128)} %gather_fusion.5, f32[32,136,128]{2,1,0:T(8,128)} %bitcast.116, pred[32]{0:T(512)(128)(4,1)S(1)} %get-tuple-element.18, ...), kind=kOutput, calls=%fused_computation.27 | convolution fusion | flops 808976384 | bytes 12583040 | tf_op jit(solution)/shard_map/rik,rkj->rij/dot_general | solution.py:70
  (50 shorter events, 1.5 us)
Async XLA Ops:
  38.6 112.5 %all-to-all-start = ((f32[2,16,2,136,128]{4,3,2,0,1:T(8,128)}), f32[2,16,2,136,128]{4,3,2,0,1:T(8,128)}, u32[]{:S(2)}, u32[]{:S(2)}) async-start(f32[2,16,2,136,128]{4,3,2,0,1:T(8,128)} %pad_maximum_fusion), calls=%async_computation | async-start | bytes 8912896 | tf_op jit(solution)/shard_map/all_to_all | solution.py:41
  48.7 306.9 %all-gather.3.cloned.1.call-start = ((), (), s32[]{:S(2)}) async-start(), calls=%async_computation.3 | async-start | bytes 9469952 | tf_op jit(solution)/shard_map/all_gather | solution.py:55
  155.5 6.9 %collective-permute-start.2 = (f32[2,136,128]{2,1,0:T(8,128)S(1)}, f32[2,136,128]{2,1,0:T(8,128)S(1)}, u32[]{:S(2)}, u32[]{:S(2)}) collective-permute-start(f32[2,136,128]{2,1,0:T(8,128)S(1)} %pad_maximum_fusion.4), channel_id=1, source_target_pairs={{48,0},{64,16},{80,32},{96,48},{112,64},{128,80},{144,96},{160,112... | collective-permute-start | bytes 417800 | tf_op jit(solution)/shard_map/ppermute | solution.py:13
  157.3 6.1 %collective-permute-start = (f32[2,136,128]{2,1,0:T(8,128)S(1)}, f32[2,136,128]{2,1,0:T(8,128)S(1)}, u32[]{:S(2)}, u32[]{:S(2)}) collective-permute-start(f32[2,136,128]{2,1,0:T(8,128)S(1)} %pad_maximum_fusion.2), channel_id=1, source_target_pairs={{16,0},{32,16},{48,32},{64,48},{80,64},{96,80},{112,96},{128,112},... | collective-permute-start | bytes 417800 | tf_op jit(solution)/shard_map/ppermute | solution.py:13
  159.9 6.0 %collective-permute-start.1 = (f32[2,136,128]{2,1,0:T(8,128)S(1)}, f32[2,136,128]{2,1,0:T(8,128)S(1)}, u32[]{:S(2)}, u32[]{:S(2)}) collective-permute-start(f32[2,136,128]{2,1,0:T(8,128)S(1)} %pad_maximum_fusion.3), channel_id=1, source_target_pairs={{32,0},{48,16},{64,32},{80,48},{96,64},{112,80},{128,96},{144,112}... | collective-permute-start | bytes 417800 | tf_op jit(solution)/shard_map/ppermute | solution.py:13
  206.6 69.3 %all-to-all-start.2 = ((f32[2,16,128,128]{3,2,0,1:T(8,128)}), f32[2,16,128,128]{3,2,0,1:T(8,128)}, u32[]{:S(2)}, u32[]{:S(2)}) async-start(f32[2,16,128,128]{3,2,0,1:T(8,128)} %all_to_all.25), calls=%async_computation.2 | async-start | bytes 4194304 | tf_op jit(solution)/shard_map/all_to_all | solution.py:44
  283.9 8.3 %copy-start.6 = (s32[32,1]{0,1:T(1,128)S(1)}, s32[32,1]{0,1:T(1,128)}, u32[]{:S(2)}) copy-start(s32[32,1]{0,1:T(1,128)} %param.6) | copy-start | bytes 388
  288.9 61.5 %collective-permute-start.4 = (f32[32,136,128]{2,1,0:T(8,128)}, f32[32,136,128]{2,1,0:T(8,128)}, u32[]{:S(2)}, u32[]{:S(2)}) collective-permute-start(f32[32,136,128]{2,1,0:T(8,128)} %copy.74), channel_id=1, source_target_pairs={{32,0},{48,16},{64,32},{80,48},{96,64},{112,80},{128,96},{144,112}... | collective-permute-start | bytes 6684680 | tf_op jit(solution)/shard_map/ppermute | solution.py:13
  292.2 81.8 %collective-permute-start.3 = (f32[32,136,128]{2,1,0:T(8,128)}, f32[32,136,128]{2,1,0:T(8,128)}, u32[]{:S(2)}, u32[]{:S(2)}) collective-permute-start(f32[32,136,128]{2,1,0:T(8,128)} %copy.74), channel_id=1, source_target_pairs={{16,0},{32,16},{48,32},{64,48},{80,64},{96,80},{112,96},{128,112},... | collective-permute-start | bytes 6684680 | tf_op jit(solution)/shard_map/ppermute | solution.py:13
  350.4 45.7 %collective-permute-start.5 = (f32[32,136,128]{2,1,0:T(8,128)}, f32[32,136,128]{2,1,0:T(8,128)}, u32[]{:S(2)}, u32[]{:S(2)}) collective-permute-start(f32[32,136,128]{2,1,0:T(8,128)} %collective-permute-done.4), channel_id=1, source_target_pairs={{16,0},{32,16},{48,32},{64,48},{80,64},{96,80},{112,96},{128,112},... | collective-permute-start | bytes 6684680 | tf_op jit(solution)/shard_map/ppermute | solution.py:13
  362.2 1.4 copy-start.1
  362.2 2.1 copy-start.3
  379.3 4.5 %copy-start.2 = (f32[1,16,2,136,128]{4,3,2,0,1:T(8,128)S(1)}, f32[1,16,2,136,128]{4,3,2,0,1:T(8,128)}, u32[]{:S(2)}) copy-start(f32[1,16,2,136,128]{4,3,2,0,1:T(8,128)} %copy-done.1) | copy-start | bytes 6684676
  379.3 4.5 %copy-start.4 = (f32[32,136,128]{2,1,0:T(8,128)S(1)}, f32[32,136,128]{2,1,0:T(8,128)}, u32[]{:S(2)}) copy-start(f32[32,136,128]{2,1,0:T(8,128)} %gather_fusion.4) | copy-start | bytes 6684676
  383.8 3.6 copy-start
  383.9 3.5 copy-start.5
Sparse Core Ops, SparseCore 0:
  168.0 187.5 all-gather.2

commit v9 on v5

v9 whole, which is shorter than its diff:
```python
import jax
import jax.numpy as jnp
from jax import lax
from jax.sharding import PartitionSpec as P

STEPS = 4
EXTRA = 8


def shifted(block, axis, distance):
    size = lax.axis_size(axis)
    route = [((i + distance) % size, i) for i in range(size)]
    return lax.ppermute(block, axis, route)


def transposed(block, rows, cols):
    route = [(b * cols + a, a * cols + b) for a in range(rows) for b in range(cols)]
    return lax.ppermute(block, ("row", "col"), route)


def shards(stored_blocks, block_cols, storage_map):
    rows = lax.axis_size("row")
    cols = lax.axis_size("col")
    local_rows = stored_blocks.shape[0]
    bs = stored_blocks.shape[-1]
    row_index = lax.axis_index("row")

    held = stored_blocks[:, 0] * storage_map.astype(jnp.float32)[:, :, None]
    own_cols = block_cols[:, 0]
    inverse = jnp.zeros((local_rows,), jnp.int32).at[own_cols].set(jnp.arange(local_rows, dtype=jnp.int32))
    mirror_out = jnp.swapaxes(held[inverse], 1, 2)
    chunk = local_rows // cols
    span = chunk * bs
    tags = jnp.zeros((cols, EXTRA, bs), jnp.float32).at[:, 0, :chunk].set(
        own_cols.astype(jnp.float32).reshape(cols, chunk)
    )
    pieces = jnp.concatenate([
        held.reshape(cols, span, bs),
        mirror_out.reshape(cols, span, bs),
        tags,
    ], axis=1)
    spread = lax.all_to_all(pieces, "col", 0, 0, tiled=True)
    first = jnp.swapaxes(spread[:, :span].reshape(cols, chunk, bs, bs), 0, 1)
    second = lax.all_to_all(first, "row", 1, 1, tiled=True)
    arrived = lax.all_to_all(second, "col", 1, 0, tiled=True).reshape(local_rows, bs, bs)
    density = held + jnp.swapaxes(arrived[own_cols], 1, 2)
    mine = []
    for step in range(STEPS):
        own = lax.dynamic_index_in_dim(spread, (row_index + step) % cols, 0, keepdims=False)
        far = lax.dynamic_index_in_dim(spread, (row_index - step) % cols, 0, keepdims=False)[span:2 * span]
        if step:
            far = shifted(far, "row", step)
        blocks = (own[:span] + far).reshape(chunk, bs, bs)
        marks = jnp.zeros((chunk, EXTRA, bs), jnp.float32).at[:, 0, 0].set(own[2 * span, :chunk])
        mine.append(jnp.concatenate([blocks, marks], axis=1))
    mine = jnp.stack(mine)
    left_all = lax.all_gather(mine, "col", axis=0, tiled=False)
    left_all = jnp.transpose(left_all, (1, 0, 2, 3, 4)).reshape(STEPS, local_rows, bs + EXTRA, bs)

    one = shifted(density, "row", 1)
    two = shifted(density, "row", 2)
    three = shifted(two, "row", 1)
    rights = [density, one, two, three]
    cols_two = shifted(own_cols, "row", 2)
    right_cols = [own_cols, shifted(own_cols, "row", 1), cols_two, shifted(cols_two, "row", 1)]

    total = jnp.zeros((local_rows, bs, bs), jnp.float32)
    for step in range(STEPS):
        left = left_all[step]
        inner = left[:, bs, 0].astype(jnp.int32)
        right = rights[step][inner]
        match = right_cols[step][inner] == own_cols
        term = jnp.einsum("rik,rkj->rij", left[:, :bs], right, precision=lax.Precision.HIGHEST)
        total = total + jnp.where(match[:, None, None], term, jnp.float32(0.0))
    return total[:, None]


def solution(mesh):
    return jax.shard_map(
        shards,
        mesh=mesh,
        in_specs=(P("row", "col", None, None), P("row", "col"), P("row", "col")),
        out_specs=P("row", "col", None, None),
        check_vma=False,
    )
```

time: 414 us -> 400 us (0.966)
  matrix products: 19 us -> 29.2 us
  local copies, waits for them, and re-layouts: 50.8 us -> 40.6 us
  waiting for transfers between devices: 234 us -> 224 us
    dot_general x4, matrix products: 19 us -> 29.2 us  [shards(): jnp.einsum('rik,rkj->rij', left[:, :bs], right, precision=lax.Precision.H...]
    ppermute x6 -> x9, waiting for transfers between devices: 66.6 us -> 57.7 us  [shifted(): return lax.ppermute(block, axis, route)]
    concatenate x2 -> x0, local copies, waits for them, and re-layouts: 6.89 us -> none  [the longest x1 4.99 us: shards(): density = jnp.concatenate([density, tag], axis=1)]
    add x2 -> x3, other arithmetic: 1.91 us -> 6.19 us  [the longest x1 3.19 us: shards(): density = held + jnp.swapaxes(arrived[own_cols], 1, 2)]
    all_to_all x1, waiting for transfers between devices: 102 us -> 98 us  [shards(): spread = lax.all_to_all(pieces, 'col', 0, 0, tiled=True)]
    ppermute x6 -> x9, starting transfers between devices: 8.87 us -> 11.1 us  [shifted(): return lax.ppermute(block, axis, route)]
  transfers between devices with their start and end apart: 9 -> 12, of which waited for: 8 -> 4; matrix products, arithmetic and copies ran while one was open for 12% -> 14% of each run, Pallas kernels for 0% -> 0%
where the time goes in v9:
time: 400 us; the launch traced here: 398 us
  waiting for transfers between devices  224 us (56%)
  local copies, waits for them, and re-layouts  40.6 us (10%)
  blocking collectives  36.7 us (9%)
  starting transfers between devices  30.1 us (8%)
  matrix products  29.2 us (7%)
  other arithmetic  23.6 us (6%)
  between operations  13.7 us (3%)
    all_to_all x1, waiting for transfers between devices, shards(): spread = lax.all_to_all(pieces, 'col', 0, 0, tiled=True)  98 us
    all_to_all x1, waiting for transfers between devices, shards(): lax.all_to_all(second, 'col', 1, 0, tiled=True).reshape(local_rows, bs, bs)  61.9 us
    ppermute x9, waiting for transfers between devices, shifted(): return lax.ppermute(block, axis, route)  57.7 us
    all_to_all x1, blocking collectives, shards(): second = lax.all_to_all(first, 'row', 1, 1, tiled=True)  36.7 us
    dot_general x4, matrix products, shards(): jnp.einsum('rik,rkj->rij', left[:, :bs], right, precision=lax.Precision.H...  29.2 us
    gather x4, local copies, waits for them, and re-layouts, shards(): right = rights[step][inner]  14.9 us
    ppermute x9, starting transfers between devices, shifted(): return lax.ppermute(block, axis, route)  11.1 us
    all_to_all x1, starting transfers between devices, shards(): spread = lax.all_to_all(pieces, 'col', 0, 0, tiled=True)  10.2 us
  transfers between devices with their start and end apart: 12, of which 4 were waited for; matrix products, arithmetic and copies ran while one was open for 14% of the time, Pallas kernels for 0%

profile of v9, /device:TPU:2, one launch (start us, length us, event | category | flops | bytes accessed | tf_op | source)
XLA Modules:
  0.0 397.6 jit_solution(14748364994326740019)
XLA Ops:
  7.2 0.7 convert_reduce_fusion.1
  8.5 0.7 convert_reduce_fusion
  9.2 0.7 scatter_custom_fusion
  10.2 1.9 copy.21
  12.1 3.6 broadcast_multiply_fusion
  15.7 1.5 bitcast_multiply_fusion
  17.2 3.6 gather_fusion
  20.8 4.5 %select_maximum_fusion = f32[16,520,128]{2,1,0:T(8,128)} fusion(f32[16,1,2]{2,1,0:T(1,128)S(1)} %bitcast.131, f32[16,256,128]{2,1,0:T(8,128)} %bitcast.122, f32[16,256,128]{2,1,0:T(8,128)} %broadcast_multiply_fusion), kind=kLoop, calls=%fused_computation.11 | loop fusion | flops 4259840 | bytes 8454272 | tf_op jit(solution)/shard_map/concatenate | solution.py:37
  25.3 10.2 %all-to-all-start = ((f32[16,520,128]{2,1,0:T(8,128)}), f32[16,520,128]{2,1,0:T(8,128)}, u32[]{:S(2)}, u32[]{:S(2)}) async-start(f32[16,520,128]{2,1,0:T(8,128)} %select_maximum_fusion), calls=%async_computation | async-start | bytes 8519680 | tf_op jit(solution)/shard_map/all_to_all | solution.py:42
  35.7 98.0 %all-to-all-done = f32[16,520,128]{2,1,0:T(8,128)} async-done(((f32[16,520,128]{2,1,0:T(8,128)}), f32[16,520,128]{2,1,0:T(8,128)}, u32[]{:S(2)}, u32[]{:S(2)}) %all-to-all-start) | async-done | bytes 4259872 | tf_op jit(solution)/shard_map/all_to_all | solution.py:42
  133.6 1.9 dynamic-slice_add_fusion
  135.5 1.7 collective-permute-start.2
  137.2 1.4 collective-permute-start.1
  138.7 2.2 collective-permute-start
  140.8 1.3 dynamic-slice_bitcast_fusion.3
  142.7 1.3 copy.36
  144.6 0.8 copy.37
  145.5 1.1 fusion.14
  147.4 0.9 pad_maximum_fusion
  148.2 1.7 slice.256
  150.0 36.7 %all_to_all.25 = f32[2,16,128,128]{3,2,0,1:T(8,128)} all-to-all(f32[2,16,128,128]{3,2,0,1:T(8,128)S(1)} %bitcast.124), channel_id=1, replica_groups=mesh['row'=16,'col'=16] {'row'}, dimensions={1} | all-to-all | bytes 4194304 | tf_op jit(solution)/shard_map/all_to_all | solution.py:44
  186.7 8.8 %all-to-all-start.2 = ((f32[2,16,128,128]{3,2,0,1:T(8,128)}), f32[2,16,128,128]{3,2,0,1:T(8,128)}, u32[]{:S(2)}, u32[]{:S(2)}) async-start(f32[2,16,128,128]{3,2,0,1:T(8,128)} %all_to_all.25), calls=%async_computation.2 | async-start | bytes 4194304 | tf_op jit(solution)/shard_map/all_to_all | solution.py:45
  195.5 61.9 %all-to-all-done.2 = f32[2,16,128,128]{3,2,0,1:T(8,128)} async-done(((f32[2,16,128,128]{3,2,0,1:T(8,128)}), f32[2,16,128,128]{3,2,0,1:T(8,128)}, u32[]{:S(2)}, u32[]{:S(2)}) %all-to-all-start.2) | async-done | bytes 2097184 | tf_op jit(solution)/shard_map/all_to_all | solution.py:45
  257.5 3.6 gather_fusion.2
  261.1 3.2 bitcast_add_fusion
  264.2 0.8 collective-permute-start.6
  265.0 2.5 collective-permute-start.5
  267.5 57.7 %collective-permute-done.5 = s32[32]{0:T(128)S(1)} collective-permute-done((s32[32]{0:T(128)S(1)}, s32[32]{0:T(128)S(1)}, u32[]{:S(2)}, u32[]{:S(2)}) %collective-permute-start.5) | collective-permute-done | bytes 160 | tf_op jit(solution)/shard_map/ppermute | solution.py:13
  325.5 2.2 collective-permute-start.8
  327.7 6.1 %all-gather.3.cloned.1.call-done = f32[64,2,136,128]{3,2,1,0:T(8,128)} async-done(((f32[4,2,136,128]{3,2,1,0:T(8,128)}), f32[64,2,136,128]{3,2,1,0:T(8,128)}) %all-gather.3.cloned.1.call-update) | async-done | bytes 8912912 | tf_op jit(solution)/shard_map/all_gather | solution.py:57
  333.8 5.6 %fusion.26 = (f32[1,16,2,136,128]{4,3,2,0,1:T(8,128)S(1)}, f32[1,16,2,136,128]{4,3,2,0,1:T(8,128)}, f32[1,16,2,136,128]{4,3,2,0,1:T(8,128)S(1)}, f32[1,16,2,136,128]{4,3,2,0,1:T(8,128)S(1)}) fusion(f32[4,16,2,136,128]{4,3,2,0,1:T(8,128)} %bitcast.113), kind=kLoop, calls=%fused_computation.88 | loop fusion | bytes 17825792 | tf_op jit(solution)/shard_map/slice | solution.py:69
  339.4 0.7 fusion.18
  340.0 0.7 fusion.16
  340.7 0.7 fusion.17
  341.4 0.7 copy-done.5
  342.1 0.7 gather_fusion.1
  342.8 3.6 gather_fusion.3
  346.5 0.7 gather_fusion.6
  347.2 3.6 gather_fusion.7
  350.8 0.7 gather_fusion.4
  351.5 1.6 fusion.15
  353.1 3.6 gather_fusion.5
  356.7 0.7 gather_fusion.8
  357.5 8.2 %fusion.6 = f32[32,128,128]{2,1,0:T(8,128)} fusion(f32[32,128,128]{1,2,0:T(8,128)} %gather_fusion.3, f32[32,136,128]{2,1,0:T(8,128)} %bitcast.119), kind=kOutput, calls=%fused_computation.19 | convolution fusion | flops 805306368 | bytes 6291456 | tf_op jit(solution)/shard_map/rik,rkj->rij/dot_general | solution.py:73
  365.7 5.8 %fusion.2 = f32[32,128,128]{2,1,0:T(8,128)} fusion(f32[32,128,128]{1,2,0:T(8,128)S(1)} %copy-done.6, f32[32,136,128]{2,1,0:T(8,128)S(1)} %bitcast.117), kind=kOutput, calls=%fused_computation.15 | convolution fusion | flops 805306368 | bytes 6291456 | tf_op jit(solution)/shard_map/rik,rkj->rij/dot_general | solution.py:73
  371.5 5.8 %fusion.4 = f32[32,128,128]{2,1,0:T(8,128)} fusion(f32[32,128,128]{1,2,0:T(8,128)S(1)} %copy-done.7, f32[32,136,128]{2,1,0:T(8,128)S(1)} %bitcast.115), kind=kOutput, calls=%fused_computation.17 | convolution fusion | flops 805306368 | bytes 6291456 | tf_op jit(solution)/shard_map/rik,rkj->rij/dot_general | solution.py:73
  377.3 4.1 %gather_fusion.9 = f32[32,128,128]{1,2,0:T(8,128)} fusion(f32[32,128,128]{1,2,0:T(8,128)} %collective-permute-done.8, s32[1024]{0:T(1024)S(1)} %pad_clamp_fusion), kind=kCustom, calls=%fused_computation.9 | custom fusion | bytes 4194432 | tf_op jit(solution)/shard_map/gather | solution.py:71
  381.4 9.3 %add_bitcast_fusion = f32[32,1,128,128]{3,2,1,0:T(8,128)} fusion(f32[32,128,128]{2,1,0:T(8,128)} %fusion.2, f32[32,128,128]{2,1,0:T(8,128)} %fusion.4, f32[32,128,128]{2,1,0:T(8,128)S(1)} %copy-done.8, pred[32]{0:T(512)(128)(4,1)S(1)} %get-tuple-element.83, pred[32]{0:T(512)(128)(4,1)S(1)} %get-tuple-element.82, pred[32]{0:T(512)(128)(4,1)S(1)} %get-tuple-element.81, ...), kind=kOutput, calls=%fused_computation.23 | convolution fusion | flops 808976384 | bytes 12583040 | tf_op jit(solution)/shard_map/rik,rkj->rij/dot_general | solution.py:73
  (61 shorter events, 4.1 us)
Async XLA Ops:
  8.5 1.4 copy-start.9
  25.3 108.3 %all-to-all-start = ((f32[16,520,128]{2,1,0:T(8,128)}), f32[16,520,128]{2,1,0:T(8,128)}, u32[]{:S(2)}, u32[]{:S(2)}) async-start(f32[16,520,128]{2,1,0:T(8,128)} %select_maximum_fusion), calls=%async_computation | async-start | bytes 8519680 | tf_op jit(solution)/shard_map/all_to_all | solution.py:42
  35.5 298.2 %all-gather.3.cloned.1.call-start = ((), (), s32[]{:S(2)}) async-start(), calls=%async_computation.3 | async-start | bytes 9469952 | tf_op jit(solution)/shard_map/all_gather | solution.py:57
  135.5 10.0 %collective-permute-start.2 = (f32[256,128]{1,0:T(8,128)}, f32[256,128]{1,0:T(8,128)S(1)}, u32[]{:S(2)}, u32[]{:S(2)}) collective-permute-start(f32[256,128]{1,0:T(8,128)} %get-tuple-element.70), channel_id=1, source_target_pairs={{48,0},{64,16},{80,32},{96,48},{112,64},{128,80},{144,96},{160,112... | collective-permute-start | bytes 393224 | tf_op jit(solution)/shard_map/ppermute | solution.py:13
  137.2 8.3 %collective-permute-start.1 = (f32[256,128]{1,0:T(8,128)S(1)}, f32[256,128]{1,0:T(8,128)S(1)}, u32[]{:S(2)}, u32[]{:S(2)}) collective-permute-start(f32[256,128]{1,0:T(8,128)S(1)} %get-tuple-element.71), channel_id=1, source_target_pairs={{32,0},{48,16},{64,32},{80,48},{96,64},{112,80},{128,96},{144,112}... | collective-permute-start | bytes 393224 | tf_op jit(solution)/shard_map/ppermute | solution.py:13
  138.7 6.8 %collective-permute-start = (f32[256,128]{1,0:T(8,128)S(1)}, f32[256,128]{1,0:T(8,128)}, u32[]{:S(2)}, u32[]{:S(2)}) collective-permute-start(f32[256,128]{1,0:T(8,128)S(1)} %get-tuple-element.72), channel_id=1, source_target_pairs={{16,0},{32,16},{48,32},{64,48},{80,64},{96,80},{112,96},{128,112},... | collective-permute-start | bytes 393224 | tf_op jit(solution)/shard_map/ppermute | solution.py:13
  186.7 8.8 %copy-start.10 = (s32[32]{0:T(128)S(1)}, s32[32]{0:T(128)}, u32[]{:S(2)}) copy-start(s32[32]{0:T(128)} %copy-done.9) | copy-start | bytes 388
  186.7 70.8 %all-to-all-start.2 = ((f32[2,16,128,128]{3,2,0,1:T(8,128)}), f32[2,16,128,128]{3,2,0,1:T(8,128)}, u32[]{:S(2)}, u32[]{:S(2)}) async-start(f32[2,16,128,128]{3,2,0,1:T(8,128)} %all_to_all.25), calls=%async_computation.2 | async-start | bytes 4194304 | tf_op jit(solution)/shard_map/all_to_all | solution.py:45
  261.0 4.0 copy-start
  264.2 61.2 %collective-permute-start.6 = (f32[32,128,128]{1,2,0:T(8,128)}, f32[32,128,128]{1,2,0:T(8,128)}, u32[]{:S(2)}, u32[]{:S(2)}) collective-permute-start(f32[32,128,128]{1,2,0:T(8,128)} %bitcast_add_fusion), channel_id=1, source_target_pairs={{32,0},{48,16},{64,32},{80,48},{96,64},{112,80},{128,96},{144,112}... | collective-permute-start | bytes 6291464 | tf_op jit(solution)/shard_map/ppermute | solution.py:13
  265.0 60.2 %collective-permute-start.5 = (s32[32]{0:T(128)S(1)}, s32[32]{0:T(128)S(1)}, u32[]{:S(2)}, u32[]{:S(2)}) collective-permute-start(s32[32]{0:T(128)S(1)} %bitcast.110), channel_id=1, source_target_pairs={{32,0},{48,16},{64,32},{80,48},{96,64},{112,80},{128,96},{144,112}... | collective-permute-start | bytes 392 | tf_op jit(solution)/shard_map/ppermute | solution.py:13
  267.5 83.3 %collective-permute-start.3 = (s32[32]{0:T(128)S(1)}, s32[32]{0:T(128)S(1)}, u32[]{:S(2)}, u32[]{:S(2)}) collective-permute-start(s32[32]{0:T(128)S(1)} %bitcast.111), channel_id=1, source_target_pairs={{16,0},{32,16},{48,32},{64,48},{80,64},{96,80},{112,96},{128,112},... | collective-permute-start | bytes 392 | tf_op jit(solution)/shard_map/ppermute | solution.py:13
  325.2 31.5 %collective-permute-start.7 = (s32[32]{0:T(128)S(1)}, s32[32]{0:T(128)S(1)}, u32[]{:S(2)}, u32[]{:S(2)}) collective-permute-start(s32[32]{0:T(128)S(1)} %collective-permute-done.5), channel_id=1, source_target_pairs={{16,0},{32,16},{48,32},{64,48},{80,64},{96,80},{112,96},{128,112},... | collective-permute-start | bytes 392 | tf_op jit(solution)/shard_map/ppermute | solution.py:13
  325.2 27.9 %collective-permute-start.4 = (f32[32,128,128]{1,2,0:T(8,128)}, f32[32,128,128]{1,2,0:T(8,128)}, u32[]{:S(2)}, u32[]{:S(2)}) collective-permute-start(f32[32,128,128]{1,2,0:T(8,128)} %bitcast_add_fusion), channel_id=1, source_target_pairs={{16,0},{32,16},{48,32},{64,48},{80,64},{96,80},{112,96},{128,112},... | collective-permute-start | bytes 6291464 | tf_op jit(solution)/shard_map/ppermute | solution.py:13
  325.5 51.8 %collective-permute-start.8 = (f32[32,128,128]{1,2,0:T(8,128)}, f32[32,128,128]{1,2,0:T(8,128)}, u32[]{:S(2)}, u32[]{:S(2)}) collective-permute-start(f32[32,128,128]{1,2,0:T(8,128)} %collective-permute-done.6), channel_id=1, source_target_pairs={{16,0},{32,16},{48,32},{64,48},{80,64},{96,80},{112,96},{128,112},... | collective-permute-start | bytes 6291464 | tf_op jit(solution)/shard_map/ppermute | solution.py:13
  339.4 1.4 copy-start.1
  339.4 2.0 copy-start.3
  339.4 2.7 copy-start.5
  357.5 8.2 %copy-start.4 = (f32[1,16,2,136,128]{4,3,2,0,1:T(8,128)S(1)}, f32[1,16,2,136,128]{4,3,2,0,1:T(8,128)}, u32[]{:S(2)}) copy-start(f32[1,16,2,136,128]{4,3,2,0,1:T(8,128)} %copy-done.3) | copy-start | bytes 6684676
  357.5 8.2 %copy-start.6 = (f32[32,128,128]{1,2,0:T(8,128)S(1)}, f32[32,128,128]{1,2,0:T(8,128)}, u32[]{:S(2)}) copy-start(f32[32,128,128]{1,2,0:T(8,128)} %gather_fusion.7) | copy-start | bytes 6291460
  365.7 5.8 %copy-start.2 = (f32[1,16,2,136,128]{4,3,2,0,1:T(8,128)S(1)}, f32[1,16,2,136,128]{4,3,2,0,1:T(8,128)}, u32[]{:S(2)}) copy-start(f32[1,16,2,136,128]{4,3,2,0,1:T(8,128)} %copy-done.1) | copy-start | bytes 6684676
  365.7 5.8 %copy-start.7 = (f32[32,128,128]{1,2,0:T(8,128)S(1)}, f32[32,128,128]{1,2,0:T(8,128)}, u32[]{:S(2)}) copy-start(f32[32,128,128]{1,2,0:T(8,128)} %gather_fusion.5) | copy-start | bytes 6291460
  377.3 4.1 %copy-start.8 = (f32[32,128,128]{2,1,0:T(8,128)S(1)}, f32[32,128,128]{2,1,0:T(8,128)}, u32[]{:S(2)}) copy-start(f32[32,128,128]{2,1,0:T(8,128)} %fusion.6) | copy-start | bytes 6291460
Sparse Core Ops, SparseCore 0:
  148.4 185.3 all-gather.2

commit v10 on v9

--- a/solution.py
+++ b/solution.py
@@ -70,7 +70,7 @@
         inner = left[:, bs, 0].astype(jnp.int32)
         right = rights[step][inner]
         match = right_cols[step][inner] == own_cols
-        term = jnp.einsum("rik,rkj->rij", left[:, :bs], right, precision=lax.Precision.HIGHEST)
+        term = jnp.einsum("rik,rkj->rij", left[:, :bs], right, precision=lax.Precision.HIGH)
         total = total + jnp.where(match[:, None, None], term, jnp.float32(0.0))
     return total[:, None]
 

time: 400 us -> 394 us (0.985)
  matrix products: 29.2 us -> 20.5 us
    dot_general x4, matrix products: 29.2 us -> 20.5 us  [shards(): jnp.einsum('rik,rkj->rij', left[:, :bs], right, precision=lax.Precision.H...]
  transfers between devices with their start and end apart: 12 -> 12, of which waited for: 4 -> 5; matrix products, arithmetic and copies ran while one was open for 14% -> 13% of each run, Pallas kernels for 0% -> 0%
where the time goes in v10:
time: 394 us; the launch traced here: 390 us
  waiting for transfers between devices  225 us (57%)
  local copies, waits for them, and re-layouts  40.2 us (10%)
  blocking collectives  36.7 us (9%)
  starting transfers between devices  30.1 us (8%)
  other arithmetic  23.6 us (6%)
  matrix products  20.5 us (5%)
  between operations  13.7 us (3%)
    all_to_all x1, waiting for transfers between devices, shards(): spread = lax.all_to_all(pieces, 'col', 0, 0, tiled=True)  98 us
    all_to_all x1, waiting for transfers between devices, shards(): lax.all_to_all(second, 'col', 1, 0, tiled=True).reshape(local_rows, bs, bs)  61.9 us
    ppermute x9, waiting for transfers between devices, shifted(): return lax.ppermute(block, axis, route)  58.7 us
    all_to_all x1, blocking collectives, shards(): second = lax.all_to_all(first, 'row', 1, 1, tiled=True)  36.7 us
    dot_general x4, matrix products, shards(): jnp.einsum('rik,rkj->rij', left[:, :bs], right, precision=lax.Precision.H...  20.5 us
    gather x4, local copies, waits for them, and re-layouts, shards(): right = rights[step][inner]  14.6 us
    ppermute x9, starting transfers between devices, shifted(): return lax.ppermute(block, axis, route)  11.1 us
    all_to_all x1, starting transfers between devices, shards(): spread = lax.all_to_all(pieces, 'col', 0, 0, tiled=True)  10.2 us
  transfers between devices with their start and end apart: 12, of which 5 were waited for; matrix products, arithmetic and copies ran while one was open for 13% of the time, Pallas kernels for 0%

profile of v10, /device:TPU:2, one launch (start us, length us, event | category | flops | bytes accessed | tf_op | source)
XLA Modules:
  0.0 389.5 jit_solution(4691405540741249810)
XLA Ops:
  7.2 0.7 convert_reduce_fusion.1
  8.5 0.7 convert_reduce_fusion
  9.2 0.7 scatter_custom_fusion
  10.2 1.9 copy.21
  12.1 3.6 broadcast_multiply_fusion
  15.7 1.5 bitcast_multiply_fusion
  17.2 3.6 gather_fusion
  20.8 4.5 %select_maximum_fusion = f32[16,520,128]{2,1,0:T(8,128)} fusion(f32[16,1,2]{2,1,0:T(1,128)S(1)} %bitcast.131, f32[16,256,128]{2,1,0:T(8,128)} %bitcast.122, f32[16,256,128]{2,1,0:T(8,128)} %broadcast_multiply_fusion), kind=kLoop, calls=%fused_computation.11 | loop fusion | flops 4259840 | bytes 8454272 | tf_op jit(solution)/shard_map/concatenate | solution.py:37
  25.3 10.2 %all-to-all-start = ((f32[16,520,128]{2,1,0:T(8,128)}), f32[16,520,128]{2,1,0:T(8,128)}, u32[]{:S(2)}, u32[]{:S(2)}) async-start(f32[16,520,128]{2,1,0:T(8,128)} %select_maximum_fusion), calls=%async_computation | async-start | bytes 8519680 | tf_op jit(solution)/shard_map/all_to_all | solution.py:42
  35.7 98.0 %all-to-all-done = f32[16,520,128]{2,1,0:T(8,128)} async-done(((f32[16,520,128]{2,1,0:T(8,128)}), f32[16,520,128]{2,1,0:T(8,128)}, u32[]{:S(2)}, u32[]{:S(2)}) %all-to-all-start) | async-done | bytes 4259872 | tf_op jit(solution)/shard_map/all_to_all | solution.py:42
  133.6 1.9 dynamic-slice_add_fusion
  135.5 1.7 collective-permute-start.2
  137.2 1.4 collective-permute-start.1
  138.7 2.2 collective-permute-start
  140.8 1.3 dynamic-slice_bitcast_fusion.3
  142.7 1.3 copy.36
  144.6 0.8 copy.37
  145.5 1.1 fusion.14
  147.4 0.9 pad_maximum_fusion
  148.2 1.7 slice.256
  150.0 36.7 %all_to_all.25 = f32[2,16,128,128]{3,2,0,1:T(8,128)} all-to-all(f32[2,16,128,128]{3,2,0,1:T(8,128)S(1)} %bitcast.124), channel_id=1, replica_groups=mesh['row'=16,'col'=16] {'row'}, dimensions={1} | all-to-all | bytes 4194304 | tf_op jit(solution)/shard_map/all_to_all | solution.py:44
  186.7 8.8 %all-to-all-start.2 = ((f32[2,16,128,128]{3,2,0,1:T(8,128)}), f32[2,16,128,128]{3,2,0,1:T(8,128)}, u32[]{:S(2)}, u32[]{:S(2)}) async-start(f32[2,16,128,128]{3,2,0,1:T(8,128)} %all_to_all.25), calls=%async_computation.2 | async-start | bytes 4194304 | tf_op jit(solution)/shard_map/all_to_all | solution.py:45
  195.5 61.9 %all-to-all-done.2 = f32[2,16,128,128]{3,2,0,1:T(8,128)} async-done(((f32[2,16,128,128]{3,2,0,1:T(8,128)}), f32[2,16,128,128]{3,2,0,1:T(8,128)}, u32[]{:S(2)}, u32[]{:S(2)}) %all-to-all-start.2) | async-done | bytes 2097184 | tf_op jit(solution)/shard_map/all_to_all | solution.py:45
  257.5 3.6 gather_fusion.2
  261.1 3.2 bitcast_add_fusion
  264.2 0.8 collective-permute-start.6
  265.0 2.5 collective-permute-start.5
  267.5 57.7 %collective-permute-done.5 = s32[32]{0:T(128)S(1)} collective-permute-done((s32[32]{0:T(128)S(1)}, s32[32]{0:T(128)S(1)}, u32[]{:S(2)}, u32[]{:S(2)}) %collective-permute-start.5) | collective-permute-done | bytes 160 | tf_op jit(solution)/shard_map/ppermute | solution.py:13
  325.5 2.2 collective-permute-start.8
  327.7 6.1 %all-gather.3.cloned.1.call-done = f32[64,2,136,128]{3,2,1,0:T(8,128)} async-done(((f32[4,2,136,128]{3,2,1,0:T(8,128)}), f32[64,2,136,128]{3,2,1,0:T(8,128)}) %all-gather.3.cloned.1.call-update) | async-done | bytes 8912912 | tf_op jit(solution)/shard_map/all_gather | solution.py:57
  333.8 5.6 %fusion.26 = (f32[1,16,2,136,128]{4,3,2,0,1:T(8,128)S(1)}, f32[1,16,2,136,128]{4,3,2,0,1:T(8,128)}, f32[1,16,2,136,128]{4,3,2,0,1:T(8,128)S(1)}, f32[1,16,2,136,128]{4,3,2,0,1:T(8,128)S(1)}) fusion(f32[4,16,2,136,128]{4,3,2,0,1:T(8,128)} %bitcast.113), kind=kLoop, calls=%fused_computation.88 | loop fusion | bytes 17825792 | tf_op jit(solution)/shard_map/slice | solution.py:69
  339.4 0.7 fusion.18
  340.0 0.7 fusion.16
  341.4 0.7 copy-done.5
  342.1 0.7 gather_fusion.1
  342.8 3.6 gather_fusion.3
  346.5 0.7 gather_fusion.6
  347.2 3.6 gather_fusion.7
  350.8 0.7 gather_fusion.4
  351.5 1.6 fusion.15
  353.1 3.6 gather_fusion.5
  356.7 0.7 gather_fusion.8
  357.5 6.1 %fusion.6 = f32[32,128,128]{2,1,0:T(8,128)} fusion(f32[32,128,128]{1,2,0:T(8,128)} %gather_fusion.3, f32[32,136,128]{2,1,0:T(8,128)} %bitcast.119), kind=kOutput, calls=%fused_computation.19 | convolution fusion | flops 402653184 | bytes 6291456 | tf_op jit(solution)/shard_map/rik,rkj->rij/dot_general | solution.py:73
  363.6 3.6 fusion.2
  367.2 3.6 fusion.4
  370.8 1.0 collective-permute-done.8
  371.8 3.7 gather_fusion.9
  375.5 7.2 %add_bitcast_fusion = f32[32,1,128,128]{3,2,1,0:T(8,128)} fusion(f32[32,128,128]{2,1,0:T(8,128)} %fusion.2, f32[32,128,128]{2,1,0:T(8,128)} %fusion.4, f32[32,128,128]{2,1,0:T(8,128)S(1)} %copy-done.8, pred[32]{0:T(512)(128)(4,1)S(1)} %get-tuple-element.83, pred[32]{0:T(512)(128)(4,1)S(1)} %get-tuple-element.82, pred[32]{0:T(512)(128)(4,1)S(1)} %get-tuple-element.81, ...), kind=kOutput, calls=%fused_computation.23 | convolution fusion | flops 406323200 | bytes 12583040 | tf_op jit(solution)/shard_map/rik,rkj->rij/dot_general | solution.py:73
  (61 shorter events, 4.8 us)
Async XLA Ops:
  8.5 1.4 copy-start.9
  25.3 108.3 %all-to-all-start = ((f32[16,520,128]{2,1,0:T(8,128)}), f32[16,520,128]{2,1,0:T(8,128)}, u32[]{:S(2)}, u32[]{:S(2)}) async-start(f32[16,520,128]{2,1,0:T(8,128)} %select_maximum_fusion), calls=%async_computation | async-start | bytes 8519680 | tf_op jit(solution)/shard_map/all_to_all | solution.py:42
  35.5 298.2 %all-gather.3.cloned.1.call-start = ((), (), s32[]{:S(2)}) async-start(), calls=%async_computation.3 | async-start | bytes 9469952 | tf_op jit(solution)/shard_map/all_gather | solution.py:57
  135.5 10.0 %collective-permute-start.2 = (f32[256,128]{1,0:T(8,128)}, f32[256,128]{1,0:T(8,128)S(1)}, u32[]{:S(2)}, u32[]{:S(2)}) collective-permute-start(f32[256,128]{1,0:T(8,128)} %get-tuple-element.70), channel_id=1, source_target_pairs={{48,0},{64,16},{80,32},{96,48},{112,64},{128,80},{144,96},{160,112... | collective-permute-start | bytes 393224 | tf_op jit(solution)/shard_map/ppermute | solution.py:13
  137.2 8.3 %collective-permute-start.1 = (f32[256,128]{1,0:T(8,128)S(1)}, f32[256,128]{1,0:T(8,128)S(1)}, u32[]{:S(2)}, u32[]{:S(2)}) collective-permute-start(f32[256,128]{1,0:T(8,128)S(1)} %get-tuple-element.71), channel_id=1, source_target_pairs={{32,0},{48,16},{64,32},{80,48},{96,64},{112,80},{128,96},{144,112}... | collective-permute-start | bytes 393224 | tf_op jit(solution)/shard_map/ppermute | solution.py:13
  138.7 6.8 %collective-permute-start = (f32[256,128]{1,0:T(8,128)S(1)}, f32[256,128]{1,0:T(8,128)}, u32[]{:S(2)}, u32[]{:S(2)}) collective-permute-start(f32[256,128]{1,0:T(8,128)S(1)} %get-tuple-element.72), channel_id=1, source_target_pairs={{16,0},{32,16},{48,32},{64,48},{80,64},{96,80},{112,96},{128,112},... | collective-permute-start | bytes 393224 | tf_op jit(solution)/shard_map/ppermute | solution.py:13
  186.7 8.8 %copy-start.10 = (s32[32]{0:T(128)S(1)}, s32[32]{0:T(128)}, u32[]{:S(2)}) copy-start(s32[32]{0:T(128)} %copy-done.9) | copy-start | bytes 388
  186.7 70.8 %all-to-all-start.2 = ((f32[2,16,128,128]{3,2,0,1:T(8,128)}), f32[2,16,128,128]{3,2,0,1:T(8,128)}, u32[]{:S(2)}, u32[]{:S(2)}) async-start(f32[2,16,128,128]{3,2,0,1:T(8,128)} %all_to_all.25), calls=%async_computation.2 | async-start | bytes 4194304 | tf_op jit(solution)/shard_map/all_to_all | solution.py:45
  261.0 4.0 %copy-start = (s32[32,1]{0,1:T(1,128)S(1)}, s32[32,1]{0,1:T(1,128)}, u32[]{:S(2)}) copy-start(s32[32,1]{0,1:T(1,128)} %param.14) | copy-start | bytes 388
  264.2 61.2 %collective-permute-start.6 = (f32[32,128,128]{1,2,0:T(8,128)}, f32[32,128,128]{1,2,0:T(8,128)}, u32[]{:S(2)}, u32[]{:S(2)}) collective-permute-start(f32[32,128,128]{1,2,0:T(8,128)} %bitcast_add_fusion), channel_id=1, source_target_pairs={{32,0},{48,16},{64,32},{80,48},{96,64},{112,80},{128,96},{144,112}... | collective-permute-start | bytes 6291464 | tf_op jit(solution)/shard_map/ppermute | solution.py:13
  265.0 60.2 %collective-permute-start.5 = (s32[32]{0:T(128)S(1)}, s32[32]{0:T(128)S(1)}, u32[]{:S(2)}, u32[]{:S(2)}) collective-permute-start(s32[32]{0:T(128)S(1)} %bitcast.110), channel_id=1, source_target_pairs={{32,0},{48,16},{64,32},{80,48},{96,64},{112,80},{128,96},{144,112}... | collective-permute-start | bytes 392 | tf_op jit(solution)/shard_map/ppermute | solution.py:13
  267.5 83.3 %collective-permute-start.3 = (s32[32]{0:T(128)S(1)}, s32[32]{0:T(128)S(1)}, u32[]{:S(2)}, u32[]{:S(2)}) collective-permute-start(s32[32]{0:T(128)S(1)} %bitcast.111), channel_id=1, source_target_pairs={{16,0},{32,16},{48,32},{64,48},{80,64},{96,80},{112,96},{128,112},... | collective-permute-start | bytes 392 | tf_op jit(solution)/shard_map/ppermute | solution.py:13
  325.2 31.5 %collective-permute-start.7 = (s32[32]{0:T(128)S(1)}, s32[32]{0:T(128)S(1)}, u32[]{:S(2)}, u32[]{:S(2)}) collective-permute-start(s32[32]{0:T(128)S(1)} %collective-permute-done.5), channel_id=1, source_target_pairs={{16,0},{32,16},{48,32},{64,48},{80,64},{96,80},{112,96},{128,112},... | collective-permute-start | bytes 392 | tf_op jit(solution)/shard_map/ppermute | solution.py:13
  325.2 27.9 %collective-permute-start.4 = (f32[32,128,128]{1,2,0:T(8,128)}, f32[32,128,128]{1,2,0:T(8,128)}, u32[]{:S(2)}, u32[]{:S(2)}) collective-permute-start(f32[32,128,128]{1,2,0:T(8,128)} %bitcast_add_fusion), channel_id=1, source_target_pairs={{16,0},{32,16},{48,32},{64,48},{80,64},{96,80},{112,96},{128,112},... | collective-permute-start | bytes 6291464 | tf_op jit(solution)/shard_map/ppermute | solution.py:13
  325.5 46.3 %collective-permute-start.8 = (f32[32,128,128]{1,2,0:T(8,128)}, f32[32,128,128]{1,2,0:T(8,128)}, u32[]{:S(2)}, u32[]{:S(2)}) collective-permute-start(f32[32,128,128]{1,2,0:T(8,128)} %collective-permute-done.6), channel_id=1, source_target_pairs={{16,0},{32,16},{48,32},{64,48},{80,64},{96,80},{112,96},{128,112},... | collective-permute-start | bytes 6291464 | tf_op jit(solution)/shard_map/ppermute | solution.py:13
  339.4 1.4 copy-start.1
  339.4 2.0 copy-start.3
  339.4 2.7 copy-start.5
  357.5 6.1 %copy-start.4 = (f32[1,16,2,136,128]{4,3,2,0,1:T(8,128)S(1)}, f32[1,16,2,136,128]{4,3,2,0,1:T(8,128)}, u32[]{:S(2)}) copy-start(f32[1,16,2,136,128]{4,3,2,0,1:T(8,128)} %copy-done.3) | copy-start | bytes 6684676
  357.5 6.1 %copy-start.6 = (f32[32,128,128]{1,2,0:T(8,128)S(1)}, f32[32,128,128]{1,2,0:T(8,128)}, u32[]{:S(2)}) copy-start(f32[32,128,128]{1,2,0:T(8,128)} %gather_fusion.7) | copy-start | bytes 6291460
  363.5 3.7 copy-start.2
  363.5 3.6 copy-start.7
  370.8 4.7 %copy-start.8 = (f32[32,128,128]{2,1,0:T(8,128)S(1)}, f32[32,128,128]{2,1,0:T(8,128)}, u32[]{:S(2)}) copy-start(f32[32,128,128]{2,1,0:T(8,128)} %fusion.6) | copy-start | bytes 6291460
Sparse Core Ops, SparseCore 0:
  148.4 185.3 all-gather.2

commit v11 on v10

--- a/solution.py
+++ b/solution.py
@@ -70,8 +70,8 @@
         inner = left[:, bs, 0].astype(jnp.int32)
         right = rights[step][inner]
         match = right_cols[step][inner] == own_cols
-        term = jnp.einsum("rik,rkj->rij", left[:, :bs], right, precision=lax.Precision.HIGH)
-        total = total + jnp.where(match[:, None, None], term, jnp.float32(0.0))
+        masked = jnp.where(match[:, None, None], left[:, :bs], jnp.float32(0.0))
+        total = total + jnp.einsum("rik,rkj->rij", masked, right, precision=lax.Precision.HIGH)
     return total[:, None]
 
 

time: 394 us -> 394 us (level)
  transfers between devices with their start and end apart: 12 -> 12, of which waited for: 5 -> 5; matrix products, arithmetic and copies ran while one was open for 13% -> 12% of each run, Pallas kernels for 0% -> 0%
where the time goes in v11:
time: 394 us; the launch traced here: 389 us
  waiting for transfers between devices  225 us (57%)
  local copies, waits for them, and re-layouts  41 us (10%)
  blocking collectives  36.8 us (9%)
  starting transfers between devices  30.1 us (8%)
  other arithmetic  23.6 us (6%)
  matrix products  19.4 us (5%)
  between operations  13.8 us (4%)
    all_to_all x1, waiting for transfers between devices, shards(): spread = lax.all_to_all(pieces, 'col', 0, 0, tiled=True)  98 us
    all_to_all x1, waiting for transfers between devices, shards(): lax.all_to_all(second, 'col', 1, 0, tiled=True).reshape(local_rows, bs, bs)  61.9 us
    ppermute x9, waiting for transfers between devices, shifted(): return lax.ppermute(block, axis, route)  58.8 us
    all_to_all x1, blocking collectives, shards(): second = lax.all_to_all(first, 'row', 1, 1, tiled=True)  36.8 us
    dot_general x4, matrix products, shards(): jnp.einsum('rik,rkj->rij', masked, right, precision=lax.Precision.HIGH)  19.4 us
    gather x4, local copies, waits for them, and re-layouts, shards(): right = rights[step][inner]  14.6 us
    ppermute x9, starting transfers between devices, shifted(): return lax.ppermute(block, axis, route)  11.1 us
    all_to_all x1, starting transfers between devices, shards(): spread = lax.all_to_all(pieces, 'col', 0, 0, tiled=True)  10.2 us
  transfers between devices with their start and end apart: 12, of which 5 were waited for; matrix products, arithmetic and copies ran while one was open for 12% of the time, Pallas kernels for 0%

profile of v11, /device:TPU:2, one launch (start us, length us, event | category | flops | bytes accessed | tf_op | source)
XLA Modules:
  0.0 389.5 jit_solution(15467039397130424935)
XLA Ops:
  7.2 0.7 convert_reduce_fusion.1
  8.5 0.7 convert_reduce_fusion
  9.2 0.7 scatter_custom_fusion
  10.2 1.9 copy.36
  12.1 3.5 broadcast_multiply_fusion
  15.7 1.5 bitcast_multiply_fusion
  17.2 3.6 gather_fusion
  20.8 4.5 %select_maximum_fusion = f32[16,520,128]{2,1,0:T(8,128)} fusion(f32[16,1,2]{2,1,0:T(1,128)S(1)} %bitcast.131, f32[16,256,128]{2,1,0:T(8,128)} %bitcast.122, f32[16,256,128]{2,1,0:T(8,128)} %broadcast_multiply_fusion), kind=kLoop, calls=%fused_computation.11 | loop fusion | flops 4259840 | bytes 8454272 | tf_op jit(solution)/shard_map/concatenate | solution.py:37
  25.3 10.2 %all-to-all-start = ((f32[16,520,128]{2,1,0:T(8,128)}), f32[16,520,128]{2,1,0:T(8,128)}, u32[]{:S(2)}, u32[]{:S(2)}) async-start(f32[16,520,128]{2,1,0:T(8,128)} %select_maximum_fusion), calls=%async_computation | async-start | bytes 8519680 | tf_op jit(solution)/shard_map/all_to_all | solution.py:42
  35.7 98.0 %all-to-all-done = f32[16,520,128]{2,1,0:T(8,128)} async-done(((f32[16,520,128]{2,1,0:T(8,128)}), f32[16,520,128]{2,1,0:T(8,128)}, u32[]{:S(2)}, u32[]{:S(2)}) %all-to-all-start) | async-done | bytes 4259872 | tf_op jit(solution)/shard_map/all_to_all | solution.py:42
  133.6 1.9 dynamic-slice_add_fusion
  135.5 1.7 collective-permute-start.2
  137.2 1.4 collective-permute-start.1
  138.6 2.2 collective-permute-start
  140.8 1.3 dynamic-slice_bitcast_fusion.3
  142.6 1.3 copy.51
  144.4 0.7 copy.52
  145.4 1.1 fusion.18
  147.2 0.8 pad_maximum_fusion
  148.1 1.7 slice.256
  149.8 36.8 %all_to_all.25 = f32[2,16,128,128]{3,2,0,1:T(8,128)} all-to-all(f32[2,16,128,128]{3,2,0,1:T(8,128)S(1)} %bitcast.124), channel_id=1, replica_groups=mesh['row'=16,'col'=16] {'row'}, dimensions={1} | all-to-all | bytes 4194304 | tf_op jit(solution)/shard_map/all_to_all | solution.py:44
  186.7 8.8 %all-to-all-start.2 = ((f32[2,16,128,128]{3,2,0,1:T(8,128)}), f32[2,16,128,128]{3,2,0,1:T(8,128)}, u32[]{:S(2)}, u32[]{:S(2)}) async-start(f32[2,16,128,128]{3,2,0,1:T(8,128)} %all_to_all.25), calls=%async_computation.2 | async-start | bytes 4194304 | tf_op jit(solution)/shard_map/all_to_all | solution.py:45
  195.5 61.9 %all-to-all-done.2 = f32[2,16,128,128]{3,2,0,1:T(8,128)} async-done(((f32[2,16,128,128]{3,2,0,1:T(8,128)}), f32[2,16,128,128]{3,2,0,1:T(8,128)}, u32[]{:S(2)}, u32[]{:S(2)}) %all-to-all-start.2) | async-done | bytes 2097184 | tf_op jit(solution)/shard_map/all_to_all | solution.py:45
  257.4 3.6 gather_fusion.2
  261.0 3.2 bitcast_add_fusion
  264.2 0.8 collective-permute-start.6
  265.0 2.5 collective-permute-start.5
  267.5 57.7 %collective-permute-done.5 = s32[32]{0:T(128)S(1)} collective-permute-done((s32[32]{0:T(128)S(1)}, s32[32]{0:T(128)S(1)}, u32[]{:S(2)}, u32[]{:S(2)}) %collective-permute-start.5) | collective-permute-done | bytes 160 | tf_op jit(solution)/shard_map/ppermute | solution.py:13
  325.5 2.2 collective-permute-start.8
  327.6 6.1 %all-gather.3.cloned.1.call-done = f32[64,2,136,128]{3,2,1,0:T(8,128)} async-done(((f32[4,2,136,128]{3,2,1,0:T(8,128)}), f32[64,2,136,128]{3,2,1,0:T(8,128)}) %all-gather.3.cloned.1.call-update) | async-done | bytes 8912912 | tf_op jit(solution)/shard_map/all_gather | solution.py:57
  333.7 5.8 %fusion.34 = (f32[1,16,2,136,128]{4,3,2,0,1:T(8,128)}, f32[1,16,2,136,128]{4,3,2,0,1:T(8,128)S(1)}, f32[1,16,2,136,128]{4,3,2,0,1:T(8,128)S(1)}, f32[1,16,2,136,128]{4,3,2,0,1:T(8,128)S(1)}) fusion(f32[4,16,2,136,128]{4,3,2,0,1:T(8,128)} %bitcast.113), kind=kLoop, calls=%fused_computation.100 | loop fusion | bytes 17825792 | tf_op jit(solution)/shard_map/slice | solution.py:69
  339.6 0.7 fusion.20
  340.2 0.7 copy-done.1
  341.6 0.7 copy-done.5
  343.0 0.7 gather_fusion.1
  343.7 3.6 gather_fusion.3
  347.4 0.7 gather_fusion.6
  348.1 3.6 gather_fusion.7
  351.7 0.7 gather_fusion.4
  352.4 1.6 fusion.19
  354.0 3.7 gather_fusion.5
  357.7 0.7 gather_fusion.8
  358.4 4.8 %fusion.3 = f32[32,128,128]{2,1,0:T(8,128)S(1)} fusion(f32[32,128,128]{1,2,0:T(8,128)} %gather_fusion.3, f32[32,136,128]{2,1,0:T(8,128)} %bitcast.121, pred[32]{0:T(512)(128)(4,1)S(1)} %get-tuple-element.81), kind=kOutput, calls=%fused_computation.20 | convolution fusion | flops 403177472 | bytes 6291488 | tf_op jit(solution)/shard_map/rik,rkj->rij/dot_general | solution.py:74
  363.2 3.8 fusion.1
  366.9 3.8 fusion.2
  370.7 1.1 collective-permute-done.8
  371.8 3.7 gather_fusion.9
  375.5 7.2 %add_bitcast_fusion = f32[32,1,128,128]{3,2,1,0:T(8,128)} fusion(f32[32,128,128]{2,1,0:T(8,128)} %fusion.1, f32[32,128,128]{2,1,0:T(8,128)S(1)} %fusion.3, f32[32,128,128]{2,1,0:T(8,128)} %fusion.2, f32[32,128,128]{1,2,0:T(8,128)} %gather_fusion.9, f32[32,136,128]{2,1,0:T(8,128)} %bitcast.115, pred[32]{0:T(512)(128)(4,1)S(1)} %get-tuple-element.80), kind=kOutput, calls=%fused_computation.23 | convolution fusion | flops 404750336 | bytes 12582944 | tf_op jit(solution)/shard_map/rik,rkj->rij/dot_general | solution.py:74
  (59 shorter events, 5.3 us)
Async XLA Ops:
  8.5 1.4 copy-start.8
  25.3 108.3 %all-to-all-start = ((f32[16,520,128]{2,1,0:T(8,128)}), f32[16,520,128]{2,1,0:T(8,128)}, u32[]{:S(2)}, u32[]{:S(2)}) async-start(f32[16,520,128]{2,1,0:T(8,128)} %select_maximum_fusion), calls=%async_computation | async-start | bytes 8519680 | tf_op jit(solution)/shard_map/all_to_all | solution.py:42
  35.5 298.2 %all-gather.3.cloned.1.call-start = ((), (), s32[]{:S(2)}) async-start(), calls=%async_computation.3 | async-start | bytes 9469952 | tf_op jit(solution)/shard_map/all_gather | solution.py:57
  135.5 9.9 %collective-permute-start.2 = (f32[256,128]{1,0:T(8,128)}, f32[256,128]{1,0:T(8,128)S(1)}, u32[]{:S(2)}, u32[]{:S(2)}) collective-permute-start(f32[256,128]{1,0:T(8,128)} %get-tuple-element.70), channel_id=1, source_target_pairs={{48,0},{64,16},{80,32},{96,48},{112,64},{128,80},{144,96},{160,112... | collective-permute-start | bytes 393224 | tf_op jit(solution)/shard_map/ppermute | solution.py:13
  137.2 8.2 %collective-permute-start.1 = (f32[256,128]{1,0:T(8,128)S(1)}, f32[256,128]{1,0:T(8,128)S(1)}, u32[]{:S(2)}, u32[]{:S(2)}) collective-permute-start(f32[256,128]{1,0:T(8,128)S(1)} %get-tuple-element.71), channel_id=1, source_target_pairs={{32,0},{48,16},{64,32},{80,48},{96,64},{112,80},{128,96},{144,112}... | collective-permute-start | bytes 393224 | tf_op jit(solution)/shard_map/ppermute | solution.py:13
  138.6 6.7 %collective-permute-start = (f32[256,128]{1,0:T(8,128)S(1)}, f32[256,128]{1,0:T(8,128)}, u32[]{:S(2)}, u32[]{:S(2)}) collective-permute-start(f32[256,128]{1,0:T(8,128)S(1)} %get-tuple-element.72), channel_id=1, source_target_pairs={{16,0},{32,16},{48,32},{64,48},{80,64},{96,80},{112,96},{128,112},... | collective-permute-start | bytes 393224 | tf_op jit(solution)/shard_map/ppermute | solution.py:13
  186.6 8.8 %copy-start.9 = (s32[32]{0:T(128)S(1)}, s32[32]{0:T(128)}, u32[]{:S(2)}) copy-start(s32[32]{0:T(128)} %copy-done.8) | copy-start | bytes 388
  186.7 70.8 %all-to-all-start.2 = ((f32[2,16,128,128]{3,2,0,1:T(8,128)}), f32[2,16,128,128]{3,2,0,1:T(8,128)}, u32[]{:S(2)}, u32[]{:S(2)}) async-start(f32[2,16,128,128]{3,2,0,1:T(8,128)} %all_to_all.25), calls=%async_computation.2 | async-start | bytes 4194304 | tf_op jit(solution)/shard_map/all_to_all | solution.py:45
  261.0 4.0 %copy-start = (s32[32,1]{0,1:T(1,128)S(1)}, s32[32,1]{0,1:T(1,128)}, u32[]{:S(2)}) copy-start(s32[32,1]{0,1:T(1,128)} %param.14) | copy-start | bytes 388
  264.2 61.2 %collective-permute-start.6 = (f32[32,128,128]{1,2,0:T(8,128)}, f32[32,128,128]{1,2,0:T(8,128)}, u32[]{:S(2)}, u32[]{:S(2)}) collective-permute-start(f32[32,128,128]{1,2,0:T(8,128)} %bitcast_add_fusion), channel_id=1, source_target_pairs={{32,0},{48,16},{64,32},{80,48},{96,64},{112,80},{128,96},{144,112}... | collective-permute-start | bytes 6291464 | tf_op jit(solution)/shard_map/ppermute | solution.py:13
  265.0 60.2 %collective-permute-start.5 = (s32[32]{0:T(128)S(1)}, s32[32]{0:T(128)S(1)}, u32[]{:S(2)}, u32[]{:S(2)}) collective-permute-start(s32[32]{0:T(128)S(1)} %bitcast.110), channel_id=1, source_target_pairs={{32,0},{48,16},{64,32},{80,48},{96,64},{112,80},{128,96},{144,112}... | collective-permute-start | bytes 392 | tf_op jit(solution)/shard_map/ppermute | solution.py:13
  267.5 84.2 %collective-permute-start.3 = (s32[32]{0:T(128)S(1)}, s32[32]{0:T(128)S(1)}, u32[]{:S(2)}, u32[]{:S(2)}) collective-permute-start(s32[32]{0:T(128)S(1)} %bitcast.111), channel_id=1, source_target_pairs={{16,0},{32,16},{48,32},{64,48},{80,64},{96,80},{112,96},{128,112},... | collective-permute-start | bytes 392 | tf_op jit(solution)/shard_map/ppermute | solution.py:13
  325.2 32.5 %collective-permute-start.7 = (s32[32]{0:T(128)S(1)}, s32[32]{0:T(128)S(1)}, u32[]{:S(2)}, u32[]{:S(2)}) collective-permute-start(s32[32]{0:T(128)S(1)} %collective-permute-done.5), channel_id=1, source_target_pairs={{16,0},{32,16},{48,32},{64,48},{80,64},{96,80},{112,96},{128,112},... | collective-permute-start | bytes 392 | tf_op jit(solution)/shard_map/ppermute | solution.py:13
  325.2 28.8 %collective-permute-start.4 = (f32[32,128,128]{1,2,0:T(8,128)}, f32[32,128,128]{1,2,0:T(8,128)}, u32[]{:S(2)}, u32[]{:S(2)}) collective-permute-start(f32[32,128,128]{1,2,0:T(8,128)} %bitcast_add_fusion), channel_id=1, source_target_pairs={{16,0},{32,16},{48,32},{64,48},{80,64},{96,80},{112,96},{128,112},... | collective-permute-start | bytes 6291464 | tf_op jit(solution)/shard_map/ppermute | solution.py:13
  325.5 46.3 %collective-permute-start.8 = (f32[32,128,128]{1,2,0:T(8,128)}, f32[32,128,128]{1,2,0:T(8,128)}, u32[]{:S(2)}, u32[]{:S(2)}) collective-permute-start(f32[32,128,128]{1,2,0:T(8,128)} %collective-permute-done.6), channel_id=1, source_target_pairs={{16,0},{32,16},{48,32},{64,48},{80,64},{96,80},{112,96},{128,112},... | collective-permute-start | bytes 6291464 | tf_op jit(solution)/shard_map/ppermute | solution.py:13
  339.6 1.4 copy-start.1
  339.6 2.0 copy-start.3
  339.6 2.7 copy-start.5
  358.4 4.8 %copy-start.4 = (f32[1,16,2,136,128]{4,3,2,0,1:T(8,128)S(1)}, f32[1,16,2,136,128]{4,3,2,0,1:T(8,128)}, u32[]{:S(2)}) copy-start(f32[1,16,2,136,128]{4,3,2,0,1:T(8,128)} %copy-done.3) | copy-start | bytes 6684676
  358.4 4.8 %copy-start.6 = (f32[32,128,128]{1,2,0:T(8,128)S(1)}, f32[32,128,128]{1,2,0:T(8,128)}, u32[]{:S(2)}) copy-start(f32[32,128,128]{1,2,0:T(8,128)} %gather_fusion.7) | copy-start | bytes 6291460
  363.2 3.8 copy-start.2
  363.2 3.8 copy-start.7
Sparse Core Ops, SparseCore 0:
  148.2 185.4 all-gather.2
